TPU v7x, 128 devices: a whole 4x4x4 slice. The times are simulated.
128 devices in a mesh: gx: 8 (over x_lo, z), gy: 16 (over x_hi, y, core).
Axes of the slice: x: 4 (x_hi: 2, x_lo: 2; x = x_hi * 2 + x_lo), y: 4, z: 4, core: 2. Of those that a mesh axis runs over, the one named last changes fastest.
Arguments:
- queries: bfloat16 [16384, 4096], P(('gx', 'gy')), may hold values from -6 to 6
- new_kv: bfloat16 [16384, 1024], P(('gx', 'gy')), may hold values from -6 to 6
- kv_cache: bfloat16 [4096, 1024], P('gx'), may hold values from -6 to 6
- residual: bfloat16 [16384, 2048], P(('gx', 'gy')), may hold values from -3 to 3
- token_request: int32 [128, 128], P(('gx', 'gy')), may hold values from 0 to 7, never falling along the last dimension, each value on 1 to 32 neighbouring positions
- request_leaf: int32 [128, 8], P(('gx', 'gy')), may hold values from 0 to 15
- mid_parent: int32 [8], replicated, may hold values from 0 to 3
- leaf_parent: int32 [16], replicated, may hold values from 0 to 7
- node_owner: int32 [28], replicated, may hold values from 0 to 7, as said below
- node_len: int32 [28], replicated, may hold values from 1 to 512, as said below
- out_weight: bfloat16 [4096, 2048], P('gy'), may hold values from -0.375 to 0.375
- norm_gain: float32 [2048], replicated, may hold values from 0.1 to 1.9
- route_experts: int32 [16384, 8], P(('gx', 'gy')), may hold values from 0 to 127, all different within a row; in each aligned block of 128 rows (0 to 127, 128 to 255, ...) at most 12 rows name the same one
- route_weights: float32 [16384, 8], P(('gx', 'gy')), may hold values from 0.25 to 2
- expert_gate: bfloat16 [128, 2048, 768], P(('gx', 'gy')), may hold values from -0.125 to 0.125
- expert_up: bfloat16 [128, 2048, 768], P(('gx', 'gy')), may hold values from -0.125 to 0.125
- expert_down: bfloat16 [128, 768, 2048], P(('gx', 'gy')), may hold values from -0.21875 to 0.21875
Outputs:
- layer_out: bfloat16 [16384, 2048], P(('gx', 'gy'))
Inputs may be any that keep to these rules, and one draw needn't show every extreme that they name: `token_request`: within one row, requests are numbered from 0 in order; each has 1 to 32 tokens and one has exactly 32. `node_owner`: every owner index holds at least one node; some owner holds exactly one node. `node_len`: the nodes of one owner have lengths that sum to exactly 512; a node that is alone on its owner has 512 rows. `route_experts`: A row's 8 experts differ; in the 128 rows of one device no expert is named more than 12 times, a bound that some block reaches.
All inputs are finite; a program needn't handle non-finite values.
Results may differ from a plain program's by a relative error of at most 0.023.
Values may be sent and summed in bfloat16 or wider, within the bound.
No kernel may reach another device: no remote copies, remote signals or barrier semaphores. Data moves between devices by JAX's collectives and lax.ppermute only.
A program may use at most 128 MiB of HBM per device.

v0:
```python
import jax
import jax.numpy as jnp
from jax import lax
from jax.sharding import PartitionSpec as P

HEADS = 32
KV_HEADS = 4
HEAD_DIM = 128
ROOTS = 4
MIDS = 8


EPSILON = 1e-06


def node_bounds(node_owner, node_len, span_rows):
    labels = jnp.arange(node_owner.shape[0], dtype=jnp.int32)
    earlier = (node_owner[:, None] == node_owner[None, :]) & (labels[None, :] < labels[:, None])
    before = jnp.sum(jnp.where(earlier, node_len[None, :], 0), axis=1)
    starts = node_owner * span_rows + before
    return (starts, starts + node_len)


def key_labels(first_row, row_count, starts, finish):
    cache_rows = first_row + jnp.arange(row_count, dtype=jnp.int32)
    inside = (cache_rows[:, None] >= starts[None, :]) & (cache_rows[:, None] < finish[None, :])
    labels = jnp.arange(starts.shape[0], dtype=jnp.int32)
    return jnp.sum(jnp.where(inside, labels[None, :], 0), axis=1)


def path_nodes(requests, leaf_table, mid_parent, leaf_parent):
    picked = requests[:, None] == jnp.arange(leaf_table.shape[0], dtype=jnp.int32)[None, :]
    leaf_node = jnp.sum(jnp.where(picked, leaf_table[None, :], 0), axis=1)
    leaf_pick = leaf_node[:, None] == jnp.arange(leaf_parent.shape[0], dtype=jnp.int32)[None, :]
    middle_node = jnp.sum(jnp.where(leaf_pick, leaf_parent[None, :], 0), axis=1)
    middle_pick = middle_node[:, None] == jnp.arange(mid_parent.shape[0], dtype=jnp.int32)[None, :]
    root_node = jnp.sum(jnp.where(middle_pick, mid_parent[None, :], 0), axis=1)
    return jnp.stack([root_node, ROOTS + middle_node, ROOTS + MIDS + leaf_node], axis=1)


def masked_scores(query_heads, key_rows, allowed, head_scale):
    scores = (
        jnp.einsum("tgsd,kgd->gstk", query_heads, key_rows, preferred_element_type=jnp.float32)
        * head_scale
    )
    return jnp.where(allowed[None, None], scores, -jnp.inf)


def on_device(
    queries,
    new_kv,
    kv_cache,
    residual,
    token_request,
    request_leaf,
    mid_parent,
    leaf_parent,
    node_owner,
    node_len,
    out_weight,
    norm_gain,
    route_experts,
    route_weights,
    expert_gate,
    expert_up,
    expert_down,
):
    tokens_here = queries.shape[0]
    model_width = residual.shape[1]
    group_size = HEADS // KV_HEADS
    kv_width = KV_HEADS * HEAD_DIM
    head_scale = HEAD_DIM ** (-0.5)
    query_heads = queries.reshape(tokens_here, KV_HEADS, group_size, HEAD_DIM)
    requests = token_request[0]
    ancestry = path_nodes(requests, request_leaf[0], mid_parent, leaf_parent)
    span_rows = kv_cache.shape[0]
    starts, finish = node_bounds(node_owner, node_len, span_rows)
    positions = jnp.arange(tokens_here, dtype=jnp.int32)
    own_mask = (requests[:, None] == requests[None, :]) & (positions[None, :] <= positions[:, None])
    new_keys = new_kv[:, :kv_width].reshape(tokens_here, KV_HEADS, HEAD_DIM)
    new_values = new_kv[:, kv_width:].reshape(tokens_here, KV_HEADS, HEAD_DIM)
    near_scores = masked_scores(query_heads, new_keys, own_mask, head_scale)
    row_max = jnp.max(near_scores, axis=3)
    near_weights = jnp.exp(near_scores - row_max[..., None])
    denominator = jnp.sum(near_weights, axis=3)
    numerator = jnp.einsum(
        "gstk,kgd->gstd",
        near_weights.astype(jnp.bfloat16),
        new_values,
        preferred_element_type=jnp.float32,
    )
    running = (row_max, denominator, numerator)
    shard_piece = lax.all_gather(kv_cache, "gx", axis=0, tiled=True)
    block_count = shard_piece.shape[0] // span_rows
    cache_blocks = shard_piece.reshape(block_count, span_rows, 2 * kv_width)

    def one_block(state, position):
        old_max, old_total, old_sum = state
        block_data = lax.dynamic_index_in_dim(cache_blocks, position, 0, keepdims=False)
        labels = key_labels(position * span_rows, span_rows, starts, finish)
        seen_mask = jnp.any(labels[None, :, None] == ancestry[:, None, :], axis=2)
        far_keys = block_data[:, :kv_width].reshape(span_rows, KV_HEADS, HEAD_DIM)
        far_values = block_data[:, kv_width:].reshape(span_rows, KV_HEADS, HEAD_DIM)
        far_scores = masked_scores(query_heads, far_keys, seen_mask, head_scale)
        new_max = jnp.maximum(old_max, jnp.max(far_scores, axis=3))
        far_weights = jnp.exp(far_scores - new_max[..., None])
        factor = jnp.exp(old_max - new_max)
        new_total = old_total * factor + jnp.sum(far_weights, axis=3)
        new_sum = old_sum * factor[..., None] + jnp.einsum(
            "gstk,kgd->gstd",
            far_weights.astype(jnp.bfloat16),
            far_values,
            preferred_element_type=jnp.float32,
        )
        return ((new_max, new_total, new_sum), None)

    running, _ = lax.scan(one_block, running, jnp.arange(block_count, dtype=jnp.int32))
    row_max, denominator, numerator = running
    heads_out = numerator / denominator[..., None]
    attended = (
        heads_out.transpose(2, 0, 1, 3).reshape(tokens_here, HEADS * HEAD_DIM).astype(jnp.bfloat16)
    )
    shard_rows = out_weight.shape[0]
    shard_piece = lax.all_gather(out_weight, "gy", axis=0, tiled=True)
    block_count = shard_piece.shape[0] // shard_rows
    columns = attended.reshape(tokens_here, block_count, shard_rows)
    partial_value = jnp.einsum(
        "tnr,nrd->ntd",
        columns,
        shard_piece.reshape(block_count, shard_rows, model_width),
        preferred_element_type=jnp.float32,
    )
    partial_value = lax.optimization_barrier(partial_value.astype(jnp.bfloat16))
    projected = jnp.sum(partial_value.astype(jnp.float32), axis=0)
    mixed_state = (residual.astype(jnp.float32) + projected).astype(jnp.bfloat16)
    mixed_float = lax.optimization_barrier(mixed_state).astype(jnp.float32)
    normed = (
        mixed_float
        * lax.rsqrt(jnp.mean(mixed_float * mixed_float, axis=1, keepdims=True) + EPSILON)
        * norm_gain
    ).astype(jnp.bfloat16)
    top_count = route_experts.shape[1]
    expert_count = lax.axis_size("gx") * lax.axis_size("gy") * expert_gate.shape[0]
    capacity = max(2, (3 * tokens_here * top_count + 2 * expert_count - 1) // (2 * expert_count))
    flat_experts = route_experts.reshape(-1)
    onehot = (flat_experts[:, None] == jnp.arange(expert_count, dtype=jnp.int32)[None, :]).astype(
        jnp.int32
    )
    slot_ids = jnp.sum((jnp.cumsum(onehot, axis=0) - onehot) * onehot, axis=1)
    target = flat_experts * capacity + slot_ids
    assignments = tokens_here * top_count
    source = (
        jnp.full((expert_count * capacity,), -1, jnp.int32)
        .at[target]
        .set(jnp.arange(assignments, dtype=jnp.int32))
    )
    is_valid = source >= 0
    source_rows = jnp.maximum(source, 0) // top_count
    outgoing = jnp.where(is_valid[:, None], normed[source_rows], jnp.zeros((), jnp.bfloat16))
    outgoing = outgoing.reshape(expert_count, capacity, model_width)
    arrived = lax.all_to_all(outgoing, ("gx", "gy"), split_axis=0, concat_axis=0, tiled=True)
    stacked = arrived.reshape(-1, model_width)
    gate_act = jnp.dot(stacked, expert_gate[0], preferred_element_type=jnp.float32)
    up_act = jnp.dot(stacked, expert_up[0], preferred_element_type=jnp.float32)
    hidden = (jax.nn.silu(gate_act) * up_act).astype(jnp.bfloat16)
    expert_out = jnp.dot(hidden, expert_down[0], preferred_element_type=jnp.float32).astype(
        jnp.bfloat16
    )
    returned = lax.all_to_all(
        expert_out.reshape(arrived.shape), ("gx", "gy"), split_axis=0, concat_axis=0, tiled=True
    )
    picked_rows = returned.reshape(expert_count * capacity, model_width)[target].reshape(
        tokens_here, top_count, model_width
    )
    routed_sum = jnp.sum(picked_rows.astype(jnp.float32) * route_weights[:, :, None], axis=1)
    return (mixed_float + routed_sum).astype(jnp.bfloat16)


def solution(mesh):
    in_specs = (
        P(("gx", "gy"), None),
        P(("gx", "gy"), None),
        P("gx", None),
        P(("gx", "gy"), None),
        P(("gx", "gy"), None),
        P(("gx", "gy"), None),
        P(),
        P(),
        P(),
        P(),
        P("gy", None),
        P(),
        P(("gx", "gy"), None),
        P(("gx", "gy"), None),
        P(("gx", "gy"), None, None),
        P(("gx", "gy"), None, None),
        P(("gx", "gy"), None, None),
    )
    out_specs = P(("gx", "gy"), None)
    return jax.shard_map(
        on_device, mesh=mesh, in_specs=in_specs, out_specs=out_specs, check_vma=False
    )
```

profile of v0, /device:TPU:1, one launch (start us, length us, event | category | flops | bytes accessed | tf_op | source)
XLA Modules:
  0.0 621.9 jit_solution(3076183210187732818)
XLA Ops:
  20.3 4.3 scatter_custom_fusion
  32.9 71.2 %all-gather.3.cloned.1.call-done = bf16[4096,1024]{1,0:T(8,128)(2,1)} async-done(((bf16[512,1024]{1,0:T(8,128)(2,1)}), bf16[4096,1024]{1,0:T(8,128)(2,1)}) %all-gather.3.cloned.1.call-update) | async-done | bytes 8388624 | tf_op jit(solution)/shard_map/all_gather | solution.py:93
  104.1 155.5 %while.14 = (s32[]{:T(128)}, f32[4,8,128]{2,1,0:T(8,128)S(1)}, f32[4,8,128]{2,1,0:T(8,128)S(1)}, f32[4,8,128,128]{3,2,1,0:T(8,128)}, s32[8]{0:T(128)S(1)}, /*ind...) while((s32[]{:T(128)}, f32[4,8,128]{2,1,0:T(8,128)S(1)}, ...), condition=%wide.region_11.12_spmd, body=%wide.region_6.11_spmd.sunk | while | flops 1098266624 | bytes 57288696 | solution.py:117
  138.6 3.1 multiply_add_fusion.7
  158.3 3.1 multiply_add_fusion.7
  197.0 3.1 multiply_add_fusion.7
  216.5 3.1 multiply_add_fusion.7
  255.2 3.1 multiply_add_fusion.7
  265.5 11.8 %convolution_convert_fusion.1 = bf16[16,128,2048]{2,1,0:T(8,128)(2,1)} fusion(bf16[128,16,256]{0,2,1:T(8,128)(2,1)} %bitcast.109, bf16[16,256,2048]{2,1,0:T(8,128)(2,1)} %bitcast.105), kind=kOutput, calls=%fused_computation.27 | convolution fusion | flops 2151677952 | bytes 26214400 | tf_op jit(solution)/shard_map/tnr,nrd->ntd/dot_general | solution.py:127
  277.3 5.4 convert_reduce_fusion
  284.6 13.8 %gather_fusion = bf16[1536,2048]{1,0:T(8,128)(2,1)} fusion(bf16[128,2048]{1,0:T(8,128)(2,1)} %fusion.22, s32[2048]{0:T(1024)S(1)} %pad_clamp_fusion), kind=kCustom, calls=%fused_computation | custom fusion | bytes 12589056 | tf_op jit(solution)/shard_map/gather | solution.py:159
  298.4 10.6 %gather.9 = bf16[128,12,2048]{2,1,0:T(8,128)(2,1)} reshape(bf16[1536,2048]{1,0:T(8,128)(2,1)} %gather_fusion) | data formatting | bytes 12582912 | tf_op jit(solution)/shard_map/gather | solution.py:159
  309.0 7.3 %broadcast_select_fusion = bf16[128,12,2048]{2,1,0:T(8,128)(2,1)} fusion(bf16[128,12,2048]{2,1,0:T(8,128)(2,1)} %gather.9, pred[128,12]{1,0:T(8,128)(4,1)S(1)} %broadcast_in_dim.145), kind=kLoop, calls=%fused_computation.25 | loop fusion | flops 3145728 | bytes 12584448 | tf_op jit(solution)/shard_map/jit(_where)/select_n | solution.py:159
  316.3 104.8 %all_to_all.10 = bf16[128,12,2048]{2,1,0:T(8,128)(2,1)} all-to-all(bf16[128,12,2048]{2,1,0:T(8,128)(2,1)} %broadcast_select_fusion), channel_id=1, replica_groups=mesh['gx'=8,'gy'=16] {'gx','gy'}, dimensions={0} | all-to-all | bytes 12582912 | tf_op jit(solution)/shard_map/all_to_all | solution.py:161
  421.0 10.7 %reshape.188 = bf16[1536,2048]{1,0:T(8,128)(2,1)} reshape(bf16[128,12,2048]{2,1,0:T(8,128)(2,1)} %all_to_all.10) | data formatting | bytes 12582912 | tf_op jit(solution)/shard_map/reshape | solution.py:162
  431.8 8.2 %fusion.16 = f32[1536,768]{1,0:T(8,128)S(1)} fusion(bf16[1536,2048]{1,0:T(8,128)(2,1)} %reshape.188, bf16[1,2048,768]{2,1,0:T(8,128)(2,1)} %param.33), kind=kOutput, calls=%fused_computation.31 | convolution fusion | flops 4831838208 | bytes 14155776 | tf_op jit(solution)/shard_map/dot_general | solution.py:163
  440.0 5.6 multiply_convert_fusion
  445.6 7.1 %convolution_convert_fusion = bf16[1536,2048]{1,0:T(8,128)(2,1)} fusion(bf16[1536,768]{1,0:T(8,128)(2,1)S(1)} %multiply_convert_fusion, bf16[1,768,2048]{2,1,0:T(8,128)(2,1)S(1)} %copy-done), kind=kOutput, calls=%fused_computation.26 | convolution fusion | flops 4834983936 | bytes 11796480 | tf_op jit(solution)/shard_map/dot_general | solution.py:166
  452.7 10.6 %reshape.189 = bf16[128,12,2048]{2,1,0:T(8,128)(2,1)} reshape(bf16[1536,2048]{1,0:T(8,128)(2,1)} %convolution_convert_fusion) | data formatting | bytes 12582912 | tf_op jit(solution)/shard_map/reshape | solution.py:170
  463.3 8.3 %all-to-all-start.1 = ((bf16[128,12,2048]{2,1,0:T(8,128)(2,1)}), bf16[128,12,2048]{2,1,0:T(8,128)(2,1)}, u32[]{:S(2)}, u32[]{:S(2)}) async-start(bf16[128,12,2048]{2,1,0:T(8,128)(2,1)} %reshape.189), calls=%async_computation.1 | async-start | bytes 16777216 | tf_op jit(solution)/shard_map/all_to_all | solution.py:169
  471.7 112.7 %all-to-all-done.1 = bf16[128,12,2048]{2,1,0:T(8,128)(2,1)} async-done(((bf16[128,12,2048]{2,1,0:T(8,128)(2,1)}), bf16[128,12,2048]{2,1,0:T(8,128)(2,1)}, u32[]{:S(2)}, u32[]{:S(2)}) %all-to-all-start.1) | async-done | bytes 6291488 | tf_op jit(solution)/shard_map/all_to_all | solution.py:169
  584.4 10.7 %reshape.190 = bf16[1536,2048]{1,0:T(8,128)(2,1)} reshape(bf16[128,12,2048]{2,1,0:T(8,128)(2,1)} %all-to-all-done.1) | data formatting | bytes 12582912 | tf_op jit(solution)/shard_map/reshape | solution.py:172
  595.1 12.4 %gather_fusion.1 = bf16[1024,2048]{1,0:T(8,128)(2,1)} fusion(bf16[1536,2048]{1,0:T(8,128)(2,1)} %reshape.190, s32[1024]{0:T(1024)S(1)} %broadcast_clamp_fusion), kind=kCustom, calls=%fused_computation.1 | custom fusion | bytes 8392704 | tf_op jit(solution)/shard_map/gather | solution.py:172
  607.5 6.6 %fusion.13 = f32[128,2048]{1,0:T(8,128)S(1)} fusion(bf16[1024,2048]{1,0:T(8,128)(2,1)} %gather_fusion.1, f32[128,8]{1,0:T(8,128)S(1)} %copy.83), kind=kLoop, calls=%fused_computation.24 | loop fusion | flops 6029312 | bytes 5246976 | tf_op jit(solution)/shard_map/reduce_sum | solution.py:175
  (232 shorter events, 151.6 us)
Async XLA Ops:
  6.5 439.1 %copy-start = (bf16[1,768,2048]{2,1,0:T(8,128)(2,1)S(1)}, bf16[1,768,2048]{2,1,0:T(8,128)(2,1)}, u32[]{:S(2)}) copy-start(bf16[1,768,2048]{2,1,0:T(8,128)(2,1)} %param.35) | copy-start | bytes 9437188
  6.5 97.6 %all-gather.3.cloned.1.call-start = ((), (), s32[]{:S(2)}) async-start(), calls=%async_computation.2 | async-start | bytes 9437184 | tf_op jit(solution)/shard_map/all_gather | solution.py:93
  7.3 258.3 %all-gather.5.cloned.1.call-start = ((), (), s32[]{:S(2)}) async-start(), calls=%async_computation.3 | async-start | bytes 17825792 | tf_op jit(solution)/shard_map/all_gather | solution.py:124
  14.8 16.1 %copy-start.12 = (s32[28]{0:T(128)S(1)}, s32[28]{0:T(128)}, u32[]{:S(2)}) copy-start(s32[28]{0:T(128)} %param.27) | copy-start | bytes 340
  14.9 16.1 %copy-start.14 = (s32[28]{0:T(128)S(1)}, s32[28]{0:T(128)}, u32[]{:S(2)}) copy-start(s32[28]{0:T(128)} %param.28) | copy-start | bytes 340
  20.3 6.7 %copy-start.9 = (s32[1024,1]{0,1:T(1,128)}, s32[1024,1]{0,1:T(1,128)S(1)}, u32[]{:S(2)}) copy-start(s32[1024,1]{0,1:T(1,128)S(1)} %compare_select_fusion) | copy-start | bytes 12292
  117.3 1.8 copy-start.1
  117.3 1.9 copy-start.2
  136.8 1.8 copy-start.1
  136.8 1.8 copy-start.2
  156.5 1.8 copy-start.1
  175.8 1.8 copy-start.1
  195.2 1.8 copy-start.1
  214.6 1.8 copy-start.1
  234.0 1.8 copy-start.1
  253.3 1.8 copy-start.1
  277.3 5.4 copy-start.8
  277.3 6.3 %copy-start.11 = (f32[2048]{0:T(1024)S(1)}, f32[2048]{0:T(1024)}, u32[]{:S(2)}) copy-start(f32[2048]{0:T(1024)} %param.30) | copy-start | bytes 24580
  431.7 8.2 %copy-start.6 = (bf16[1536,2048]{1,0:T(8,128)(2,1)S(1)}, bf16[1536,2048]{1,0:T(8,128)(2,1)}, u32[]{:S(2)}) copy-start(bf16[1536,2048]{1,0:T(8,128)(2,1)} %reshape.188) | copy-start | bytes 18874372
  431.7 8.2 %copy-start.15 = (bf16[1,2048,768]{2,1,0:T(8,128)(2,1)S(1)}, bf16[1,2048,768]{2,1,0:T(8,128)(2,1)}, u32[]{:S(2)}) copy-start(bf16[1,2048,768]{2,1,0:T(8,128)(2,1)} %param.34) | copy-start | bytes 9437188
  463.3 8.3 %copy-start.13 = (f32[128,8]{0,1:T(8,128)S(1)}, f32[128,8]{0,1:T(8,128)}, u32[]{:S(2)}) copy-start(f32[128,8]{0,1:T(8,128)} %param.32) | copy-start | bytes 12292
  463.3 8.4 %copy-start.10 = (s32[1024,1]{0,1:T(1,128)S(1)}, s32[1024,1]{0,1:T(1,128)}, u32[]{:S(2)}) copy-start(s32[1024,1]{0,1:T(1,128)} %copy-done.9) | copy-start | bytes 12292
  463.3 121.1 %all-to-all-start.1 = ((bf16[128,12,2048]{2,1,0:T(8,128)(2,1)}), bf16[128,12,2048]{2,1,0:T(8,128)(2,1)}, u32[]{:S(2)}, u32[]{:S(2)}) async-start(bf16[128,12,2048]{2,1,0:T(8,128)(2,1)} %reshape.189), calls=%async_computation.1 | async-start | bytes 16777216 | tf_op jit(solution)/shard_map/all_to_all | solution.py:169
  607.5 6.6 %copy-start.5 = (bf16[128,2048]{1,0:T(8,128)(2,1)S(1)}, bf16[128,2048]{1,0:T(8,128)(2,1)}, u32[]{:S(2)}) copy-start(bf16[128,2048]{1,0:T(8,128)(2,1)} %copy-done.4) | copy-start | bytes 1572868
  (16 other events, 23.6 us)
Sparse Core Ops, SparseCore 0:
  9.0 95.0 all-gather.2
  106.6 107.7 all-gather.4
where the time goes:
time: 625 us; the launch traced here: 622 us
  waiting for transfers between devices  185 us (30%)
  local copies, waits for them, and re-layouts  159 us (25%)
  blocking collectives  105 us (17%)
  matrix products  83.7 us (13%)
  other arithmetic  48.2 us (8%)
  loops' own time  19.2 us (3%)
  between operations  13.7 us (2%)
  starting transfers between devices  8.33 us (1%)
    all_to_all x1, waiting for transfers between devices, on_device(): lax.all_to_all(expert_out.reshape(arrived.shape), ('gx', 'gy'), split_axi...  113 us
    all_to_all x1, blocking collectives, on_device(): lax.all_to_all(outgoing, ('gx', 'gy'), split_axis=0, concat_axis=0, tiled...  105 us
    all_gather x1, waiting for transfers between devices, on_device(): shard_piece = lax.all_gather(kv_cache, 'gx', axis=0, tiled=True)  71.2 us
    dynamic_slice x16, local copies, waits for them, and re-layouts, one_block(): lax.dynamic_index_in_dim(cache_blocks, position, 0, keepdims=False)  37.3 us
    dot_general x8, matrix products, one_block(): jnp.einsum('gstk,kgd->gstd', far_weights.astype(jnp.bfloat16), far_values...  24.7 us
    gather x2, local copies, waits for them, and re-layouts, on_device(): normed[source_rows]  24.4 us
    dot_general x9, matrix products, masked_scores(): jnp.einsum('tgsd,kgd->gstk', query_heads, key_rows, preferred_element_typ...  24.3 us
    another operation x1, loops' own time, on_device(): lax.scan(one_block, running, jnp.arange(block_count, dtype=jnp.int32))  19.2 us
  transfers between devices with their start and end apart: 3, of which 2 were waited for; matrix products, arithmetic and copies ran while one was open for 25% of the time, Pallas kernels for 0%

commit v1 on v0

--- a/solution.py
+++ b/solution.py
@@ -2,6 +2,8 @@
 import jax.numpy as jnp
 from jax import lax
 from jax.sharding import PartitionSpec as P
+from jax.experimental import pallas as pl
+from jax.experimental.pallas import tpu as pltpu
 
 HEADS = 32
 KV_HEADS = 4
@@ -44,6 +46,52 @@
         * head_scale
     )
     return jnp.where(allowed[None, None], scores, -jnp.inf)
+
+
+def attention_kernel(q_ref, kc_ref, vc_ref, kn_ref, vn_ref, bf_ref, bn_ref, o_ref):
+    head_scale = HEAD_DIM ** (-0.5)
+    contract = (((1,), (1,)), ((), ()))
+    far_keys = kc_ref[...]
+    far_values = vc_ref[...]
+    near_keys = kn_ref[...]
+    near_values = vn_ref[...]
+    far_bias = bf_ref[...]
+    near_bias = bn_ref[...]
+    for head in range(HEADS // KV_HEADS):
+        cols = slice(head * HEAD_DIM, (head + 1) * HEAD_DIM)
+        query = q_ref[:, cols]
+        far = lax.dot_general(query, far_keys, contract, preferred_element_type=jnp.float32) + far_bias
+        near = lax.dot_general(query, near_keys, contract, preferred_element_type=jnp.float32) + near_bias
+        top = jnp.maximum(jnp.max(far, axis=1, keepdims=True), jnp.max(near, axis=1, keepdims=True))
+        far_p = jnp.exp((far - top) * head_scale)
+        near_p = jnp.exp((near - top) * head_scale)
+        total = jnp.sum(far_p, axis=1, keepdims=True) + jnp.sum(near_p, axis=1, keepdims=True)
+        summed = jnp.dot(
+            far_p.astype(jnp.bfloat16), far_values, preferred_element_type=jnp.float32
+        ) + jnp.dot(near_p.astype(jnp.bfloat16), near_values, preferred_element_type=jnp.float32)
+        o_ref[:, cols] = (summed / total).astype(o_ref.dtype)
+
+
+def tree_attention(queries, cache, new_kv, far_bias, near_bias):
+    tokens = queries.shape[0]
+    rows = cache.shape[0]
+    group_cols = (HEADS // KV_HEADS) * HEAD_DIM
+    return pl.pallas_call(
+        attention_kernel,
+        grid=(KV_HEADS,),
+        in_specs=[
+            pl.BlockSpec((tokens, group_cols), lambda g: (0, g)),
+            pl.BlockSpec((rows, HEAD_DIM), lambda g: (0, g)),
+            pl.BlockSpec((rows, HEAD_DIM), lambda g: (0, KV_HEADS + g)),
+            pl.BlockSpec((tokens, HEAD_DIM), lambda g: (0, g)),
+            pl.BlockSpec((tokens, HEAD_DIM), lambda g: (0, KV_HEADS + g)),
+            pl.BlockSpec((tokens, rows), lambda g: (0, 0)),
+            pl.BlockSpec((tokens, tokens), lambda g: (0, 0)),
+        ],
+        out_specs=pl.BlockSpec((tokens, group_cols), lambda g: (0, g)),
+        out_shape=jax.ShapeDtypeStruct((tokens, HEADS * HEAD_DIM), jnp.bfloat16),
+        compiler_params=pltpu.CompilerParams(vmem_limit_bytes=48 * 1024 * 1024),
+    )(queries, cache, cache, new_kv, new_kv, far_bias, near_bias)
 
 
 def on_device(
@@ -70,56 +118,18 @@
     group_size = HEADS // KV_HEADS
     kv_width = KV_HEADS * HEAD_DIM
     head_scale = HEAD_DIM ** (-0.5)
-    query_heads = queries.reshape(tokens_here, KV_HEADS, group_size, HEAD_DIM)
     requests = token_request[0]
     ancestry = path_nodes(requests, request_leaf[0], mid_parent, leaf_parent)
     span_rows = kv_cache.shape[0]
     starts, finish = node_bounds(node_owner, node_len, span_rows)
     positions = jnp.arange(tokens_here, dtype=jnp.int32)
     own_mask = (requests[:, None] == requests[None, :]) & (positions[None, :] <= positions[:, None])
-    new_keys = new_kv[:, :kv_width].reshape(tokens_here, KV_HEADS, HEAD_DIM)
-    new_values = new_kv[:, kv_width:].reshape(tokens_here, KV_HEADS, HEAD_DIM)
-    near_scores = masked_scores(query_heads, new_keys, own_mask, head_scale)
-    row_max = jnp.max(near_scores, axis=3)
-    near_weights = jnp.exp(near_scores - row_max[..., None])
-    denominator = jnp.sum(near_weights, axis=3)
-    numerator = jnp.einsum(
-        "gstk,kgd->gstd",
-        near_weights.astype(jnp.bfloat16),
-        new_values,
-        preferred_element_type=jnp.float32,
-    )
-    running = (row_max, denominator, numerator)
-    shard_piece = lax.all_gather(kv_cache, "gx", axis=0, tiled=True)
-    block_count = shard_piece.shape[0] // span_rows
-    cache_blocks = shard_piece.reshape(block_count, span_rows, 2 * kv_width)
-
-    def one_block(state, position):
-        old_max, old_total, old_sum = state
-        block_data = lax.dynamic_index_in_dim(cache_blocks, position, 0, keepdims=False)
-        labels = key_labels(position * span_rows, span_rows, starts, finish)
-        seen_mask = jnp.any(labels[None, :, None] == ancestry[:, None, :], axis=2)
-        far_keys = block_data[:, :kv_width].reshape(span_rows, KV_HEADS, HEAD_DIM)
-        far_values = block_data[:, kv_width:].reshape(span_rows, KV_HEADS, HEAD_DIM)
-        far_scores = masked_scores(query_heads, far_keys, seen_mask, head_scale)
-        new_max = jnp.maximum(old_max, jnp.max(far_scores, axis=3))
-        far_weights = jnp.exp(far_scores - new_max[..., None])
-        factor = jnp.exp(old_max - new_max)
-        new_total = old_total * factor + jnp.sum(far_weights, axis=3)
-        new_sum = old_sum * factor[..., None] + jnp.einsum(
-            "gstk,kgd->gstd",
-            far_weights.astype(jnp.bfloat16),
-            far_values,
-            preferred_element_type=jnp.float32,
-        )
-        return ((new_max, new_total, new_sum), None)
-
-    running, _ = lax.scan(one_block, running, jnp.arange(block_count, dtype=jnp.int32))
-    row_max, denominator, numerator = running
-    heads_out = numerator / denominator[..., None]
-    attended = (
-        heads_out.transpose(2, 0, 1, 3).reshape(tokens_here, HEADS * HEAD_DIM).astype(jnp.bfloat16)
-    )
+    cache_all = lax.all_gather(kv_cache, "gx", axis=0, tiled=True)
+    labels = key_labels(0, cache_all.shape[0], starts, finish)
+    seen_mask = jnp.any(labels[None, :, None] == ancestry[:, None, :], axis=2)
+    far_bias = jnp.where(seen_mask, 0.0, -jnp.inf).astype(jnp.float32)
+    near_bias = jnp.where(own_mask, 0.0, -jnp.inf).astype(jnp.float32)
+    attended = tree_attention(queries, cache_all, new_kv, far_bias, near_bias)
     shard_rows = out_weight.shape[0]
     shard_piece = lax.all_gather(out_weight, "gy", axis=0, tiled=True)
     block_count = shard_piece.shape[0] // shard_rows

time: 625 us -> 572 us (0.915)
  local copies, waits for them, and re-layouts: 159 us -> 80.8 us
  waiting for transfers between devices: 185 us -> 260 us
  matrix products: 83.7 us -> 32.6 us
  Pallas kernels: 0 us -> 38.9 us
  loops' own time: 19.2 us -> 0 us
  other arithmetic: 48.2 us -> 32.9 us
    all_gather x1, waiting for transfers between devices: 0.01 us -> 67.5 us  [on_device(): shard_piece = lax.all_gather(out_weight, 'gy', axis=0, tiled=True)]
    dot_general x18 -> x0, matrix products: 51 us -> none  [the longest x8 24.7 us: one_block(): jnp.einsum('gstk,kgd->gstd', far_weights.astype(jnp.bfloat16), far_values...]
    dynamic_slice x24 -> x0, local copies, waits for them, and re-layouts: 42 us -> none  [the longest x16 37.3 us: one_block(): lax.dynamic_index_in_dim(cache_blocks, position, 0, keepdims=False)]
    pallas_call x0 -> x1, Pallas kernels: none -> 38.9 us  [tree_attention(): pl.pallas_call(attention_kernel, grid=(KV_HEADS,), in_specs=[pl.BlockSpec...]
    slice x9 -> x0, local copies, waits for them, and re-layouts: 19.3 us -> none  [the longest x8 18.3 us: one_block(): far_values = block_data[:, kv_width:].reshape(span_rows, KV_HEADS, HEAD_DIM)]
    another operation x1 -> x0, loops' own time: 19.2 us -> none  [on_device(): lax.scan(one_block, running, jnp.arange(block_count, dtype=jnp.int32))]
    while x58 -> x0, local copies, waits for them, and re-layouts: 16.5 us -> none
    reduce_sum x9 -> x0, other arithmetic: 14.4 us -> none  [the longest x8 14 us: one_block(): new_total = old_total * factor + jnp.sum(far_weights, axis=3)]
  transfers between devices with their start and end apart: 3 -> 3, of which waited for: 2 -> 3; matrix products, arithmetic and copies ran while one was open for 25% -> 3% of each run, Pallas kernels for 0% -> 7%
where the time goes in v1:
time: 572 us; the launch traced here: 570 us
  waiting for transfers between devices  260 us (45%)
  blocking collectives  103 us (18%)
  local copies, waits for them, and re-layouts  80.8 us (14%)
  Pallas kernels  38.9 us (7%)
  other arithmetic  32.9 us (6%)
  matrix products  32.6 us (6%)
  between operations  13.6 us (2%)
  starting transfers between devices  8.33 us (1%)
    all_to_all x1, waiting for transfers between devices, on_device(): lax.all_to_all(expert_out.reshape(arrived.shape), ('gx', 'gy'), split_axi...  113 us
    all_to_all x1, blocking collectives, on_device(): lax.all_to_all(outgoing, ('gx', 'gy'), split_axis=0, concat_axis=0, tiled...  103 us
    all_gather x1, waiting for transfers between devices, on_device(): cache_all = lax.all_gather(kv_cache, 'gx', axis=0, tiled=True)  78.1 us
    all_gather x1, waiting for transfers between devices, on_device(): shard_piece = lax.all_gather(out_weight, 'gy', axis=0, tiled=True)  67.5 us
    pallas_call x1, Pallas kernels, tree_attention(): pl.pallas_call(attention_kernel, grid=(KV_HEADS,), in_specs=[pl.BlockSpec...  38.9 us
    gather x2, local copies, waits for them, and re-layouts, on_device(): normed[source_rows]  24.4 us
    gather x1, local copies, waits for them, and re-layouts, on_device(): returned.reshape(expert_count * capacity, model_width)[target]  12.4 us
    dot_general x1, matrix products, on_device(): jnp.einsum('tnr,nrd->ntd', columns, shard_piece.reshape(block_count, shar...  11.7 us
  transfers between devices with their start and end apart: 3, of which 3 were waited for; matrix products, arithmetic and copies ran while one was open for 3% of the time, Pallas kernels for 7%

profile of v1, /device:TPU:1, one launch (start us, length us, event | category | flops | bytes accessed | tf_op | source)
XLA Modules:
  0.0 570.0 jit_solution(7040413337037012869)
XLA Ops:
  13.0 1.4 fusion.12
  14.4 4.3 scatter_custom_fusion
  24.3 1.7 broadcast_select_fusion.1.bf_ref
  26.0 78.1 %all-gather.3.cloned.1.call-done.kc_ref.vc_ref = bf16[4096,1024]{1,0:T(8,128)(2,1)} async-done(((bf16[512,1024]{1,0:T(8,128)(2,1)}), bf16[4096,1024]{1,0:T(8,128)(2,1)}) %all-gather.3.cloned.1.call-update) | async-done | bytes 8388624 | tf_op jit(solution)/shard_map/all_gather | solution.py:127
  104.1 1.6 copy-done.1
  106.9 38.9 %shard_map.163 = bf16[128,4096]{1,0:T(8,128)(2,1)S(1)} custom-call(bf16[128,4096]{1,0:T(8,128)(2,1)S(1)} %copy-done.4, bf16[4096,1024]{1,0:T(8,128)(2,1)} %all-gather.3.cloned.1.call-done.kc_ref.vc_ref, bf16[4096,1024]{1,0:T(8,128)(2,1)} %all-gather.3.cloned.1.call-done.kc_ref.vc_ref, bf16[128,1024]{1,0:T(8,128)(2,1)S(1)} %copy-done.3, ...), custom_call_target="tpu_custom_call" | custom-call | tf_op jit(solution)/shard_map/pallas_call | solution.py:79
  146.9 67.5 %all-gather.5.cloned.1.call-done = bf16[4096,2048]{1,0:T(8,128)(2,1)} async-done(((bf16[256,2048]{1,0:T(8,128)(2,1)}), bf16[4096,2048]{1,0:T(8,128)(2,1)}) %all-gather.5.cloned.1.call-update) | async-done | bytes 16777232 | tf_op jit(solution)/shard_map/all_gather | solution.py:134
  214.4 11.7 %convolution_convert_fusion.1 = bf16[16,128,2048]{2,1,0:T(8,128)(2,1)} fusion(bf16[16,256,2048]{2,1,0:T(8,128)(2,1)} %bitcast.41, bf16[16,16,8,256]{3,2,1,0:T(8,128)(2,1)} %bitcast.40), kind=kOutput, calls=%fused_computation.9 | convolution fusion | flops 2151677952 | bytes 26214400 | tf_op jit(solution)/shard_map/tnr,nrd->ntd/dot_general | solution.py:137
  226.1 5.4 convert_reduce_fusion
  233.4 13.8 %gather_fusion = bf16[1536,2048]{1,0:T(8,128)(2,1)} fusion(bf16[128,2048]{1,0:T(8,128)(2,1)} %fusion.7, s32[2048]{0:T(1024)S(1)} %pad_clamp_fusion), kind=kCustom, calls=%fused_computation | custom fusion | bytes 12589056 | tf_op jit(solution)/shard_map/gather | solution.py:169
  247.2 10.6 %gather.9 = bf16[128,12,2048]{2,1,0:T(8,128)(2,1)} reshape(bf16[1536,2048]{1,0:T(8,128)(2,1)} %gather_fusion) | data formatting | bytes 12582912 | tf_op jit(solution)/shard_map/gather | solution.py:169
  257.8 7.3 %broadcast_select_fusion = bf16[128,12,2048]{2,1,0:T(8,128)(2,1)} fusion(bf16[128,12,2048]{2,1,0:T(8,128)(2,1)} %gather.9, pred[128,12]{1,0:T(8,128)(4,1)S(1)} %broadcast_in_dim.135), kind=kLoop, calls=%fused_computation.6 | loop fusion | flops 3145728 | bytes 12584448 | tf_op jit(solution)/shard_map/jit(_where)/select_n | solution.py:169
  265.0 103.1 %all_to_all.10 = bf16[128,12,2048]{2,1,0:T(8,128)(2,1)} all-to-all(bf16[128,12,2048]{2,1,0:T(8,128)(2,1)} %broadcast_select_fusion), channel_id=1, replica_groups=mesh['gx'=8,'gy'=16] {'gx','gy'}, dimensions={0} | all-to-all | bytes 12582912 | tf_op jit(solution)/shard_map/all_to_all | solution.py:171
  368.1 10.7 %reshape.115 = bf16[1536,2048]{1,0:T(8,128)(2,1)} reshape(bf16[128,12,2048]{2,1,0:T(8,128)(2,1)} %all_to_all.10) | data formatting | bytes 12582912 | tf_op jit(solution)/shard_map/reshape | solution.py:172
  378.8 8.2 %fusion.3 = f32[1536,768]{1,0:T(8,128)S(1)} fusion(bf16[1536,2048]{1,0:T(8,128)(2,1)} %reshape.115, bf16[1,2048,768]{2,1,0:T(8,128)(2,1)} %param.31), kind=kOutput, calls=%fused_computation.13 | convolution fusion | flops 4831838208 | bytes 14155776 | tf_op jit(solution)/shard_map/dot_general | solution.py:173
  387.1 5.6 multiply_convert_fusion
  392.7 7.1 %convolution_convert_fusion = bf16[1536,2048]{1,0:T(8,128)(2,1)} fusion(bf16[1536,768]{1,0:T(8,128)(2,1)S(1)} %multiply_convert_fusion, bf16[1,768,2048]{2,1,0:T(8,128)(2,1)S(1)} %copy-done), kind=kOutput, calls=%fused_computation.7 | convolution fusion | flops 4834983936 | bytes 11796480 | tf_op jit(solution)/shard_map/dot_general | solution.py:176
  399.8 10.6 %reshape.116 = bf16[128,12,2048]{2,1,0:T(8,128)(2,1)} reshape(bf16[1536,2048]{1,0:T(8,128)(2,1)} %convolution_convert_fusion) | data formatting | bytes 12582912 | tf_op jit(solution)/shard_map/reshape | solution.py:180
  410.4 8.3 %all-to-all-start.1 = ((bf16[128,12,2048]{2,1,0:T(8,128)(2,1)}), bf16[128,12,2048]{2,1,0:T(8,128)(2,1)}, u32[]{:S(2)}, u32[]{:S(2)}) async-start(bf16[128,12,2048]{2,1,0:T(8,128)(2,1)} %reshape.116), calls=%async_computation.1 | async-start | bytes 16777216 | tf_op jit(solution)/shard_map/all_to_all | solution.py:179
  418.8 112.7 %all-to-all-done.1 = bf16[128,12,2048]{2,1,0:T(8,128)(2,1)} async-done(((bf16[128,12,2048]{2,1,0:T(8,128)(2,1)}), bf16[128,12,2048]{2,1,0:T(8,128)(2,1)}, u32[]{:S(2)}, u32[]{:S(2)}) %all-to-all-start.1) | async-done | bytes 6291488 | tf_op jit(solution)/shard_map/all_to_all | solution.py:179
  531.5 10.7 %reshape.117 = bf16[1536,2048]{1,0:T(8,128)(2,1)} reshape(bf16[128,12,2048]{2,1,0:T(8,128)(2,1)} %all-to-all-done.1) | data formatting | bytes 12582912 | tf_op jit(solution)/shard_map/reshape | solution.py:182
  542.2 12.4 %gather_fusion.1 = bf16[1024,2048]{1,0:T(8,128)(2,1)} fusion(bf16[1536,2048]{1,0:T(8,128)(2,1)} %reshape.117, s32[1024]{0:T(1024)S(1)} %broadcast_clamp_fusion), kind=kCustom, calls=%fused_computation.1 | custom fusion | bytes 8392704 | tf_op jit(solution)/shard_map/gather | solution.py:182
  554.6 6.5 %fusion = f32[128,2048]{1,0:T(8,128)S(1)} fusion(bf16[1024,2048]{1,0:T(8,128)(2,1)} %gather_fusion.1, f32[128,8]{1,0:T(8,128)S(1)} %copy.35), kind=kLoop, calls=%fused_computation.5 | loop fusion | flops 6029312 | bytes 5246976 | tf_op jit(solution)/shard_map/reduce_sum | solution.py:185
  561.2 2.0 fusion.8
  (64 shorter events, 16.2 us)
Async XLA Ops:
  6.5 386.2 %copy-start = (bf16[1,768,2048]{2,1,0:T(8,128)(2,1)S(1)}, bf16[1,768,2048]{2,1,0:T(8,128)(2,1)}, u32[]{:S(2)}) copy-start(bf16[1,768,2048]{2,1,0:T(8,128)(2,1)} %param.33) | copy-start | bytes 9437188
  6.5 17.7 %copy-start.11 = (s32[1,128]{1,0:T(1,128)S(1)}, s32[1,128]{1,0:T(1,128)}, u32[]{:S(2)}) copy-start(s32[1,128]{1,0:T(1,128)} %param.21) | copy-start | bytes 1540
  6.5 97.6 %copy-start.3 = (bf16[128,1024]{1,0:T(8,128)(2,1)S(1)}, bf16[128,1024]{1,0:T(8,128)(2,1)}, u32[]{:S(2)}) copy-start(bf16[128,1024]{1,0:T(8,128)(2,1)} %vn_ref.1) | copy-start | bytes 786436
  6.5 97.6 %all-gather.3.cloned.1.call-start = ((), (), s32[]{:S(2)}) async-start(), calls=%async_computation.2 | async-start | bytes 9437184 | tf_op jit(solution)/shard_map/all_gather | solution.py:127
  7.3 207.1 %all-gather.5.cloned.1.call-start = ((), (), s32[]{:S(2)}) async-start(), calls=%async_computation.3 | async-start | bytes 17825792 | tf_op jit(solution)/shard_map/all_gather | solution.py:134
  9.3 0.8 copy-start.7
  104.1 1.6 copy-start.1
  105.7 1.2 copy-start.4
  145.9 1.1 copy-start.2
  226.1 5.4 copy-start.8
  226.1 6.3 %copy-start.9 = (f32[2048]{0:T(1024)S(1)}, f32[2048]{0:T(1024)}, u32[]{:S(2)}) copy-start(f32[2048]{0:T(1024)} %param.28) | copy-start | bytes 24580
  231.6 0.8 copy-start.5
  378.8 8.2 %copy-start.6 = (bf16[1536,2048]{1,0:T(8,128)(2,1)S(1)}, bf16[1536,2048]{1,0:T(8,128)(2,1)}, u32[]{:S(2)}) copy-start(bf16[1536,2048]{1,0:T(8,128)(2,1)} %reshape.115) | copy-start | bytes 18874372
  378.8 8.2 %copy-start.12 = (bf16[1,2048,768]{2,1,0:T(8,128)(2,1)S(1)}, bf16[1,2048,768]{2,1,0:T(8,128)(2,1)}, u32[]{:S(2)}) copy-start(bf16[1,2048,768]{2,1,0:T(8,128)(2,1)} %param.32) | copy-start | bytes 9437188
  410.4 8.3 %copy-start.10 = (f32[128,8]{0,1:T(8,128)S(1)}, f32[128,8]{0,1:T(8,128)}, u32[]{:S(2)}) copy-start(f32[128,8]{0,1:T(8,128)} %param.30) | copy-start | bytes 12292
  410.4 121.1 %all-to-all-start.1 = ((bf16[128,12,2048]{2,1,0:T(8,128)(2,1)}), bf16[128,12,2048]{2,1,0:T(8,128)(2,1)}, u32[]{:S(2)}, u32[]{:S(2)}) async-start(bf16[128,12,2048]{2,1,0:T(8,128)(2,1)} %reshape.116), calls=%async_computation.1 | async-start | bytes 16777216 | tf_op jit(solution)/shard_map/all_to_all | solution.py:179
Sparse Core Ops, SparseCore 0:
  9.0 95.0 all-gather.2
  106.6 107.7 all-gather.4

commit v2 on v1

--- a/solution.py
+++ b/solution.py
@@ -157,34 +157,43 @@
         jnp.int32
     )
     slot_ids = jnp.sum((jnp.cumsum(onehot, axis=0) - onehot) * onehot, axis=1)
-    target = flat_experts * capacity + slot_ids
-    assignments = tokens_here * top_count
-    source = (
-        jnp.full((expert_count * capacity,), -1, jnp.int32)
-        .at[target]
-        .set(jnp.arange(assignments, dtype=jnp.int32))
-    )
-    is_valid = source >= 0
-    source_rows = jnp.maximum(source, 0) // top_count
-    outgoing = jnp.where(is_valid[:, None], normed[source_rows], jnp.zeros((), jnp.bfloat16))
-    outgoing = outgoing.reshape(expert_count, capacity, model_width)
+    slot_ids = slot_ids.reshape(tokens_here, top_count)
+    slot_range = jnp.arange(capacity, dtype=jnp.int32)[:, None, None, None]
+    expert_range = jnp.arange(expert_count, dtype=jnp.int32)[None, None, :, None]
+    match = (slot_ids[None, :, None, :] == slot_range) & (route_experts[None, :, None, :] == expert_range)
+    pick = jnp.any(match, axis=3).astype(jnp.bfloat16)
+    weight_pick = jnp.sum(jnp.where(match, route_weights[None, :, None, :], 0.0), axis=3)
+    outgoing = jnp.concatenate(
+        [
+            jnp.dot(pick[slot].T, normed, preferred_element_type=jnp.float32).astype(jnp.bfloat16)
+            for slot in range(capacity)
+        ],
+        axis=1,
+    )
     arrived = lax.all_to_all(outgoing, ("gx", "gy"), split_axis=0, concat_axis=0, tiled=True)
-    stacked = arrived.reshape(-1, model_width)
+    stacked = jnp.concatenate(
+        [arrived[:, slot * model_width : (slot + 1) * model_width] for slot in range(capacity)], axis=0
+    )
     gate_act = jnp.dot(stacked, expert_gate[0], preferred_element_type=jnp.float32)
     up_act = jnp.dot(stacked, expert_up[0], preferred_element_type=jnp.float32)
     hidden = (jax.nn.silu(gate_act) * up_act).astype(jnp.bfloat16)
     expert_out = jnp.dot(hidden, expert_down[0], preferred_element_type=jnp.float32).astype(
         jnp.bfloat16
     )
-    returned = lax.all_to_all(
-        expert_out.reshape(arrived.shape), ("gx", "gy"), split_axis=0, concat_axis=0, tiled=True
-    )
-    picked_rows = returned.reshape(expert_count * capacity, model_width)[target].reshape(
-        tokens_here, top_count, model_width
-    )
-    routed_sum = jnp.sum(picked_rows.astype(jnp.float32) * route_weights[:, :, None], axis=1)
-    return (mixed_float + routed_sum).astype(jnp.bfloat16)
-
+    sources = arrived.shape[0]
+    backward = jnp.concatenate(
+        [expert_out[slot * sources : (slot + 1) * sources] for slot in range(capacity)], axis=1
+    )
+    returned = lax.all_to_all(backward, ("gx", "gy"), split_axis=0, concat_axis=0, tiled=True)
+    routed_sum = mixed_float
+    for slot in range(capacity):
+        routed_sum = routed_sum + jnp.dot(
+            weight_pick[slot],
+            returned[:, slot * model_width : (slot + 1) * model_width].astype(jnp.float32),
+            precision=lax.Precision.HIGHEST,
+            preferred_element_type=jnp.float32,
+        )
+    return routed_sum.astype(jnp.bfloat16)
 
 def solution(mesh):
     in_specs = (

time: 572 us -> 606 us (1.059)
  local copies, waits for them, and re-layouts: 80.8 us -> 141 us
  waiting for transfers between devices: 260 us -> 213 us
  blocking collectives: 103 us -> 81.2 us
  matrix products: 32.6 us -> 53.3 us
  other arithmetic: 32.9 us -> 51.6 us
    unnamed x28 -> x72, local copies, waits for them, and re-layouts: 6.17 us -> 138 us
    all_to_all x1, waiting for transfers between devices: 113 us -> 71.6 us  [on_device(): lax.all_to_all(backward, ('gx', 'gy'), split_axis=0, concat_axis=0, tiled...]
    gather x3 -> x0, local copies, waits for them, and re-layouts: 36.8 us -> none  [the longest x2 24.4 us: on_device(): normed[source_rows]]
    reshape x3 -> x0, local copies, waits for them, and re-layouts: 32 us -> none  [the longest x1 10.7 us: on_device(): stacked = arrived.reshape(-1, model_width)]
    dot_general x0 -> x24, matrix products: none -> 25.3 us  [the longest x12 14.3 us: on_device(): jnp.dot(pick[slot].T, normed, preferred_element_type=jnp.float32)]
    all_to_all x1, blocking collectives: 103 us -> 81.2 us  [on_device(): lax.all_to_all(outgoing, ('gx', 'gy'), split_axis=0, concat_axis=0, tiled...]
    all_to_all x0 -> x2, other arithmetic: none -> 17.9 us  [the longest x1 8.95 us: on_device(): lax.all_to_all(outgoing, ('gx', 'gy'), split_axis=0, concat_axis=0, tiled...]
    reduce_or x0 -> x1, other arithmetic: none -> 9.26 us  [on_device(): pick = jnp.any(match, axis=3).astype(jnp.bfloat16)]
  transfers between devices with their start and end apart: 3 -> 3, of which waited for: 3 -> 3; matrix products, arithmetic and copies ran while one was open for 3% -> 5% of each run, Pallas kernels for 7% -> 6%
where the time goes in v2:
time: 606 us; the launch traced here: 601 us
  waiting for transfers between devices  213 us (35%)
  local copies, waits for them, and re-layouts  141 us (23%)
  blocking collectives  81.2 us (13%)
  matrix products  53.3 us (9%)
  other arithmetic  51.6 us (9%)
  Pallas kernels  39 us (6%)
  between operations  14.1 us (2%)
  starting transfers between devices  7.59 us (1%)
    unnamed x72, local copies, waits for them, and re-layouts  138 us
    all_to_all x1, blocking collectives, on_device(): lax.all_to_all(outgoing, ('gx', 'gy'), split_axis=0, concat_axis=0, tiled...  81.2 us
    all_gather x1, waiting for transfers between devices, on_device(): cache_all = lax.all_gather(kv_cache, 'gx', axis=0, tiled=True)  72.7 us
    all_to_all x1, waiting for transfers between devices, on_device(): lax.all_to_all(backward, ('gx', 'gy'), split_axis=0, concat_axis=0, tiled...  71.6 us
    all_gather x1, waiting for transfers between devices, on_device(): shard_piece = lax.all_gather(out_weight, 'gy', axis=0, tiled=True)  67.4 us
    pallas_call x1, Pallas kernels, tree_attention(): pl.pallas_call(attention_kernel, grid=(KV_HEADS,), in_specs=[pl.BlockSpec...  39 us
    dot_general x12, matrix products, on_device(): jnp.dot(pick[slot].T, normed, preferred_element_type=jnp.float32)  14.3 us
  transfers between devices with their start and end apart: 3, of which 3 were waited for; matrix products, arithmetic and copies ran while one was open for 5% of the time, Pallas kernels for 6%

profile of v2, /device:TPU:1, one launch (start us, length us, event | category | flops | bytes accessed | tf_op | source)
XLA Modules:
  0.0 600.5 jit_solution(4938949325512270133)
XLA Ops:
  20.5 9.3 %and_reduce_fusion = pred[12,128,128]{2,1,0:T(8,128)(4,1)} fusion(pred[128,128,8]{1,2,0:T(8,128)(4,1)S(1)} %iota_compare_fusion.1, pred[12,128,8]{2,1,0:T(8,128)(4,1)S(1)} %iota_compare_fusion), kind=kLoop, calls=%fused_computation.1 | loop fusion | flops 2949120 | bytes 339968 | tf_op jit(solution)/shard_map/reduce_or | solution.py:164
  29.7 1.7 broadcast_select_fusion.bf_ref
  31.4 72.7 %all-gather.3.cloned.1.call-done.kc_ref.vc_ref = bf16[4096,1024]{1,0:T(8,128)(2,1)} async-done(((bf16[512,1024]{1,0:T(8,128)(2,1)}), bf16[4096,1024]{1,0:T(8,128)(2,1)}) %all-gather.3.cloned.1.call-update) | async-done | bytes 8388624 | tf_op jit(solution)/shard_map/all_gather | solution.py:127
  106.9 39.0 %shard_map.163 = bf16[128,4096]{1,0:T(8,128)(2,1)S(1)} custom-call(bf16[128,4096]{1,0:T(8,128)(2,1)S(1)} %copy-done.4, bf16[4096,1024]{1,0:T(8,128)(2,1)} %all-gather.3.cloned.1.call-done.kc_ref.vc_ref, bf16[4096,1024]{1,0:T(8,128)(2,1)} %all-gather.3.cloned.1.call-done.kc_ref.vc_ref, bf16[128,1024]{1,0:T(8,128)(2,1)S(1)} %copy-done.3, ...), custom_call_target="tpu_custom_call" | custom-call | tf_op jit(solution)/shard_map/pallas_call | solution.py:79
  147.0 67.4 %all-gather.5.cloned.1.call-done = bf16[4096,2048]{1,0:T(8,128)(2,1)} async-done(((bf16[256,2048]{1,0:T(8,128)(2,1)}), bf16[4096,2048]{1,0:T(8,128)(2,1)}) %all-gather.5.cloned.1.call-update) | async-done | bytes 16777232 | tf_op jit(solution)/shard_map/all_gather | solution.py:134
  214.4 11.7 %convolution_convert_fusion.1 = bf16[16,128,2048]{2,1,0:T(8,128)(2,1)} fusion(bf16[16,256,2048]{2,1,0:T(8,128)(2,1)} %bitcast.116, bf16[16,16,8,256]{3,2,1,0:T(8,128)(2,1)} %bitcast.115), kind=kOutput, calls=%fused_computation.8 | convolution fusion | flops 2151677952 | bytes 26214400 | tf_op jit(solution)/shard_map/tnr,nrd->ntd/dot_general | solution.py:137
  226.1 5.4 convert_reduce_fusion
  246.6 8.9 %reduce = bf16[128,24576]{1,0:T(8,128)(2,1)} reduce(bf16[128,1,24576]{2,0,1:T(8,128)(2,1)} %bitcast.22, bf16[]{:T(256)} %broadcast.87), dimensions={1}, to_apply=%copy.57.reduce_sub_computation | reduce | bytes 12582914 | tf_op jit(solution)/shard_map/all_to_all | solution.py:173
  255.6 9.3 %reshape.86 = bf16[128,2,12288]{2,1,0:T(2,128)(2,1)} reshape(bf16[128,24576]{1,0:T(8,128)(2,1)} %reduce) | data formatting | bytes 12582912
  264.9 81.2 %all_to_all.24 = bf16[128,2,12288]{2,1,0:T(2,128)(2,1)} all-to-all(bf16[128,2,12288]{2,1,0:T(2,128)(2,1)} %reshape.86), channel_id=1, replica_groups=mesh['gx'=8,'gy'=16] {'gx','gy'}, dimensions={0} | all-to-all | bytes 12582912 | tf_op jit(solution)/shard_map/all_to_all | solution.py:173
  346.1 34.3 %reshape.87 = bf16[128,1,24576]{2,1,0:T(2,128)(2,1)} reshape(bf16[128,2,12288]{2,1,0:T(2,128)(2,1)} %all_to_all.24) | data formatting | bytes 12582912
  380.3 14.0 %copy.69 = bf16[128,1,24576]{2,0,1:T(8,128)(2,1)} copy(bf16[128,1,24576]{2,1,0:T(2,128)(2,1)} %reshape.87) | data formatting | bytes 12582912
  402.0 5.4 fusion.3
  407.4 5.6 multiply_convert_fusion
  413.0 5.4 convolution_convert_fusion
  428.4 8.9 %reduce.1 = bf16[128,24576]{1,0:T(8,128)(2,1)} reduce(bf16[128,1,24576]{2,0,1:T(8,128)(2,1)} %bitcast.26, bf16[]{:T(256)} %broadcast.87), dimensions={1}, to_apply=%copy.58.reduce_sub_computation | reduce | bytes 12582914 | tf_op jit(solution)/shard_map/all_to_all | solution.py:187
  437.3 9.4 %reshape.88 = bf16[128,2,12288]{2,1,0:T(2,128)(2,1)} reshape(bf16[128,24576]{1,0:T(8,128)(2,1)} %reduce.1) | data formatting | bytes 12582912
  446.7 7.5 %all-to-all-start.1 = ((bf16[128,2,12288]{2,1,0:T(2,128)(2,1)}), bf16[128,2,12288]{2,1,0:T(2,128)(2,1)}, u32[]{:S(2)}, u32[]{:S(2)}) async-start(bf16[128,2,12288]{2,1,0:T(2,128)(2,1)} %reshape.88), calls=%async_computation.1 | async-start | bytes 12582912 | tf_op jit(solution)/shard_map/all_to_all | solution.py:187
  454.4 8.1 %fusion = f32[12,128,128]{2,1,0:T(8,128)} fusion(f32[128,8]{1,0:T(8,128)S(1)} %copy.56, pred[128,128,8]{1,2,0:T(8,128)(4,1)S(1)} %copy-done.14, pred[12,128,8]{2,1,0:T(8,128)(4,1)S(1)} %copy-done.12), kind=kLoop, calls=%fused_computation.4 | loop fusion | flops 4521984 | bytes 933888 | tf_op jit(solution)/shard_map/reduce_sum | solution.py:165
  462.5 71.6 %all-to-all-done.1 = bf16[128,2,12288]{2,1,0:T(2,128)(2,1)} async-done(((bf16[128,2,12288]{2,1,0:T(2,128)(2,1)}), bf16[128,2,12288]{2,1,0:T(2,128)(2,1)}, u32[]{:S(2)}, u32[]{:S(2)}) %all-to-all-start.1) | async-done | bytes 6291488 | tf_op jit(solution)/shard_map/all_to_all | solution.py:187
  534.2 34.0 %reshape.89 = bf16[128,1,24576]{2,1,0:T(2,128)(2,1)} reshape(bf16[128,2,12288]{2,1,0:T(2,128)(2,1)} %all-to-all-done.1) | data formatting | bytes 12582912
  568.2 14.1 %copy.68 = bf16[128,1,24576]{2,0,1:T(8,128)(2,1)} copy(bf16[128,1,24576]{2,1,0:T(2,128)(2,1)} %reshape.89) | data formatting | bytes 12582912
  582.3 1.8 convolution_add_fusion.11
  584.1 1.8 convolution_add_fusion.10
  (121 shorter events, 58.0 us)
Async XLA Ops:
  6.5 406.5 %copy-start = (bf16[1,768,2048]{2,1,0:T(8,128)(2,1)S(1)}, bf16[1,768,2048]{2,1,0:T(8,128)(2,1)}, u32[]{:S(2)}) copy-start(bf16[1,768,2048]{2,1,0:T(8,128)(2,1)} %param.33) | copy-start | bytes 9437188
  6.5 97.6 %copy-start.3 = (bf16[128,1024]{1,0:T(8,128)(2,1)S(1)}, bf16[128,1024]{1,0:T(8,128)(2,1)}, u32[]{:S(2)}) copy-start(bf16[128,1024]{1,0:T(8,128)(2,1)} %vn_ref.1) | copy-start | bytes 786436
  6.5 97.6 %all-gather.3.cloned.1.call-start = ((), (), s32[]{:S(2)}) async-start(), calls=%async_computation.2 | async-start | bytes 9437184 | tf_op jit(solution)/shard_map/all_gather | solution.py:127
  7.3 207.1 %all-gather.5.cloned.1.call-start = ((), (), s32[]{:S(2)}) async-start(), calls=%async_computation.3 | async-start | bytes 17825792 | tf_op jit(solution)/shard_map/all_gather | solution.py:134
  9.3 0.8 copy-start.10
  18.8 1.0 copy-start.13
  19.8 0.7 copy-start.11
  104.1 1.6 copy-start.1
  105.7 1.2 copy-start.4
  145.9 1.1 copy-start.2
  226.1 5.4 copy-start.15
  226.1 5.7 copy-start.16
  226.1 5.7 copy-start.20
  231.6 13.3 %copy-start.7 = (bf16[128,2048]{1,0:T(8,128)(2,1)}, bf16[128,2048]{1,0:T(8,128)(2,1)S(1)}, u32[]{:S(2)}) copy-start(bf16[128,2048]{1,0:T(8,128)(2,1)S(1)} %add_convert_fusion) | copy-start | bytes 1572868
  394.3 7.4 %copy-start.6 = (bf16[128,1,24576]{2,0,1:T(8,128)(2,1)S(1)}, bf16[128,1,24576]{2,0,1:T(8,128)(2,1)}, u32[]{:S(2)}) copy-start(bf16[128,1,24576]{2,0,1:T(8,128)(2,1)} %copy.69) | copy-start | bytes 18874372
  394.3 7.6 %copy-start.18 = (bf16[1,2048,768]{2,1,0:T(8,128)(2,1)S(1)}, bf16[1,2048,768]{2,1,0:T(8,128)(2,1)}, u32[]{:S(2)}) copy-start(bf16[1,2048,768]{2,1,0:T(8,128)(2,1)} %param.31) | copy-start | bytes 9437188
  402.0 5.4 copy-start.19
  446.7 7.6 %copy-start.17 = (f32[128,8]{0,1:T(8,128)S(1)}, f32[128,8]{0,1:T(8,128)}, u32[]{:S(2)}) copy-start(f32[128,8]{0,1:T(8,128)} %param.30) | copy-start | bytes 12292
  446.7 7.7 %copy-start.12 = (pred[12,128,8]{2,1,0:T(8,128)(4,1)S(1)}, pred[12,128,8]{2,1,0:T(8,128)(4,1)}, u32[]{:S(2)}) copy-start(pred[12,128,8]{2,1,0:T(8,128)(4,1)} %copy-done.11) | copy-start | bytes 36868
  446.7 7.7 %copy-start.14 = (pred[128,128,8]{1,2,0:T(8,128)(4,1)S(1)}, pred[128,128,8]{1,2,0:T(8,128)(4,1)}, u32[]{:S(2)}) copy-start(pred[128,128,8]{1,2,0:T(8,128)(4,1)} %copy-done.13) | copy-start | bytes 393220
  446.7 87.4 %all-to-all-start.1 = ((bf16[128,2,12288]{2,1,0:T(2,128)(2,1)}), bf16[128,2,12288]{2,1,0:T(2,128)(2,1)}, u32[]{:S(2)}, u32[]{:S(2)}) async-start(bf16[128,2,12288]{2,1,0:T(2,128)(2,1)} %reshape.88), calls=%async_computation.1 | async-start | bytes 12582912 | tf_op jit(solution)/shard_map/all_to_all | solution.py:187
  568.2 14.1 %copy-start.8 = (bf16[128,2048]{1,0:T(8,128)(2,1)S(1)}, bf16[128,2048]{1,0:T(8,128)(2,1)}, u32[]{:S(2)}) copy-start(bf16[128,2048]{1,0:T(8,128)(2,1)} %copy-done.7) | copy-start | bytes 1572868
  568.2 14.1 %copy-start.9 = (f32[12,128,128]{2,1,0:T(8,128)S(1)}, f32[12,128,128]{2,1,0:T(8,128)}, u32[]{:S(2)}) copy-start(f32[12,128,128]{2,1,0:T(8,128)} %fusion) | copy-start | bytes 2359300
  582.3 5.2 copy-start.5
Sparse Core Ops, SparseCore 0:
  9.0 95.0 all-gather.2
  106.6 107.7 all-gather.4

commit v3 on v1

--- a/solution.py
+++ b/solution.py
@@ -152,22 +152,21 @@
     top_count = route_experts.shape[1]
     expert_count = lax.axis_size("gx") * lax.axis_size("gy") * expert_gate.shape[0]
     capacity = max(2, (3 * tokens_here * top_count + 2 * expert_count - 1) // (2 * expert_count))
+    slots = -(-capacity // 16) * 16
     flat_experts = route_experts.reshape(-1)
     onehot = (flat_experts[:, None] == jnp.arange(expert_count, dtype=jnp.int32)[None, :]).astype(
         jnp.int32
     )
     slot_ids = jnp.sum((jnp.cumsum(onehot, axis=0) - onehot) * onehot, axis=1)
-    target = flat_experts * capacity + slot_ids
-    assignments = tokens_here * top_count
-    source = (
-        jnp.full((expert_count * capacity,), -1, jnp.int32)
-        .at[target]
-        .set(jnp.arange(assignments, dtype=jnp.int32))
-    )
-    is_valid = source >= 0
-    source_rows = jnp.maximum(source, 0) // top_count
-    outgoing = jnp.where(is_valid[:, None], normed[source_rows], jnp.zeros((), jnp.bfloat16))
-    outgoing = outgoing.reshape(expert_count, capacity, model_width)
+    target = (flat_experts * slots + slot_ids).reshape(tokens_here, top_count)
+    row_range = jnp.arange(expert_count * slots, dtype=jnp.int32)
+    pick = jnp.any(target[None, :, :] == row_range[:, None, None], axis=2).astype(jnp.bfloat16)
+    weight_pick = jnp.sum(
+        jnp.where(target[:, None, :] == row_range[None, :, None], route_weights[:, None, :], 0.0),
+        axis=2,
+    )
+    outgoing = jnp.dot(pick, normed, preferred_element_type=jnp.float32).astype(jnp.bfloat16)
+    outgoing = outgoing.reshape(expert_count, slots, model_width)
     arrived = lax.all_to_all(outgoing, ("gx", "gy"), split_axis=0, concat_axis=0, tiled=True)
     stacked = arrived.reshape(-1, model_width)
     gate_act = jnp.dot(stacked, expert_gate[0], preferred_element_type=jnp.float32)
@@ -179,12 +178,13 @@
     returned = lax.all_to_all(
         expert_out.reshape(arrived.shape), ("gx", "gy"), split_axis=0, concat_axis=0, tiled=True
     )
-    picked_rows = returned.reshape(expert_count * capacity, model_width)[target].reshape(
-        tokens_here, top_count, model_width
-    )
-    routed_sum = jnp.sum(picked_rows.astype(jnp.float32) * route_weights[:, :, None], axis=1)
+    routed_sum = jnp.dot(
+        weight_pick,
+        returned.reshape(-1, model_width).astype(jnp.float32),
+        precision=lax.Precision.HIGHEST,
+        preferred_element_type=jnp.float32,
+    )
     return (mixed_float + routed_sum).astype(jnp.bfloat16)
-
 
 def solution(mesh):
     in_specs = (

time: 572 us -> 513 us (0.90)
  local copies, waits for them, and re-layouts: 80.8 us -> 9.43 us
  matrix products: 32.6 us -> 52 us
  other arithmetic: 32.9 us -> 26.3 us
    gather x3 -> x0, local copies, waits for them, and re-layouts: 36.8 us -> none  [the longest x2 24.4 us: on_device(): normed[source_rows]]
    reshape x3 -> x0, local copies, waits for them, and re-layouts: 32 us -> none  [the longest x1 10.7 us: on_device(): stacked = arrived.reshape(-1, model_width)]
    dot_general x1, matrix products: 7.09 us -> 21.3 us  [on_device(): jnp.dot(hidden, expert_down[0], preferred_element_type=jnp.float32)]
    reduce_or x0 -> x1, other arithmetic: none -> 8.14 us  [on_device(): jnp.any(target[None, :, :] == row_range[:, None, None], axis=2)]
    select_n x3 -> x0, other arithmetic: 7.27 us -> none  [the longest x1 7.25 us: on_device(): jnp.where(is_valid[:, None], normed[source_rows], jnp.zeros((), jnp.bfloa...]
  transfers between devices with their start and end apart: 3 -> 3, of which waited for: 3 -> 3; matrix products, arithmetic and copies ran while one was open for 3% -> 4% of each run, Pallas kernels for 7% -> 8%
where the time goes in v3:
time: 513 us; the launch traced here: 508 us
  waiting for transfers between devices  255 us (50%)
  blocking collectives  103 us (20%)
  matrix products  52 us (10%)
  Pallas kernels  39.5 us (8%)
  other arithmetic  26.3 us (5%)
  between operations  13.9 us (3%)
  local copies, waits for them, and re-layouts  9.43 us (2%)
  starting transfers between devices  8.87 us (2%)
    all_to_all x1, waiting for transfers between devices, on_device(): lax.all_to_all(expert_out.reshape(arrived.shape), ('gx', 'gy'), split_axi...  109 us
    all_to_all x1, blocking collectives, on_device(): lax.all_to_all(outgoing, ('gx', 'gy'), split_axis=0, concat_axis=0, tiled...  103 us
    all_gather x1, waiting for transfers between devices, on_device(): cache_all = lax.all_gather(kv_cache, 'gx', axis=0, tiled=True)  77 us
    all_gather x1, waiting for transfers between devices, on_device(): shard_piece = lax.all_gather(out_weight, 'gy', axis=0, tiled=True)  66.9 us
    pallas_call x1, Pallas kernels, tree_attention(): pl.pallas_call(attention_kernel, grid=(KV_HEADS,), in_specs=[pl.BlockSpec...  39.5 us
    dot_general x1, matrix products, on_device(): jnp.dot(hidden, expert_down[0], preferred_element_type=jnp.float32)  21.3 us
    dot_general x1, matrix products, on_device(): jnp.einsum('tnr,nrd->ntd', columns, shard_piece.reshape(block_count, shar...  11.7 us
  transfers between devices with their start and end apart: 3, of which 3 were waited for; matrix products, arithmetic and copies ran while one was open for 4% of the time, Pallas kernels for 8%

profile of v3, /device:TPU:1, one launch (start us, length us, event | category | flops | bytes accessed | tf_op | source)
XLA Modules:
  0.0 507.5 jit_solution(16064664991194476042)
XLA Ops:
  8.0 0.8 copy.42
  9.3 0.8 copy-done.7
  10.1 1.1 broadcast_add_fusion
  14.1 0.9 select_reduce_fusion.2
  15.9 1.3 compare_reduce_fusion
  17.2 8.1 %fusion = pred[2048,128]{1,0:T(8,128)(4,1)} fusion(s32[128,8]{0,1:T(8,128)S(1)} %multiply_add_fusion), kind=kLoop, calls=%fused_computation.4 | loop fusion | flops 3932160 | bytes 266240 | tf_op jit(solution)/shard_map/reduce_or | solution.py:163
  25.4 1.7 broadcast_select_fusion.bf_ref
  27.1 77.0 %all-gather.3.cloned.1.call-done.kc_ref.vc_ref = bf16[4096,1024]{1,0:T(8,128)(2,1)} async-done(((bf16[512,1024]{1,0:T(8,128)(2,1)}), bf16[4096,1024]{1,0:T(8,128)(2,1)}) %all-gather.3.cloned.1.call-update) | async-done | bytes 8388624 | tf_op jit(solution)/shard_map/all_gather | solution.py:127
  104.1 1.6 copy-done.1
  105.7 1.2 copy-done.4
  106.9 39.5 %shard_map.163 = bf16[128,4096]{1,0:T(8,128)(2,1)S(1)} custom-call(bf16[128,4096]{1,0:T(8,128)(2,1)S(1)} %copy-done.4, bf16[4096,1024]{1,0:T(8,128)(2,1)} %all-gather.3.cloned.1.call-done.kc_ref.vc_ref, bf16[4096,1024]{1,0:T(8,128)(2,1)} %all-gather.3.cloned.1.call-done.kc_ref.vc_ref, bf16[128,1024]{1,0:T(8,128)(2,1)S(1)} %copy-done.3, ...), custom_call_target="tpu_custom_call" | custom-call | tf_op jit(solution)/shard_map/pallas_call | solution.py:79
  146.4 1.1 copy-done.2
  147.5 66.9 %all-gather.5.cloned.1.call-done = bf16[4096,2048]{1,0:T(8,128)(2,1)} async-done(((bf16[256,2048]{1,0:T(8,128)(2,1)}), bf16[4096,2048]{1,0:T(8,128)(2,1)}) %all-gather.5.cloned.1.call-update) | async-done | bytes 16777232 | tf_op jit(solution)/shard_map/all_gather | solution.py:134
  214.4 11.7 %convolution_convert_fusion.2 = bf16[16,128,2048]{2,1,0:T(8,128)(2,1)} fusion(bf16[16,256,2048]{2,1,0:T(8,128)(2,1)} %bitcast.44, bf16[16,16,8,256]{3,2,1,0:T(8,128)(2,1)} %bitcast.42), kind=kOutput, calls=%fused_computation.9 | convolution fusion | flops 2151677952 | bytes 26214400 | tf_op jit(solution)/shard_map/tnr,nrd->ntd/dot_general | solution.py:137
  226.1 5.4 %convert_reduce_fusion = f32[128,2048]{1,0:T(8,128)S(1)} fusion(bf16[16,128,2048]{2,1,0:T(8,128)(2,1)} %convolution_convert_fusion.2), kind=kLoop, calls=%fused_computation | loop fusion | flops 8126464 | bytes 9437184 | tf_op jit(solution)/shard_map/reduce_sum | solution.py:144
  231.9 2.4 convolution_convert_fusion.1
  234.3 103.0 %all_to_all.10 = bf16[128,16,2048]{2,1,0:T(8,128)(2,1)S(1)} all-to-all(bf16[128,16,2048]{2,1,0:T(8,128)(2,1)S(1)} %bitcast.43), channel_id=1, replica_groups=mesh['gx'=8,'gy'=16] {'gx','gy'}, dimensions={0} | all-to-all | bytes 16777216 | tf_op jit(solution)/shard_map/all_to_all | solution.py:170
  337.3 3.2 copy-done.6
  340.5 8.6 %fusion.4 = f32[2048,768]{1,0:T(8,128)} fusion(bf16[2048,2048]{1,0:T(8,128)(2,1)S(1)} %bitcast.46, bf16[1,2048,768]{2,1,0:T(8,128)(2,1)S(1)} %copy-done.14), kind=kOutput, calls=%fused_computation.12 | convolution fusion | flops 6442450944 | bytes 17825792 | tf_op jit(solution)/shard_map/dot_general | solution.py:172
  349.1 21.3 %convolution_convert_fusion = bf16[2048,2048]{1,0:T(8,128)(2,1)} fusion(f32[2048,768]{1,0:T(8,128)} %fusion.4, bf16[2048,2048]{1,0:T(8,128)(2,1)} %bitcast.47, bf16[1,768,2048]{2,1,0:T(8,128)(2,1)S(1)} %copy-done, bf16[1,2048,768]{2,1,0:T(8,128)(2,1)} %param.32), kind=kOutput, calls=%fused_computation.5 | convolution fusion | flops 12898533376 | bytes 29360128 | tf_op jit(solution)/shard_map/dot_general | solution.py:175
  370.4 8.8 %all-to-all-start.1 = ((bf16[128,16,2048]{2,1,0:T(8,128)(2,1)}), bf16[128,16,2048]{2,1,0:T(8,128)(2,1)}, u32[]{:S(2)}, u32[]{:S(2)}) async-start(bf16[128,16,2048]{2,1,0:T(8,128)(2,1)} %bitcast.45), calls=%async_computation.1 | async-start | bytes 16777216 | tf_op jit(solution)/shard_map/all_to_all | solution.py:178
  379.4 3.7 select_reduce_fusion
  383.1 109.3 %all-to-all-done.1 = bf16[128,16,2048]{2,1,0:T(8,128)(2,1)} async-done(((bf16[128,16,2048]{2,1,0:T(8,128)(2,1)}), bf16[128,16,2048]{2,1,0:T(8,128)(2,1)}, u32[]{:S(2)}, u32[]{:S(2)}) %all-to-all-start.1) | async-done | bytes 8388640 | tf_op jit(solution)/shard_map/all_to_all | solution.py:178
  492.4 8.0 %fusion.7 = bf16[128,2048]{1,0:T(8,128)(2,1)} fusion(f32[128,2048]{1,0:T(8,128)} %select_reduce_fusion, bf16[2048,2048]{1,0:T(8,128)(2,1)} %bitcast.15, bf16[128,2048]{1,0:T(8,128)(2,1)} %copy-done.5), kind=kOutput, calls=%fused_computation.16 | convolution fusion | flops 6443237376 | bytes 10485760 | tf_op jit(solution)/shard_map/dot_general | solution.py:181
  (54 shorter events, 6.3 us)
Async XLA Ops:
  6.5 342.6 %copy-start = (bf16[1,768,2048]{2,1,0:T(8,128)(2,1)S(1)}, bf16[1,768,2048]{2,1,0:T(8,128)(2,1)}, u32[]{:S(2)}) copy-start(bf16[1,768,2048]{2,1,0:T(8,128)(2,1)} %param.33) | copy-start | bytes 9437188
  6.5 10.6 %copy-start.10 = (s32[128,8]{0,1:T(8,128)S(1)}, s32[128,8]{0,1:T(8,128)}, u32[]{:S(2)}) copy-start(s32[128,8]{0,1:T(8,128)} %param.29) | copy-start | bytes 12292
  6.5 18.8 %copy-start.13 = (s32[1,128]{1,0:T(1,128)S(1)}, s32[1,128]{1,0:T(1,128)}, u32[]{:S(2)}) copy-start(s32[1,128]{1,0:T(1,128)} %param.21) | copy-start | bytes 1540
  6.5 97.6 %copy-start.3 = (bf16[128,1024]{1,0:T(8,128)(2,1)S(1)}, bf16[128,1024]{1,0:T(8,128)(2,1)}, u32[]{:S(2)}) copy-start(bf16[128,1024]{1,0:T(8,128)(2,1)} %vn_ref.1) | copy-start | bytes 786436
  6.5 97.6 %all-gather.3.cloned.1.call-start = ((), (), s32[]{:S(2)}) async-start(), calls=%async_computation.2 | async-start | bytes 9437184 | tf_op jit(solution)/shard_map/all_gather | solution.py:127
  7.3 207.1 %all-gather.5.cloned.1.call-start = ((), (), s32[]{:S(2)}) async-start(), calls=%async_computation.3 | async-start | bytes 17825792 | tf_op jit(solution)/shard_map/all_gather | solution.py:134
  9.3 0.8 copy-start.7
  104.1 1.6 copy-start.1
  105.7 1.2 copy-start.4
  146.4 1.1 copy-start.2
  226.1 5.4 %copy-start.9 = (bf16[128,2048]{1,0:T(8,128)(2,1)S(1)}, bf16[128,2048]{1,0:T(8,128)(2,1)}, u32[]{:S(2)}) copy-start(bf16[128,2048]{1,0:T(8,128)(2,1)} %param.20) | copy-start | bytes 1572868
  226.1 5.8 %copy-start.8 = (pred[2048,128]{1,0:T(8,128)(4,1)S(1)}, pred[2048,128]{1,0:T(8,128)(4,1)}, u32[]{:S(2)}) copy-start(pred[2048,128]{1,0:T(8,128)(4,1)} %fusion) | copy-start | bytes 786436
  226.1 5.8 %copy-start.11 = (f32[2048]{0:T(1024)S(1)}, f32[2048]{0:T(1024)}, u32[]{:S(2)}) copy-start(f32[2048]{0:T(1024)} %param.28) | copy-start | bytes 24580
  231.6 2.6 copy-start.5
  234.3 106.2 %copy-start.14 = (bf16[1,2048,768]{2,1,0:T(8,128)(2,1)S(1)}, bf16[1,2048,768]{2,1,0:T(8,128)(2,1)}, u32[]{:S(2)}) copy-start(bf16[1,2048,768]{2,1,0:T(8,128)(2,1)} %param.31) | copy-start | bytes 9437188
  337.3 3.2 copy-start.6
  370.4 8.9 %copy-start.12 = (f32[128,8]{0,1:T(8,128)S(1)}, f32[128,8]{0,1:T(8,128)}, u32[]{:S(2)}) copy-start(f32[128,8]{0,1:T(8,128)} %param.30) | copy-start | bytes 12292
  370.4 122.0 %all-to-all-start.1 = ((bf16[128,16,2048]{2,1,0:T(8,128)(2,1)}), bf16[128,16,2048]{2,1,0:T(8,128)(2,1)}, u32[]{:S(2)}, u32[]{:S(2)}) async-start(bf16[128,16,2048]{2,1,0:T(8,128)(2,1)} %bitcast.45), calls=%async_computation.1 | async-start | bytes 16777216 | tf_op jit(solution)/shard_map/all_to_all | solution.py:178
Sparse Core Ops, SparseCore 0:
  9.0 95.0 all-gather.2
  106.6 107.7 all-gather.4

commit v4 on v3

--- a/solution.py
+++ b/solution.py
@@ -131,17 +131,24 @@
     near_bias = jnp.where(own_mask, 0.0, -jnp.inf).astype(jnp.float32)
     attended = tree_attention(queries, cache_all, new_kv, far_bias, near_bias)
     shard_rows = out_weight.shape[0]
-    shard_piece = lax.all_gather(out_weight, "gy", axis=0, tiled=True)
-    block_count = shard_piece.shape[0] // shard_rows
-    columns = attended.reshape(tokens_here, block_count, shard_rows)
+    core = lax.axis_index("core")
+    swap = [(0, 1), (1, 0)]
+    parity_rows = lax.all_gather(out_weight, "gyo", axis=0, tiled=False)
+    partner = lax.ppermute(attended, "core", swap)
+    pair = jnp.concatenate([attended, partner], axis=0)
+    columns = jnp.stack(
+        [
+            lax.dynamic_slice_in_dim(pair, (2 * group + core) * shard_rows, shard_rows, axis=1)
+            for group in range(parity_rows.shape[0])
+        ],
+        axis=1,
+    )
     partial_value = jnp.einsum(
-        "tnr,nrd->ntd",
-        columns,
-        shard_piece.reshape(block_count, shard_rows, model_width),
-        preferred_element_type=jnp.float32,
+        "tnr,nrd->ntd", columns, parity_rows, preferred_element_type=jnp.float32
     )
     partial_value = lax.optimization_barrier(partial_value.astype(jnp.bfloat16))
-    projected = jnp.sum(partial_value.astype(jnp.float32), axis=0)
+    pair_sum = jnp.sum(partial_value.astype(jnp.float32), axis=0)
+    projected = pair_sum[:tokens_here] + lax.ppermute(pair_sum[tokens_here:], "core", swap)
     mixed_state = (residual.astype(jnp.float32) + projected).astype(jnp.bfloat16)
     mixed_float = lax.optimization_barrier(mixed_state).astype(jnp.float32)
     normed = (
@@ -150,7 +157,7 @@
         * norm_gain
     ).astype(jnp.bfloat16)
     top_count = route_experts.shape[1]
-    expert_count = lax.axis_size("gx") * lax.axis_size("gy") * expert_gate.shape[0]
+    expert_count = lax.axis_size("gx") * lax.axis_size("gyo") * lax.axis_size("core") * expert_gate.shape[0]
     capacity = max(2, (3 * tokens_here * top_count + 2 * expert_count - 1) // (2 * expert_count))
     slots = -(-capacity // 16) * 16
     flat_experts = route_experts.reshape(-1)
@@ -167,7 +174,7 @@
     )
     outgoing = jnp.dot(pick, normed, preferred_element_type=jnp.float32).astype(jnp.bfloat16)
     outgoing = outgoing.reshape(expert_count, slots, model_width)
-    arrived = lax.all_to_all(outgoing, ("gx", "gy"), split_axis=0, concat_axis=0, tiled=True)
+    arrived = lax.all_to_all(outgoing, TOKEN_AXES, split_axis=0, concat_axis=0, tiled=True)
     stacked = arrived.reshape(-1, model_width)
     gate_act = jnp.dot(stacked, expert_gate[0], preferred_element_type=jnp.float32)
     up_act = jnp.dot(stacked, expert_up[0], preferred_element_type=jnp.float32)
@@ -176,7 +183,7 @@
         jnp.bfloat16
     )
     returned = lax.all_to_all(
-        expert_out.reshape(arrived.shape), ("gx", "gy"), split_axis=0, concat_axis=0, tiled=True
+        expert_out.reshape(arrived.shape), TOKEN_AXES, split_axis=0, concat_axis=0, tiled=True
     )
     routed_sum = jnp.dot(
         weight_pick,
@@ -186,27 +193,34 @@
     )
     return (mixed_float + routed_sum).astype(jnp.bfloat16)
 
+TOKEN_AXES = ("gx", "gyo", "core")
+
+
 def solution(mesh):
+    rows = P(TOKEN_AXES, None)
+    split_mesh = jax.sharding.Mesh(
+        mesh.devices.reshape(mesh.shape["gx"], mesh.shape["gy"] // 2, 2), TOKEN_AXES
+    )
     in_specs = (
-        P(("gx", "gy"), None),
-        P(("gx", "gy"), None),
+        rows,
+        rows,
         P("gx", None),
-        P(("gx", "gy"), None),
-        P(("gx", "gy"), None),
-        P(("gx", "gy"), None),
-        P(),
-        P(),
-        P(),
-        P(),
-        P("gy", None),
-        P(),
-        P(("gx", "gy"), None),
-        P(("gx", "gy"), None),
-        P(("gx", "gy"), None, None),
-        P(("gx", "gy"), None, None),
-        P(("gx", "gy"), None, None),
-    )
-    out_specs = P(("gx", "gy"), None)
+        rows,
+        rows,
+        rows,
+        P(),
+        P(),
+        P(),
+        P(),
+        P(("gyo", "core"), None),
+        P(),
+        rows,
+        rows,
+        P(TOKEN_AXES, None, None),
+        P(TOKEN_AXES, None, None),
+        P(TOKEN_AXES, None, None),
+    )
+    out_specs = rows
     return jax.shard_map(
-        on_device, mesh=mesh, in_specs=in_specs, out_specs=out_specs, check_vma=False
-    )
+        on_device, mesh=split_mesh, in_specs=in_specs, out_specs=out_specs, check_vma=False
+    )

time: 513 us -> 519 us (1.012)
  other arithmetic: 26.3 us -> 37.4 us
  waiting for transfers between devices: 255 us -> 248 us
  matrix products: 52 us -> 46.3 us
    all_gather x1, waiting for transfers between devices: 66.9 us -> 47.9 us  [on_device(): parity_rows = lax.all_gather(out_weight, 'gyo', axis=0, tiled=False)]
    all_gather x1, waiting for transfers between devices: 77 us -> 88.3 us  [on_device(): cache_all = lax.all_gather(kv_cache, 'gx', axis=0, tiled=True)]
    unnamed x0 -> x7, other arithmetic: none -> 10.7 us
    dot_general x1, matrix products: 11.7 us -> 6.07 us  [on_device(): jnp.einsum('tnr,nrd->ntd', columns, parity_rows, preferred_element_type=j...]
  transfers between devices with their start and end apart: 3 -> 5, of which waited for: 3 -> 4; matrix products, arithmetic and copies ran while one was open for 4% -> 7% of each run, Pallas kernels for 8% -> 8%
where the time goes in v4:
time: 519 us; the launch traced here: 510 us
  waiting for transfers between devices  248 us (48%)
  blocking collectives  103 us (20%)
  matrix products  46.3 us (9%)
  Pallas kernels  39.4 us (8%)
  other arithmetic  37.4 us (7%)
  between operations  14 us (3%)
  starting transfers between devices  11.2 us (2%)
  local copies, waits for them, and re-layouts  10.9 us (2%)
    all_to_all x1, waiting for transfers between devices, on_device(): lax.all_to_all(expert_out.reshape(arrived.shape), TOKEN_AXES, split_axis=...  109 us
    all_to_all x1, blocking collectives, on_device(): lax.all_to_all(outgoing, TOKEN_AXES, split_axis=0, concat_axis=0, tiled=T...  103 us
    all_gather x1, waiting for transfers between devices, on_device(): cache_all = lax.all_gather(kv_cache, 'gx', axis=0, tiled=True)  88.3 us
    all_gather x1, waiting for transfers between devices, on_device(): parity_rows = lax.all_gather(out_weight, 'gyo', axis=0, tiled=False)  47.9 us
    pallas_call x1, Pallas kernels, tree_attention(): pl.pallas_call(attention_kernel, grid=(KV_HEADS,), in_specs=[pl.BlockSpec...  39.4 us
    dot_general x1, matrix products, on_device(): jnp.dot(hidden, expert_down[0], preferred_element_type=jnp.float32)  21.3 us
    unnamed x7, other arithmetic  10.7 us
  transfers between devices with their start and end apart: 5, of which 4 were waited for; matrix products, arithmetic and copies ran while one was open for 7% of the time, Pallas kernels for 8%

profile of v4, /device:TPU:1, one launch (start us, length us, event | category | flops | bytes accessed | tf_op | source)
XLA Modules:
  0.0 510.5 jit_solution(14673004185587160558)
XLA Ops:
  14.2 1.6 broadcast_select_fusion.bf_ref
  15.8 88.3 %all-gather.4.cloned.1.call-done.kc_ref.vc_ref = bf16[4096,1024]{1,0:T(8,128)(2,1)} async-done(((bf16[512,1024]{1,0:T(8,128)(2,1)}), bf16[4096,1024]{1,0:T(8,128)(2,1)}) %all-gather.4.cloned.1.call-update) | async-done | bytes 8388624 | tf_op jit(solution)/shard_map/all_gather | solution.py:127
  104.1 1.6 copy-done.1
  107.9 39.4 %shard_map.163 = bf16[128,4096]{1,0:T(8,128)(2,1)} custom-call(bf16[128,4096]{1,0:T(8,128)(2,1)S(1)} %copy-done.3, bf16[4096,1024]{1,0:T(8,128)(2,1)} %all-gather.4.cloned.1.call-done.kc_ref.vc_ref, bf16[4096,1024]{1,0:T(8,128)(2,1)} %all-gather.4.cloned.1.call-done.kc_ref.vc_ref, bf16[128,1024]{1,0:T(8,128)(2,1)S(1)} %copy-done.2, ...), custom_call_target="tpu_custom_call" | custom-call | tf_op jit(solution)/shard_map/pallas_call | solution.py:79
  150.9 1.5 bitcast_dynamic-update-slice_fusion.7
  153.9 1.5 bitcast_dynamic-update-slice_fusion.5
  155.5 1.5 bitcast_dynamic-update-slice_fusion.4
  158.5 1.5 bitcast_dynamic-update-slice_fusion.2
  160.1 1.5 bitcast_dynamic-update-slice_fusion.1
  161.6 1.5 bitcast_dynamic-update-slice_fusion
  163.1 47.9 %all-gather.6.cloned.1.call-done = bf16[2048,2048]{1,0:T(8,128)(2,1)} async-done(((bf16[256,2048]{1,0:T(8,128)(2,1)}), bf16[2048,2048]{1,0:T(8,128)(2,1)}) %all-gather.6.cloned.1.call-update) | async-done | bytes 8388624 | tf_op jit(solution)/shard_map/all_gather | solution.py:136
  211.0 6.1 %convolution_convert_fusion.2 = bf16[8,256,2048]{2,1,0:T(8,128)(2,1)S(1)} fusion(bf16[256,8,256]{2,0,1:T(8,128)(2,1)} %bitcast_dynamic-update-slice_fusion, bf16[8,256,2048]{2,1,0:T(8,128)(2,1)} %bitcast.56), kind=kOutput, calls=%fused_computation.9 | convolution fusion | flops 2151677952 | bytes 17825792 | tf_op jit(solution)/shard_map/tnr,nrd->ntd/dot_general | solution.py:146
  217.1 1.8 convert_reduce_fusion
  225.1 7.4 %fusion = pred[2048,128]{1,0:T(8,128)(4,1)S(1)} fusion(s32[128,8]{0,1:T(8,128)S(1)} %multiply_add_fusion), kind=kLoop, calls=%fused_computation.4 | loop fusion | flops 3932160 | bytes 266240 | tf_op jit(solution)/shard_map/reduce_or | solution.py:170
  232.6 1.8 fusion.12
  234.6 2.4 convolution_convert_fusion.1
  237.1 103.0 %all_to_all.10 = bf16[128,16,2048]{2,1,0:T(8,128)(2,1)S(1)} all-to-all(bf16[128,16,2048]{2,1,0:T(8,128)(2,1)S(1)} %bitcast.55), channel_id=1, replica_groups=mesh['gx'=8,'gyo'=8,'core'=2] {'gx','gyo','core'}, dimensions={0} | all-to-all | bytes 16777216 | tf_op jit(solution)/shard_map/all_to_all | solution.py:177
  340.1 3.2 copy-done.6
  343.3 8.6 %fusion.4 = f32[2048,768]{1,0:T(8,128)} fusion(bf16[2048,2048]{1,0:T(8,128)(2,1)S(1)} %bitcast.58, bf16[1,2048,768]{2,1,0:T(8,128)(2,1)S(1)} %copy-done.10), kind=kOutput, calls=%fused_computation.28 | convolution fusion | flops 6442450944 | bytes 17825792 | tf_op jit(solution)/shard_map/dot_general | solution.py:179
  351.9 21.3 %convolution_convert_fusion = bf16[2048,2048]{1,0:T(8,128)(2,1)} fusion(f32[2048,768]{1,0:T(8,128)} %fusion.4, bf16[2048,2048]{1,0:T(8,128)(2,1)} %bitcast.59, bf16[1,768,2048]{2,1,0:T(8,128)(2,1)S(1)} %copy-done, bf16[1,2048,768]{2,1,0:T(8,128)(2,1)} %param.32), kind=kOutput, calls=%fused_computation.5 | convolution fusion | flops 12898533376 | bytes 29360128 | tf_op jit(solution)/shard_map/dot_general | solution.py:182
  373.2 8.8 %all-to-all-start.1 = ((bf16[128,16,2048]{2,1,0:T(8,128)(2,1)}), bf16[128,16,2048]{2,1,0:T(8,128)(2,1)}, u32[]{:S(2)}, u32[]{:S(2)}) async-start(bf16[128,16,2048]{2,1,0:T(8,128)(2,1)} %bitcast.57), calls=%async_computation.1 | async-start | bytes 16777216 | tf_op jit(solution)/shard_map/all_to_all | solution.py:185
  382.2 3.7 select_reduce_fusion
  385.9 109.3 %all-to-all-done.1 = bf16[128,16,2048]{2,1,0:T(8,128)(2,1)} async-done(((bf16[128,16,2048]{2,1,0:T(8,128)(2,1)}), bf16[128,16,2048]{2,1,0:T(8,128)(2,1)}, u32[]{:S(2)}, u32[]{:S(2)}) %all-to-all-start.1) | async-done | bytes 8388640 | tf_op jit(solution)/shard_map/all_to_all | solution.py:185
  495.2 8.0 %fusion.7 = bf16[128,2048]{1,0:T(8,128)(2,1)} fusion(f32[128,2048]{1,0:T(8,128)} %select_reduce_fusion, bf16[2048,2048]{1,0:T(8,128)(2,1)} %bitcast.23, bf16[128,2048]{1,0:T(8,128)(2,1)} %copy-done.5), kind=kOutput, calls=%fused_computation.32 | convolution fusion | flops 6443237376 | bytes 10485760 | tf_op jit(solution)/shard_map/dot_general | solution.py:188
  (59 shorter events, 23.0 us)
Async XLA Ops:
  6.5 345.4 %copy-start = (bf16[1,768,2048]{2,1,0:T(8,128)(2,1)S(1)}, bf16[1,768,2048]{2,1,0:T(8,128)(2,1)}, u32[]{:S(2)}) copy-start(bf16[1,768,2048]{2,1,0:T(8,128)(2,1)} %param.33) | copy-start | bytes 9437188
  6.5 97.6 %all-gather.4.cloned.1.call-start = ((), (), s32[]{:S(2)}) async-start(), calls=%async_computation.2 | async-start | bytes 9437184 | tf_op jit(solution)/shard_map/all_gather | solution.py:127
  7.3 203.8 %all-gather.6.cloned.1.call-start = ((), (), s32[]{:S(2)}) async-start(), calls=%async_computation.3 | async-start | bytes 9437184 | tf_op jit(solution)/shard_map/all_gather | solution.py:136
  104.1 1.6 copy-start.1
  105.7 0.9 copy-start.2
  106.6 1.2 copy-start.3
  107.9 40.4 %copy-start.7 = (s32[128,8]{0,1:T(8,128)S(1)}, s32[128,8]{0,1:T(8,128)}, u32[]{:S(2)}) copy-start(s32[128,8]{0,1:T(8,128)} %param.29) | copy-start | bytes 12292
  147.3 3.6 collective-permute-start
  218.9 1.4 copy-start.4
  220.3 14.4 %copy-start.8 = (f32[2048]{0:T(1024)S(1)}, f32[2048]{0:T(1024)}, u32[]{:S(2)}) copy-start(f32[2048]{0:T(1024)} %param.28) | copy-start | bytes 24580
  221.3 11.3 %collective-permute-start.1 = (f32[128,2048]{1,0:T(8,128)}, f32[128,2048]{1,0:T(8,128)}, u32[]{:S(2)}, u32[]{:S(2)}) collective-permute-start(f32[128,2048]{1,0:T(8,128)} %slice.17), channel_id=1, source_target_pairs={{0,1},{1,0},{2,3},{3,2},{4,5},{5,4},{6,7},{7,6},{8,9},{9,8},{10,11... | collective-permute-start | bytes 3145736 | tf_op jit(solution)/shard_map/ppermute | solution.py:151
  234.4 2.6 copy-start.5
  237.1 106.3 %copy-start.10 = (bf16[1,2048,768]{2,1,0:T(8,128)(2,1)S(1)}, bf16[1,2048,768]{2,1,0:T(8,128)(2,1)}, u32[]{:S(2)}) copy-start(bf16[1,2048,768]{2,1,0:T(8,128)(2,1)} %param.31) | copy-start | bytes 9437188
  340.1 3.2 copy-start.6
  373.2 8.9 %copy-start.9 = (f32[128,8]{0,1:T(8,128)S(1)}, f32[128,8]{0,1:T(8,128)}, u32[]{:S(2)}) copy-start(f32[128,8]{0,1:T(8,128)} %param.30) | copy-start | bytes 12292
  373.2 122.0 %all-to-all-start.1 = ((bf16[128,16,2048]{2,1,0:T(8,128)(2,1)}), bf16[128,16,2048]{2,1,0:T(8,128)(2,1)}, u32[]{:S(2)}, u32[]{:S(2)}) async-start(bf16[128,16,2048]{2,1,0:T(8,128)(2,1)} %bitcast.57), calls=%async_computation.1 | async-start | bytes 16777216 | tf_op jit(solution)/shard_map/all_to_all | solution.py:185
Sparse Core Ops, SparseCore 0:
  9.0 95.0 all-gather.3
  106.5 104.5 all-gather.5

commit v5 on v3

--- a/solution.py
+++ b/solution.py
@@ -92,6 +92,30 @@
         out_shape=jax.ShapeDtypeStruct((tokens, HEADS * HEAD_DIM), jnp.bfloat16),
         compiler_params=pltpu.CompilerParams(vmem_limit_bytes=48 * 1024 * 1024),
     )(queries, cache, cache, new_kv, new_kv, far_bias, near_bias)
+
+
+def projection_kernel(a_ref, w_ref, o_ref):
+    @pl.when(pl.program_id(0) == 0)
+    def _():
+        o_ref[...] = jnp.zeros_like(o_ref)
+
+    part = jnp.dot(a_ref[...], w_ref[...], preferred_element_type=jnp.float32)
+    o_ref[...] += part.astype(jnp.bfloat16).astype(jnp.float32)
+
+
+def projection(attended, weight, group_rows):
+    tokens = attended.shape[0]
+    width = weight.shape[1]
+    return pl.pallas_call(
+        projection_kernel,
+        grid=(weight.shape[0] // group_rows,),
+        in_specs=[
+            pl.BlockSpec((tokens, group_rows), lambda j: (0, j)),
+            pl.BlockSpec((group_rows, width), lambda j: (j, 0)),
+        ],
+        out_specs=pl.BlockSpec((tokens, width), lambda j: (0, 0)),
+        out_shape=jax.ShapeDtypeStruct((tokens, width), jnp.float32),
+    )(attended, weight)
 
 
 def on_device(
@@ -132,16 +156,7 @@
     attended = tree_attention(queries, cache_all, new_kv, far_bias, near_bias)
     shard_rows = out_weight.shape[0]
     shard_piece = lax.all_gather(out_weight, "gy", axis=0, tiled=True)
-    block_count = shard_piece.shape[0] // shard_rows
-    columns = attended.reshape(tokens_here, block_count, shard_rows)
-    partial_value = jnp.einsum(
-        "tnr,nrd->ntd",
-        columns,
-        shard_piece.reshape(block_count, shard_rows, model_width),
-        preferred_element_type=jnp.float32,
-    )
-    partial_value = lax.optimization_barrier(partial_value.astype(jnp.bfloat16))
-    projected = jnp.sum(partial_value.astype(jnp.float32), axis=0)
+    projected = projection(attended, shard_piece, shard_rows)
     mixed_state = (residual.astype(jnp.float32) + projected).astype(jnp.bfloat16)
     mixed_float = lax.optimization_barrier(mixed_state).astype(jnp.float32)
     normed = (
@@ -181,7 +196,7 @@
     routed_sum = jnp.dot(
         weight_pick,
         returned.reshape(-1, model_width).astype(jnp.float32),
-        precision=lax.Precision.HIGHEST,
+        precision=lax.Precision.HIGH,
         preferred_element_type=jnp.float32,
     )
     return (mixed_float + routed_sum).astype(jnp.bfloat16)

time: 513 us -> 505 us (0.984)
  Pallas kernels: 39.5 us -> 53.4 us
  matrix products: 52 us -> 39.3 us
    pallas_call x0 -> x1, Pallas kernels: none -> 14.6 us  [projection(): pl.pallas_call(projection_kernel, grid=(weight.shape[0] // group_rows,),...]
    dot_general x1 -> x0, matrix products: 11.7 us -> none  [on_device(): jnp.einsum('tnr,nrd->ntd', columns, shard_piece.reshape(block_count, shar...]
    reduce_sum x1 -> x0, other arithmetic: 5.41 us -> none  [on_device(): projected = jnp.sum(partial_value.astype(jnp.float32), axis=0)]
where the time goes in v5:
time: 505 us; the launch traced here: 504 us
  waiting for transfers between devices  255 us (50%)
  blocking collectives  103 us (20%)
  Pallas kernels  53.4 us (11%)
  matrix products  39.3 us (8%)
  other arithmetic  22.3 us (4%)
  between operations  13.6 us (3%)
  local copies, waits for them, and re-layouts  9.36 us (2%)
  starting transfers between devices  8.41 us (2%)
    all_to_all x1, waiting for transfers between devices, on_device(): lax.all_to_all(expert_out.reshape(arrived.shape), ('gx', 'gy'), split_axi...  109 us
    all_to_all x1, blocking collectives, on_device(): lax.all_to_all(outgoing, ('gx', 'gy'), split_axis=0, concat_axis=0, tiled...  103 us
    all_gather x1, waiting for transfers between devices, on_device(): cache_all = lax.all_gather(kv_cache, 'gx', axis=0, tiled=True)  77 us
    all_gather x1, waiting for transfers between devices, on_device(): shard_piece = lax.all_gather(out_weight, 'gy', axis=0, tiled=True)  67.7 us
    pallas_call x1, Pallas kernels, tree_attention(): pl.pallas_call(attention_kernel, grid=(KV_HEADS,), in_specs=[pl.BlockSpec...  38.8 us
    dot_general x1, matrix products, on_device(): jnp.dot(hidden, expert_down[0], preferred_element_type=jnp.float32)  21.3 us
    pallas_call x1, Pallas kernels, projection(): pl.pallas_call(projection_kernel, grid=(weight.shape[0] // group_rows,),...  14.6 us
  transfers between devices with their start and end apart: 3, of which 3 were waited for; matrix products, arithmetic and copies ran while one was open for 4% of the time, Pallas kernels for 8%

profile of v5, /device:TPU:1, one launch (start us, length us, event | category | flops | bytes accessed | tf_op | source)
XLA Modules:
  0.0 504.1 jit_solution(10554116858509482219)
XLA Ops:
  8.0 0.8 copy.38
  9.3 0.8 copy-done.8
  10.1 1.1 broadcast_add_fusion
  14.1 0.9 select_reduce_fusion.2
  15.9 1.3 compare_reduce_fusion
  17.2 8.1 %fusion = pred[2048,128]{1,0:T(8,128)(4,1)} fusion(s32[128,8]{0,1:T(8,128)S(1)} %multiply_add_fusion), kind=kLoop, calls=%fused_computation.3 | loop fusion | flops 3932160 | bytes 266240 | tf_op jit(solution)/shard_map/reduce_or | solution.py:178
  25.4 1.7 broadcast_select_fusion.bf_ref
  27.1 77.0 %all-gather.3.cloned.1.call-done.kc_ref.vc_ref = bf16[4096,1024]{1,0:T(8,128)(2,1)} async-done(((bf16[512,1024]{1,0:T(8,128)(2,1)}), bf16[4096,1024]{1,0:T(8,128)(2,1)}) %all-gather.3.cloned.1.call-update) | async-done | bytes 8388624 | tf_op jit(solution)/shard_map/all_gather | solution.py:151
  104.1 1.6 copy-done.2
  105.7 1.2 copy-done.5
  106.9 38.8 %shard_map.163.a_ref = bf16[128,4096]{1,0:T(8,128)(2,1)S(1)} custom-call(bf16[128,4096]{1,0:T(8,128)(2,1)S(1)} %copy-done.5, bf16[4096,1024]{1,0:T(8,128)(2,1)} %all-gather.3.cloned.1.call-done.kc_ref.vc_ref, bf16[4096,1024]{1,0:T(8,128)(2,1)} %all-gather.3.cloned.1.call-done.kc_ref.vc_ref, bf16[128,1024]{1,0:T(8,128)(2,1)S(1)} %copy-done.4, ...), custom_call_target="tpu_custom_call" | custom-call | tf_op jit(solution)/shard_map/pallas_call | solution.py:79
  145.7 1.0 copy-done.3
  146.7 67.7 %all-gather.5.cloned.1.call-done.w_ref = bf16[4096,2048]{1,0:T(8,128)(2,1)} async-done(((bf16[256,2048]{1,0:T(8,128)(2,1)}), bf16[4096,2048]{1,0:T(8,128)(2,1)}) %all-gather.5.cloned.1.call-update) | async-done | bytes 16777232 | tf_op jit(solution)/shard_map/all_gather | solution.py:158
  214.4 14.6 %shard_map.164 = f32[128,2048]{1,0:T(8,128)} custom-call(bf16[128,4096]{1,0:T(8,128)(2,1)} %copy-done.3, bf16[4096,2048]{1,0:T(8,128)(2,1)} %all-gather.5.cloned.1.call-done.w_ref), custom_call_target="tpu_custom_call" | custom-call | tf_op jit(solution)/shard_map/pallas_call | solution.py:109
  229.0 1.5 add_convert_fusion
  230.7 2.4 convolution_convert_fusion.1
  233.2 102.8 %all_to_all.10 = bf16[128,16,2048]{2,1,0:T(8,128)(2,1)S(1)} all-to-all(bf16[128,16,2048]{2,1,0:T(8,128)(2,1)S(1)} %bitcast.36), channel_id=1, replica_groups=mesh['gx'=8,'gy'=16] {'gx','gy'}, dimensions={0} | all-to-all | bytes 16777216 | tf_op jit(solution)/shard_map/all_to_all | solution.py:185
  336.0 3.2 copy-done.7
  339.2 8.6 %fusion.4 = f32[2048,768]{1,0:T(8,128)} fusion(bf16[2048,2048]{1,0:T(8,128)(2,1)S(1)} %bitcast.38, bf16[1,2048,768]{2,1,0:T(8,128)(2,1)S(1)} %copy-done.14), kind=kOutput, calls=%fused_computation.10 | convolution fusion | flops 6442450944 | bytes 17825792 | tf_op jit(solution)/shard_map/dot_general | solution.py:187
  347.7 21.3 %convolution_convert_fusion = bf16[2048,2048]{1,0:T(8,128)(2,1)} fusion(f32[2048,768]{1,0:T(8,128)} %fusion.4, bf16[2048,2048]{1,0:T(8,128)(2,1)} %bitcast.39, bf16[1,768,2048]{2,1,0:T(8,128)(2,1)S(1)} %copy-done, bf16[1,2048,768]{2,1,0:T(8,128)(2,1)} %param.32), kind=kOutput, calls=%fused_computation.4 | convolution fusion | flops 12898533376 | bytes 29360128 | tf_op jit(solution)/shard_map/dot_general | solution.py:190
  369.0 8.3 %all-to-all-start.1 = ((bf16[128,16,2048]{2,1,0:T(8,128)(2,1)}), bf16[128,16,2048]{2,1,0:T(8,128)(2,1)}, u32[]{:S(2)}, u32[]{:S(2)}) async-start(bf16[128,16,2048]{2,1,0:T(8,128)(2,1)} %bitcast.37), calls=%async_computation.1 | async-start | bytes 16777216 | tf_op jit(solution)/shard_map/all_to_all | solution.py:193
  377.6 3.7 select_reduce_fusion
  381.3 108.9 %all-to-all-done.1 = bf16[128,16,2048]{2,1,0:T(8,128)(2,1)} async-done(((bf16[128,16,2048]{2,1,0:T(8,128)(2,1)}), bf16[128,16,2048]{2,1,0:T(8,128)(2,1)}, u32[]{:S(2)}, u32[]{:S(2)}) %all-to-all-start.1) | async-done | bytes 8388640 | tf_op jit(solution)/shard_map/all_to_all | solution.py:193
  490.2 7.1 %fusion.7 = bf16[128,2048]{1,0:T(8,128)(2,1)} fusion(f32[128,2048]{1,0:T(8,128)} %select_reduce_fusion, bf16[2048,2048]{1,0:T(8,128)(2,1)} %bitcast.14, bf16[128,2048]{1,0:T(8,128)(2,1)} %copy-done.6), kind=kOutput, calls=%fused_computation.14 | convolution fusion | flops 3222011904 | bytes 10485760 | tf_op jit(solution)/shard_map/dot_general | solution.py:196
  (53 shorter events, 6.2 us)
Async XLA Ops:
  6.5 341.2 %copy-start = (bf16[1,768,2048]{2,1,0:T(8,128)(2,1)S(1)}, bf16[1,768,2048]{2,1,0:T(8,128)(2,1)}, u32[]{:S(2)}) copy-start(bf16[1,768,2048]{2,1,0:T(8,128)(2,1)} %param.33) | copy-start | bytes 9437188
  6.5 10.6 %copy-start.10 = (s32[128,8]{0,1:T(8,128)S(1)}, s32[128,8]{0,1:T(8,128)}, u32[]{:S(2)}) copy-start(s32[128,8]{0,1:T(8,128)} %param.29) | copy-start | bytes 12292
  6.5 18.8 %copy-start.13 = (s32[1,128]{1,0:T(1,128)S(1)}, s32[1,128]{1,0:T(1,128)}, u32[]{:S(2)}) copy-start(s32[1,128]{1,0:T(1,128)} %param.21) | copy-start | bytes 1540
  6.5 97.6 %copy-start.4 = (bf16[128,1024]{1,0:T(8,128)(2,1)S(1)}, bf16[128,1024]{1,0:T(8,128)(2,1)}, u32[]{:S(2)}) copy-start(bf16[128,1024]{1,0:T(8,128)(2,1)} %vn_ref.1) | copy-start | bytes 786436
  6.5 97.6 %all-gather.3.cloned.1.call-start = ((), (), s32[]{:S(2)}) async-start(), calls=%async_computation.2 | async-start | bytes 9437184 | tf_op jit(solution)/shard_map/all_gather | solution.py:151
  7.3 207.1 %all-gather.5.cloned.1.call-start = ((), (), s32[]{:S(2)}) async-start(), calls=%async_computation.3 | async-start | bytes 17825792 | tf_op jit(solution)/shard_map/all_gather | solution.py:158
  9.3 0.8 copy-start.8
  104.1 1.6 copy-start.2
  105.7 1.2 copy-start.5
  145.7 1.0 copy-start.3
  146.7 84.0 %copy-start.9 = (pred[2048,128]{1,0:T(8,128)(4,1)S(1)}, pred[2048,128]{1,0:T(8,128)(4,1)}, u32[]{:S(2)}) copy-start(pred[2048,128]{1,0:T(8,128)(4,1)} %fusion) | copy-start | bytes 786436
  146.7 84.0 %copy-start.11 = (f32[2048]{0:T(1024)S(1)}, f32[2048]{0:T(1024)}, u32[]{:S(2)}) copy-start(f32[2048]{0:T(1024)} %param.28) | copy-start | bytes 24580
  230.5 2.6 copy-start.6
  233.2 106.0 %copy-start.14 = (bf16[1,2048,768]{2,1,0:T(8,128)(2,1)S(1)}, bf16[1,2048,768]{2,1,0:T(8,128)(2,1)}, u32[]{:S(2)}) copy-start(bf16[1,2048,768]{2,1,0:T(8,128)(2,1)} %param.31) | copy-start | bytes 9437188
  336.0 3.2 copy-start.7
  369.0 8.5 %copy-start.12 = (f32[128,8]{0,1:T(8,128)S(1)}, f32[128,8]{0,1:T(8,128)}, u32[]{:S(2)}) copy-start(f32[128,8]{0,1:T(8,128)} %param.30) | copy-start | bytes 12292
  369.0 121.2 %all-to-all-start.1 = ((bf16[128,16,2048]{2,1,0:T(8,128)(2,1)}), bf16[128,16,2048]{2,1,0:T(8,128)(2,1)}, u32[]{:S(2)}, u32[]{:S(2)}) async-start(bf16[128,16,2048]{2,1,0:T(8,128)(2,1)} %bitcast.37), calls=%async_computation.1 | async-start | bytes 16777216 | tf_op jit(solution)/shard_map/all_to_all | solution.py:193
  490.2 7.1 %copy-start.1 = (bf16[1,768,2048]{2,1,0:T(8,128)(2,1)S(1)}, bf16[1,768,2048]{2,1,0:T(8,128)(2,1)}, u32[]{:S(2)}) copy-start(bf16[1,768,2048]{2,1,0:T(8,128)(2,1)} %param.33) | copy-start | bytes 9437188
Sparse Core Ops, SparseCore 0:
  9.0 95.0 all-gather.2
  106.6 107.7 all-gather.4

commit v6 on v5

--- a/solution.py
+++ b/solution.py
@@ -76,22 +76,35 @@
     tokens = queries.shape[0]
     rows = cache.shape[0]
     group_cols = (HEADS // KV_HEADS) * HEAD_DIM
+    local_heads = cache.shape[1] // (2 * HEAD_DIM)
     return pl.pallas_call(
         attention_kernel,
-        grid=(KV_HEADS,),
+        grid=(local_heads,),
         in_specs=[
             pl.BlockSpec((tokens, group_cols), lambda g: (0, g)),
             pl.BlockSpec((rows, HEAD_DIM), lambda g: (0, g)),
-            pl.BlockSpec((rows, HEAD_DIM), lambda g: (0, KV_HEADS + g)),
+            pl.BlockSpec((rows, HEAD_DIM), lambda g: (0, local_heads + g)),
             pl.BlockSpec((tokens, HEAD_DIM), lambda g: (0, g)),
-            pl.BlockSpec((tokens, HEAD_DIM), lambda g: (0, KV_HEADS + g)),
+            pl.BlockSpec((tokens, HEAD_DIM), lambda g: (0, local_heads + g)),
             pl.BlockSpec((tokens, rows), lambda g: (0, 0)),
             pl.BlockSpec((tokens, tokens), lambda g: (0, 0)),
         ],
         out_specs=pl.BlockSpec((tokens, group_cols), lambda g: (0, g)),
-        out_shape=jax.ShapeDtypeStruct((tokens, HEADS * HEAD_DIM), jnp.bfloat16),
+        out_shape=jax.ShapeDtypeStruct((tokens, local_heads * group_cols), jnp.bfloat16),
         compiler_params=pltpu.CompilerParams(vmem_limit_bytes=48 * 1024 * 1024),
     )(queries, cache, cache, new_kv, new_kv, far_bias, near_bias)
+
+
+def head_half(x, half, width):
+    return lax.dynamic_slice_in_dim(x, half * width, width, axis=1)
+
+
+def kv_half(x, half):
+    kv_width = KV_HEADS * HEAD_DIM
+    width = kv_width // 2
+    return jnp.concatenate(
+        [head_half(x[:, :kv_width], half, width), head_half(x[:, kv_width:], half, width)], axis=1
+    )
 
 
 def projection_kernel(a_ref, w_ref, o_ref):
@@ -148,14 +161,29 @@
     starts, finish = node_bounds(node_owner, node_len, span_rows)
     positions = jnp.arange(tokens_here, dtype=jnp.int32)
     own_mask = (requests[:, None] == requests[None, :]) & (positions[None, :] <= positions[:, None])
-    cache_all = lax.all_gather(kv_cache, "gx", axis=0, tiled=True)
-    labels = key_labels(0, cache_all.shape[0], starts, finish)
+    core = lax.axis_index("core")
+    other_core = 1 - core
+    swap = [(0, 1), (1, 0)]
+    cache_mine = lax.all_gather(kv_half(kv_cache, core), "gx", axis=0, tiled=True)
+    cache_other = lax.ppermute(cache_mine, "core", swap)
+    labels = key_labels(0, cache_mine.shape[0], starts, finish)
     seen_mask = jnp.any(labels[None, :, None] == ancestry[:, None, :], axis=2)
     far_bias = jnp.where(seen_mask, 0.0, -jnp.inf).astype(jnp.float32)
     near_bias = jnp.where(own_mask, 0.0, -jnp.inf).astype(jnp.float32)
-    attended = tree_attention(queries, cache_all, new_kv, far_bias, near_bias)
+    query_cols = queries.shape[1] // 2
+    attended_mine = tree_attention(
+        head_half(queries, core, query_cols), cache_mine, kv_half(new_kv, core), far_bias, near_bias
+    )
+    attended_other = tree_attention(
+        head_half(queries, other_core, query_cols), cache_other, kv_half(new_kv, other_core), far_bias, near_bias
+    )
+    attended = jnp.where(
+        core == 0,
+        jnp.concatenate([attended_mine, attended_other], axis=1),
+        jnp.concatenate([attended_other, attended_mine], axis=1),
+    )
     shard_rows = out_weight.shape[0]
-    shard_piece = lax.all_gather(out_weight, "gy", axis=0, tiled=True)
+    shard_piece = lax.all_gather(out_weight, ("gyo", "core"), axis=0, tiled=True)
     projected = projection(attended, shard_piece, shard_rows)
     mixed_state = (residual.astype(jnp.float32) + projected).astype(jnp.bfloat16)
     mixed_float = lax.optimization_barrier(mixed_state).astype(jnp.float32)
@@ -165,7 +193,7 @@
         * norm_gain
     ).astype(jnp.bfloat16)
     top_count = route_experts.shape[1]
-    expert_count = lax.axis_size("gx") * lax.axis_size("gy") * expert_gate.shape[0]
+    expert_count = lax.axis_size("gx") * lax.axis_size("gyo") * lax.axis_size("core") * expert_gate.shape[0]
     capacity = max(2, (3 * tokens_here * top_count + 2 * expert_count - 1) // (2 * expert_count))
     slots = -(-capacity // 16) * 16
     flat_experts = route_experts.reshape(-1)
@@ -182,7 +210,7 @@
     )
     outgoing = jnp.dot(pick, normed, preferred_element_type=jnp.float32).astype(jnp.bfloat16)
     outgoing = outgoing.reshape(expert_count, slots, model_width)
-    arrived = lax.all_to_all(outgoing, ("gx", "gy"), split_axis=0, concat_axis=0, tiled=True)
+    arrived = lax.all_to_all(outgoing, TOKEN_AXES, split_axis=0, concat_axis=0, tiled=True)
     stacked = arrived.reshape(-1, model_width)
     gate_act = jnp.dot(stacked, expert_gate[0], preferred_element_type=jnp.float32)
     up_act = jnp.dot(stacked, expert_up[0], preferred_element_type=jnp.float32)
@@ -191,7 +219,7 @@
         jnp.bfloat16
     )
     returned = lax.all_to_all(
-        expert_out.reshape(arrived.shape), ("gx", "gy"), split_axis=0, concat_axis=0, tiled=True
+        expert_out.reshape(arrived.shape), TOKEN_AXES, split_axis=0, concat_axis=0, tiled=True
     )
     routed_sum = jnp.dot(
         weight_pick,
@@ -201,27 +229,34 @@
     )
     return (mixed_float + routed_sum).astype(jnp.bfloat16)
 
+TOKEN_AXES = ("gx", "gyo", "core")
+
+
 def solution(mesh):
+    rows = P(TOKEN_AXES, None)
+    split_mesh = jax.sharding.Mesh(
+        mesh.devices.reshape(mesh.shape["gx"], mesh.shape["gy"] // 2, 2), TOKEN_AXES
+    )
     in_specs = (
-        P(("gx", "gy"), None),
-        P(("gx", "gy"), None),
+        rows,
+        rows,
         P("gx", None),
-        P(("gx", "gy"), None),
-        P(("gx", "gy"), None),
-        P(("gx", "gy"), None),
-        P(),
-        P(),
-        P(),
-        P(),
-        P("gy", None),
-        P(),
-        P(("gx", "gy"), None),
-        P(("gx", "gy"), None),
-        P(("gx", "gy"), None, None),
-        P(("gx", "gy"), None, None),
-        P(("gx", "gy"), None, None),
-    )
-    out_specs = P(("gx", "gy"), None)
+        rows,
+        rows,
+        rows,
+        P(),
+        P(),
+        P(),
+        P(),
+        P(("gyo", "core"), None),
+        P(),
+        rows,
+        rows,
+        P(TOKEN_AXES, None, None),
+        P(TOKEN_AXES, None, None),
+        P(TOKEN_AXES, None, None),
+    )
+    out_specs = rows
     return jax.shard_map(
-        on_device, mesh=mesh, in_specs=in_specs, out_specs=out_specs, check_vma=False
-    )
+        on_device, mesh=split_mesh, in_specs=in_specs, out_specs=out_specs, check_vma=False
+    )

time: 505 us -> 475 us (0.941); the launches traced: 504 us -> 468 us
  waiting for transfers between devices: 255 us -> 214 us
    all_gather x2, waiting for transfers between devices: 145 us -> 104 us  [the longest x1 53.2 us: on_device(): lax.all_gather(kv_half(kv_cache, core), 'gx', axis=0, tiled=True)]
    pallas_call x1 -> x2, Pallas kernels: 38.8 us -> 40.7 us  [tree_attention(): pl.pallas_call(attention_kernel, grid=(local_heads,), in_specs=[pl.BlockS...]
  transfers between devices with their start and end apart: 3 -> 4, of which waited for: 3 -> 3; matrix products, arithmetic and copies ran while one was open for 4% -> 5% of each run, Pallas kernels for 8% -> 9%
where the time goes in v6:
time: 475 us; the launch traced here: 468 us
  waiting for transfers between devices  214 us (45%)
  blocking collectives  103 us (22%)
  Pallas kernels  55.6 us (12%)
  matrix products  39.3 us (8%)
  other arithmetic  22.9 us (5%)
  between operations  14.1 us (3%)
  local copies, waits for them, and re-layouts  10.3 us (2%)
  starting transfers between devices  9.72 us (2%)
    all_to_all x1, waiting for transfers between devices, on_device(): lax.all_to_all(expert_out.reshape(arrived.shape), TOKEN_AXES, split_axis=...  109 us
    all_to_all x1, blocking collectives, on_device(): lax.all_to_all(outgoing, TOKEN_AXES, split_axis=0, concat_axis=0, tiled=T...  103 us
    all_gather x1, waiting for transfers between devices, on_device(): lax.all_gather(kv_half(kv_cache, core), 'gx', axis=0, tiled=True)  53.2 us
    all_gather x1, waiting for transfers between devices, on_device(): lax.all_gather(out_weight, ('gyo', 'core'), axis=0, tiled=True)  50.5 us
    pallas_call x2, Pallas kernels, tree_attention(): pl.pallas_call(attention_kernel, grid=(local_heads,), in_specs=[pl.BlockS...  40.7 us
    dot_general x1, matrix products, on_device(): jnp.dot(hidden, expert_down[0], preferred_element_type=jnp.float32)  21.3 us
    pallas_call x1, Pallas kernels, projection(): pl.pallas_call(projection_kernel, grid=(weight.shape[0] // group_rows,),...  14.9 us
  transfers between devices with their start and end apart: 4, of which 3 were waited for; matrix products, arithmetic and copies ran while one was open for 5% of the time, Pallas kernels for 9%

profile of v6, /device:TPU:1, one launch (start us, length us, event | category | flops | bytes accessed | tf_op | source)
XLA Modules:
  0.0 468.4 jit_solution(13837944579061282015)
XLA Ops:
  6.6 2.4 fusion.25
  9.0 1.1 constant_dynamic-slice_fusion.5
  12.6 1.0 fusion.16
  13.6 53.2 %all-gather.3.cloned.1.call-done.kc_ref.vc_ref = bf16[4096,512]{1,0:T(8,128)(2,1)} async-done(((bf16[512,512]{1,0:T(8,128)(2,1)}), bf16[4096,512]{1,0:T(8,128)(2,1)}) %all-gather.3.cloned.1.call-update) | async-done | bytes 4194320 | tf_op jit(solution)/shard_map/all_gather | solution.py:167
  66.8 0.8 collective-permute-start
  68.5 1.1 broadcast_add_fusion
  74.2 1.3 compare_reduce_fusion
  75.6 7.4 %fusion = pred[2048,128]{1,0:T(8,128)(4,1)S(1)} fusion(s32[128,8]{0,1:T(8,128)S(1)} %multiply_add_fusion), kind=kLoop, calls=%fused_computation.3 | loop fusion | flops 3932160 | bytes 266240 | tf_op jit(solution)/shard_map/reduce_or | solution.py:206
  83.1 1.3 constant_dynamic-slice_fusion.7
  84.6 20.3 %shard_map.163 = bf16[128,2048]{1,0:T(8,128)(2,1)S(1)} custom-call(bf16[128,2048]{1,0:T(8,128)(2,1)S(1)} %get-tuple-element.7.q_ref, bf16[4096,512]{1,0:T(8,128)(2,1)} %all-gather.3.cloned.1.call-done.kc_ref.vc_ref, bf16[4096,512]{1,0:T(8,128)(2,1)} %all-gather.3.cloned.1.call-done.kc_ref.vc_ref, bf16[128,512]{1,0:T(8,128)(2,1)S(1)} %pad_maximum_fusion.1.kn_ref.vn_ref, ...), custom_call_target="tpu_custom_call" | custom-call | tf_op jit(solution)/shard_map/pallas_call | solution.py:80
  105.0 20.4 %shard_map.164 = bf16[128,2048]{1,0:T(8,128)(2,1)S(1)} custom-call(bf16[128,2048]{1,0:T(8,128)(2,1)S(1)} %get-tuple-element.8.q_ref, bf16[4096,512]{1,0:T(8,128)(2,1)} %collective-permute-done.kc_ref.vc_ref, bf16[4096,512]{1,0:T(8,128)(2,1)} %collective-permute-done.kc_ref.vc_ref, bf16[128,512]{1,0:T(8,128)(2,1)S(1)} %pad_maximum_fusion.2.kn_ref.vn_ref, ...), custom_call_target="tpu_custom_call" | custom-call | tf_op jit(solution)/shard_map/pallas_call | solution.py:80
  125.4 1.2 maximum_select_fusion.a_ref
  126.6 50.5 %all-gather.5.cloned.1.call-done.w_ref = bf16[4096,2048]{1,0:T(8,128)(2,1)} async-done(((bf16[256,2048]{1,0:T(8,128)(2,1)}), bf16[4096,2048]{1,0:T(8,128)(2,1)}) %all-gather.5.cloned.1.call-update) | async-done | bytes 16777232 | tf_op jit(solution)/shard_map/all_gather | solution.py:186
  177.1 14.9 %shard_map.165 = f32[128,2048]{1,0:T(8,128)} custom-call(bf16[128,4096]{1,0:T(8,128)(2,1)} %maximum_select_fusion.a_ref, bf16[4096,2048]{1,0:T(8,128)(2,1)} %all-gather.5.cloned.1.call-done.w_ref), custom_call_target="tpu_custom_call" | custom-call | tf_op jit(solution)/shard_map/pallas_call | solution.py:122
  192.0 1.5 add_convert_fusion
  193.7 2.4 convolution_convert_fusion.1
  196.1 102.8 %all_to_all.10 = bf16[128,16,2048]{2,1,0:T(8,128)(2,1)S(1)} all-to-all(bf16[128,16,2048]{2,1,0:T(8,128)(2,1)S(1)} %bitcast.36), channel_id=1, replica_groups=mesh['gx'=8,'gyo'=8,'core'=2] {'gx','gyo','core'}, dimensions={0} | all-to-all | bytes 16777216 | tf_op jit(solution)/shard_map/all_to_all | solution.py:213
  298.9 3.2 copy-done.3
  302.1 8.6 %fusion.4 = f32[2048,768]{1,0:T(8,128)} fusion(bf16[2048,2048]{1,0:T(8,128)(2,1)S(1)} %bitcast.38, bf16[1,2048,768]{2,1,0:T(8,128)(2,1)S(1)} %copy-done.10), kind=kOutput, calls=%fused_computation.10 | convolution fusion | flops 6442450944 | bytes 17825792 | tf_op jit(solution)/shard_map/dot_general | solution.py:215
  310.7 21.3 %convolution_convert_fusion = bf16[2048,2048]{1,0:T(8,128)(2,1)} fusion(f32[2048,768]{1,0:T(8,128)} %fusion.4, bf16[2048,2048]{1,0:T(8,128)(2,1)} %bitcast.39, bf16[1,768,2048]{2,1,0:T(8,128)(2,1)S(1)} %copy-done, bf16[1,2048,768]{2,1,0:T(8,128)(2,1)} %param.32), kind=kOutput, calls=%fused_computation.4 | convolution fusion | flops 12898533376 | bytes 29360128 | tf_op jit(solution)/shard_map/dot_general | solution.py:218
  332.0 8.8 %all-to-all-start.1 = ((bf16[128,16,2048]{2,1,0:T(8,128)(2,1)}), bf16[128,16,2048]{2,1,0:T(8,128)(2,1)}, u32[]{:S(2)}, u32[]{:S(2)}) async-start(bf16[128,16,2048]{2,1,0:T(8,128)(2,1)} %bitcast.37), calls=%async_computation.1 | async-start | bytes 16777216 | tf_op jit(solution)/shard_map/all_to_all | solution.py:221
  341.0 3.7 select_reduce_fusion
  344.7 109.3 %all-to-all-done.1 = bf16[128,16,2048]{2,1,0:T(8,128)(2,1)} async-done(((bf16[128,16,2048]{2,1,0:T(8,128)(2,1)}), bf16[128,16,2048]{2,1,0:T(8,128)(2,1)}, u32[]{:S(2)}, u32[]{:S(2)}) %all-to-all-start.1) | async-done | bytes 8388640 | tf_op jit(solution)/shard_map/all_to_all | solution.py:221
  454.0 7.1 %fusion.7 = bf16[128,2048]{1,0:T(8,128)(2,1)} fusion(f32[128,2048]{1,0:T(8,128)} %select_reduce_fusion, bf16[2048,2048]{1,0:T(8,128)(2,1)} %bitcast.14, bf16[128,2048]{1,0:T(8,128)(2,1)} %copy-done.2), kind=kOutput, calls=%fused_computation.14 | convolution fusion | flops 3222011904 | bytes 10485760 | tf_op jit(solution)/shard_map/dot_general | solution.py:224
  (57 shorter events, 8.8 us)
Async XLA Ops:
  6.5 304.2 %copy-start = (bf16[1,768,2048]{2,1,0:T(8,128)(2,1)S(1)}, bf16[1,768,2048]{2,1,0:T(8,128)(2,1)}, u32[]{:S(2)}) copy-start(bf16[1,768,2048]{2,1,0:T(8,128)(2,1)} %param.33) | copy-start | bytes 9437188
  6.5 69.0 %copy-start.5 = (s32[128,8]{0,1:T(8,128)S(1)}, s32[128,8]{0,1:T(8,128)}, u32[]{:S(2)}) copy-start(s32[128,8]{0,1:T(8,128)} %param.29) | copy-start | bytes 12292
  6.5 63.6 %copy-start.9 = (s32[1,128]{1,0:T(1,128)S(1)}, s32[1,128]{1,0:T(1,128)}, u32[]{:S(2)}) copy-start(s32[1,128]{1,0:T(1,128)} %param.21) | copy-start | bytes 1540
  6.5 65.9 %copy-start.7 = (s32[28]{0:T(128)S(1)}, s32[28]{0:T(128)}, u32[]{:S(2)}) copy-start(s32[28]{0:T(128)} %param.25) | copy-start | bytes 340
  6.5 66.7 %copy-start.4 = (bf16[128,1024]{1,0:T(8,128)(2,1)S(1)}, bf16[128,1024]{1,0:T(8,128)(2,1)}, u32[]{:S(2)}) copy-start(bf16[128,1024]{1,0:T(8,128)(2,1)} %param.18) | copy-start | bytes 786436
  6.5 60.3 %all-gather.3.cloned.1.call-start = ((), (), s32[]{:S(2)}) async-start(), calls=%async_computation.2 | async-start | bytes 4718592 | tf_op jit(solution)/shard_map/all_gather | solution.py:167
  10.9 166.2 %all-gather.5.cloned.1.call-start = ((), (), s32[]{:S(2)}) async-start(), calls=%async_computation.3 | async-start | bytes 17825792 | tf_op jit(solution)/shard_map/all_gather | solution.py:186
  66.8 38.2 %collective-permute-start = (bf16[4096,512]{1,0:T(8,128)(2,1)}, bf16[4096,512]{1,0:T(8,128)(2,1)}, u32[]{:S(2)}, u32[]{:S(2)}) collective-permute-start(bf16[4096,512]{1,0:T(8,128)(2,1)} %all-gather.3.cloned.1.call-done.kc_ref.vc_ref), channel_id=1, source_target_pairs={{0,1},{1,0},{2,3},{3,2},{4,5},{5,4},{6,7},{7,6},{8,9},{9,8},{10,11... | collective-permute-start | bytes 12582920 | tf_op jit(solution)/shard_map/ppermute | solution.py:168
  126.6 67.1 %copy-start.6 = (f32[2048]{0:T(1024)S(1)}, f32[2048]{0:T(1024)}, u32[]{:S(2)}) copy-start(f32[2048]{0:T(1024)} %param.28) | copy-start | bytes 24580
  193.5 2.6 copy-start.2
  196.1 106.0 %copy-start.10 = (bf16[1,2048,768]{2,1,0:T(8,128)(2,1)S(1)}, bf16[1,2048,768]{2,1,0:T(8,128)(2,1)}, u32[]{:S(2)}) copy-start(bf16[1,2048,768]{2,1,0:T(8,128)(2,1)} %param.31) | copy-start | bytes 9437188
  298.9 3.2 copy-start.3
  332.0 8.9 %copy-start.8 = (f32[128,8]{0,1:T(8,128)S(1)}, f32[128,8]{0,1:T(8,128)}, u32[]{:S(2)}) copy-start(f32[128,8]{0,1:T(8,128)} %param.30) | copy-start | bytes 12292
  332.0 122.0 %all-to-all-start.1 = ((bf16[128,16,2048]{2,1,0:T(8,128)(2,1)}), bf16[128,16,2048]{2,1,0:T(8,128)(2,1)}, u32[]{:S(2)}, u32[]{:S(2)}) async-start(bf16[128,16,2048]{2,1,0:T(8,128)(2,1)} %bitcast.37), calls=%async_computation.1 | async-start | bytes 16777216 | tf_op jit(solution)/shard_map/all_to_all | solution.py:221
  454.0 7.1 %copy-start.1 = (bf16[1,768,2048]{2,1,0:T(8,128)(2,1)S(1)}, bf16[1,768,2048]{2,1,0:T(8,128)(2,1)}, u32[]{:S(2)}) copy-start(bf16[1,768,2048]{2,1,0:T(8,128)(2,1)} %param.33) | copy-start | bytes 9437188
Sparse Core Ops, SparseCore 0:
  11.0 55.7 all-gather.2
  69.3 107.7 all-gather.4

commit v7 on v6

--- a/solution.py
+++ b/solution.py
@@ -129,6 +129,32 @@
         out_specs=pl.BlockSpec((tokens, width), lambda j: (0, 0)),
         out_shape=jax.ShapeDtypeStruct((tokens, width), jnp.float32),
     )(attended, weight)
+
+
+def expert_kernel(x_ref, wg_ref, wu_ref, wd_ref, o_ref):
+    x = x_ref[...]
+    gate = jnp.dot(x, wg_ref[...], preferred_element_type=jnp.float32)
+    up = jnp.dot(x, wu_ref[...], preferred_element_type=jnp.float32)
+    hidden = (gate / (1.0 + jnp.exp(-gate)) * up).astype(jnp.bfloat16)
+    o_ref[...] = jnp.dot(hidden, wd_ref[...], preferred_element_type=jnp.float32).astype(o_ref.dtype)
+
+
+def expert_ffn(stacked, gate_w, up_w, down_w, block_rows=256):
+    rows, width = stacked.shape
+    hidden = gate_w.shape[1]
+    return pl.pallas_call(
+        expert_kernel,
+        grid=(rows // block_rows,),
+        in_specs=[
+            pl.BlockSpec((block_rows, width), lambda i: (i, 0)),
+            pl.BlockSpec((width, hidden), lambda i: (0, 0)),
+            pl.BlockSpec((width, hidden), lambda i: (0, 0)),
+            pl.BlockSpec((hidden, width), lambda i: (0, 0)),
+        ],
+        out_specs=pl.BlockSpec((block_rows, width), lambda i: (i, 0)),
+        out_shape=jax.ShapeDtypeStruct((rows, width), jnp.bfloat16),
+        compiler_params=pltpu.CompilerParams(vmem_limit_bytes=48 * 1024 * 1024),
+    )(stacked, gate_w, up_w, down_w)
 
 
 def on_device(
@@ -212,12 +238,7 @@
     outgoing = outgoing.reshape(expert_count, slots, model_width)
     arrived = lax.all_to_all(outgoing, TOKEN_AXES, split_axis=0, concat_axis=0, tiled=True)
     stacked = arrived.reshape(-1, model_width)
-    gate_act = jnp.dot(stacked, expert_gate[0], preferred_element_type=jnp.float32)
-    up_act = jnp.dot(stacked, expert_up[0], preferred_element_type=jnp.float32)
-    hidden = (jax.nn.silu(gate_act) * up_act).astype(jnp.bfloat16)
-    expert_out = jnp.dot(hidden, expert_down[0], preferred_element_type=jnp.float32).astype(
-        jnp.bfloat16
-    )
+    expert_out = expert_ffn(stacked, expert_gate[0], expert_up[0], expert_down[0])
     returned = lax.all_to_all(
         expert_out.reshape(arrived.shape), TOKEN_AXES, split_axis=0, concat_axis=0, tiled=True
     )

time: 475 us -> 462 us (0.973)
  matrix products: 39.3 us -> 8.99 us
  Pallas kernels: 55.6 us -> 80.9 us
  local copies, waits for them, and re-layouts: 10.3 us -> 3.12 us
  other arithmetic: 22.9 us -> 16.7 us
  waiting for transfers between devices: 214 us -> 220 us
    dot_general x2 -> x0, matrix products: 29.8 us -> none  [the longest x1 21.3 us: on_device(): jnp.dot(hidden, expert_down[0], preferred_element_type=jnp.float32)]
    pallas_call x0 -> x1, Pallas kernels: none -> 25.2 us  [expert_ffn(): pl.pallas_call(expert_kernel, grid=(rows // block_rows,), in_specs=[pl.Bl...]
    all_gather x1, waiting for transfers between devices: 50.5 us -> 56.6 us  [on_device(): lax.all_gather(out_weight, ('gyo', 'core'), axis=0, tiled=True)]
  transfers between devices with their start and end apart: 4 -> 4, of which waited for: 3 -> 3; matrix products, arithmetic and copies ran while one was open for 5% -> 4% of each run, Pallas kernels for 9% -> 9%
where the time goes in v7:
time: 462 us; the launch traced here: 456 us
  waiting for transfers between devices  220 us (48%)
  blocking collectives  103 us (22%)
  Pallas kernels  80.9 us (18%)
  other arithmetic  16.7 us (4%)
  between operations  14.2 us (3%)
  starting transfers between devices  9.25 us (2%)
  matrix products  8.99 us (2%)
    all_to_all x1, waiting for transfers between devices, on_device(): lax.all_to_all(expert_out.reshape(arrived.shape), TOKEN_AXES, split_axis=...  108 us
    all_to_all x1, blocking collectives, on_device(): lax.all_to_all(outgoing, TOKEN_AXES, split_axis=0, concat_axis=0, tiled=T...  103 us
    all_gather x1, waiting for transfers between devices, on_device(): lax.all_gather(out_weight, ('gyo', 'core'), axis=0, tiled=True)  56.6 us
    all_gather x1, waiting for transfers between devices, on_device(): lax.all_gather(kv_half(kv_cache, core), 'gx', axis=0, tiled=True)  54 us
    pallas_call x2, Pallas kernels, tree_attention(): pl.pallas_call(attention_kernel, grid=(local_heads,), in_specs=[pl.BlockS...  40.8 us
    pallas_call x1, Pallas kernels, expert_ffn(): pl.pallas_call(expert_kernel, grid=(rows // block_rows,), in_specs=[pl.Bl...  25.2 us
    pallas_call x1, Pallas kernels, projection(): pl.pallas_call(projection_kernel, grid=(weight.shape[0] // group_rows,),...  14.9 us
  transfers between devices with their start and end apart: 4, of which 3 were waited for; matrix products, arithmetic and copies ran while one was open for 4% of the time, Pallas kernels for 9%

profile of v7, /device:TPU:1, one launch (start us, length us, event | category | flops | bytes accessed | tf_op | source)
XLA Modules:
  0.0 455.5 jit_solution(4735375580676113811)
XLA Ops:
  6.6 1.4 fusion.18
  8.1 0.8 pad_maximum_fusion
  9.0 0.7 all-gather.5.cloned.1.call-update
  9.7 0.8 copy.38
  10.7 0.2 fusion.10
  10.9 54.0 %all-gather.3.cloned.1.call-done.kc_ref.vc_ref = bf16[4096,512]{1,0:T(8,128)(2,1)} async-done(((bf16[512,512]{1,0:T(8,128)(2,1)}), bf16[4096,512]{1,0:T(8,128)(2,1)}) %all-gather.3.cloned.1.call-update) | async-done | bytes 4194320 | tf_op jit(solution)/shard_map/all_gather | solution.py:193
  64.8 0.8 collective-permute-start
  66.0 0.4 fusion.7
  67.3 1.3 compare_reduce_fusion
  68.6 7.4 %fusion = pred[2048,128]{1,0:T(8,128)(4,1)S(1)} fusion(s32[128,8]{0,1:T(8,128)S(1)} %multiply_add_fusion), kind=kLoop, calls=%fused_computation.3 | loop fusion | flops 3932160 | bytes 266240 | tf_op jit(solution)/shard_map/reduce_or | solution.py:232
  76.2 0.2 broadcast_select_fusion.bf_ref
  76.5 20.5 %shard_map.163 = bf16[128,2048]{1,0:T(8,128)(2,1)S(1)} custom-call(bf16[128,2048]{1,0:T(8,128)(2,1)S(1)} %get-tuple-element.7.q_ref, bf16[4096,512]{1,0:T(8,128)(2,1)} %all-gather.3.cloned.1.call-done.kc_ref.vc_ref, bf16[4096,512]{1,0:T(8,128)(2,1)} %all-gather.3.cloned.1.call-done.kc_ref.vc_ref, bf16[128,512]{1,0:T(8,128)(2,1)S(1)} %pad_maximum_fusion.1.kn_ref.vn_ref, ...), custom_call_target="tpu_custom_call" | custom-call | tf_op jit(solution)/shard_map/pallas_call | solution.py:80
  97.0 20.4 %shard_map.164 = bf16[128,2048]{1,0:T(8,128)(2,1)S(1)} custom-call(bf16[128,2048]{1,0:T(8,128)(2,1)S(1)} %get-tuple-element.8.q_ref, bf16[4096,512]{1,0:T(8,128)(2,1)} %collective-permute-done.kc_ref.vc_ref, bf16[4096,512]{1,0:T(8,128)(2,1)} %collective-permute-done.kc_ref.vc_ref, bf16[128,512]{1,0:T(8,128)(2,1)S(1)} %pad_maximum_fusion.2.kn_ref.vn_ref, ...), custom_call_target="tpu_custom_call" | custom-call | tf_op jit(solution)/shard_map/pallas_call | solution.py:80
  117.3 1.2 maximum_select_fusion.a_ref
  118.6 56.6 %all-gather.5.cloned.1.call-done.w_ref = bf16[4096,2048]{1,0:T(8,128)(2,1)} async-done(((bf16[256,2048]{1,0:T(8,128)(2,1)}), bf16[4096,2048]{1,0:T(8,128)(2,1)}) %all-gather.5.cloned.1.call-update) | async-done | bytes 16777232 | tf_op jit(solution)/shard_map/all_gather | solution.py:212
  175.1 14.9 %shard_map.165 = f32[128,2048]{1,0:T(8,128)} custom-call(bf16[128,4096]{1,0:T(8,128)(2,1)} %maximum_select_fusion.a_ref, bf16[4096,2048]{1,0:T(8,128)(2,1)} %all-gather.5.cloned.1.call-done.w_ref), custom_call_target="tpu_custom_call" | custom-call | tf_op jit(solution)/shard_map/pallas_call | solution.py:122
  190.0 1.3 add_convert_fusion
  191.6 2.4 convolution_convert_fusion
  194.0 102.9 %all_to_all.10 = bf16[128,16,2048]{2,1,0:T(8,128)(2,1)} all-to-all(bf16[128,16,2048]{2,1,0:T(8,128)(2,1)S(1)} %bitcast.28), channel_id=1, replica_groups=mesh['gx'=8,'gyo'=8,'core'=2] {'gx','gyo','core'}, dimensions={0} | all-to-all | bytes 16777216 | tf_op jit(solution)/shard_map/all_to_all | solution.py:239
  296.9 25.2 %shard_map.166 = bf16[2048,2048]{1,0:T(8,128)(2,1)} custom-call(bf16[2048,2048]{1,0:T(8,128)(2,1)} %bitcast.30, bf16[2048,768]{1,0:T(8,128)(2,1)S(1)} %bitcast.27, bf16[2048,768]{1,0:T(8,128)(2,1)} %bitcast.31, bf16[768,2048]{1,0:T(8,128)(2,1)} %bitcast.32), custom_call_target="tpu_custom_call" | custom-call | tf_op jit(solution)/shard_map/pallas_call | solution.py:145
  322.1 8.3 %all-to-all-start.1 = ((bf16[128,16,2048]{2,1,0:T(8,128)(2,1)}), bf16[128,16,2048]{2,1,0:T(8,128)(2,1)}, u32[]{:S(2)}, u32[]{:S(2)}) async-start(bf16[128,16,2048]{2,1,0:T(8,128)(2,1)} %bitcast.29), calls=%async_computation.1 | async-start | bytes 16777216 | tf_op jit(solution)/shard_map/all_to_all | solution.py:242
  330.6 2.7 select_reduce_fusion
  333.4 108.3 %all-to-all-done.1 = bf16[128,16,2048]{2,1,0:T(8,128)(2,1)} async-done(((bf16[128,16,2048]{2,1,0:T(8,128)(2,1)}), bf16[128,16,2048]{2,1,0:T(8,128)(2,1)}, u32[]{:S(2)}, u32[]{:S(2)}) %all-to-all-start.1) | async-done | bytes 8388640 | tf_op jit(solution)/shard_map/all_to_all | solution.py:242
  441.7 6.6 %fusion.1 = bf16[128,2048]{1,0:T(8,128)(2,1)} fusion(f32[128,2048]{1,0:T(8,128)S(1)} %select_reduce_fusion, bf16[2048,2048]{1,0:T(8,128)(2,1)} %bitcast.14, bf16[128,2048]{1,0:T(8,128)(2,1)S(1)} %add_convert_fusion), kind=kOutput, calls=%fused_computation.7 | convolution fusion | flops 3222011904 | bytes 10485760 | tf_op jit(solution)/shard_map/dot_general | solution.py:245
  (60 shorter events, 2.1 us)
Async XLA Ops:
  6.5 62.0 %copy-start.4 = (s32[128,8]{0,1:T(8,128)S(1)}, s32[128,8]{0,1:T(8,128)}, u32[]{:S(2)}) copy-start(s32[128,8]{0,1:T(8,128)} %param.29) | copy-start | bytes 12292
  6.5 59.9 %copy-start.8 = (s32[1,128]{1,0:T(1,128)S(1)}, s32[1,128]{1,0:T(1,128)}, u32[]{:S(2)}) copy-start(s32[1,128]{1,0:T(1,128)} %param.21) | copy-start | bytes 1540
  6.5 59.9 %copy-start.10 = (s32[1,8]{1,0:T(1,128)S(1)}, s32[1,8]{1,0:T(1,128)}, u32[]{:S(2)}) copy-start(s32[1,8]{1,0:T(1,128)} %param.22) | copy-start | bytes 100
  6.5 60.0 %copy-start.11 = (s32[16]{0:T(128)S(1)}, s32[16]{0:T(128)}, u32[]{:S(2)}) copy-start(s32[16]{0:T(128)} %param.24) | copy-start | bytes 196
  6.5 60.1 %copy-start.12 = (s32[8]{0:T(128)S(1)}, s32[8]{0:T(128)}, u32[]{:S(2)}) copy-start(s32[8]{0:T(128)} %param.23) | copy-start | bytes 100
  6.5 60.2 %copy-start.6 = (s32[28]{0:T(128)S(1)}, s32[28]{0:T(128)}, u32[]{:S(2)}) copy-start(s32[28]{0:T(128)} %param.25) | copy-start | bytes 340
  6.6 60.2 %copy-start.9 = (s32[28]{0:T(128)S(1)}, s32[28]{0:T(128)}, u32[]{:S(2)}) copy-start(s32[28]{0:T(128)} %param.26) | copy-start | bytes 340
  6.6 60.4 %copy-start.3 = (bf16[128,1024]{1,0:T(8,128)(2,1)S(1)}, bf16[128,1024]{1,0:T(8,128)(2,1)}, u32[]{:S(2)}) copy-start(bf16[128,1024]{1,0:T(8,128)(2,1)} %param.18) | copy-start | bytes 786436
  6.6 69.5 %copy-start.1 = (bf16[128,4096]{1,0:T(8,128)(2,1)S(1)}, bf16[128,4096]{1,0:T(8,128)(2,1)}, u32[]{:S(2)}) copy-start(bf16[128,4096]{1,0:T(8,128)(2,1)} %param.17) | copy-start | bytes 3145732
  6.6 58.3 %all-gather.3.cloned.1.call-start = ((), (), s32[]{:S(2)}) async-start(), calls=%async_computation.2 | async-start | bytes 4718592 | tf_op jit(solution)/shard_map/all_gather | solution.py:193
  8.9 166.2 %all-gather.5.cloned.1.call-start = ((), (), s32[]{:S(2)}) async-start(), calls=%async_computation.3 | async-start | bytes 17825792 | tf_op jit(solution)/shard_map/all_gather | solution.py:212
  64.8 32.1 %collective-permute-start = (bf16[4096,512]{1,0:T(8,128)(2,1)}, bf16[4096,512]{1,0:T(8,128)(2,1)}, u32[]{:S(2)}, u32[]{:S(2)}) collective-permute-start(bf16[4096,512]{1,0:T(8,128)(2,1)} %all-gather.3.cloned.1.call-done.kc_ref.vc_ref), channel_id=1, source_target_pairs={{0,1},{1,0},{2,3},{3,2},{4,5},{5,4},{6,7},{7,6},{8,9},{9,8},{10,11... | collective-permute-start | bytes 12582920 | tf_op jit(solution)/shard_map/ppermute | solution.py:194
  118.6 71.5 %copy-start.2 = (bf16[128,2048]{1,0:T(8,128)(2,1)S(1)}, bf16[128,2048]{1,0:T(8,128)(2,1)}, u32[]{:S(2)}) copy-start(bf16[128,2048]{1,0:T(8,128)(2,1)} %param.20) | copy-start | bytes 1572868
  118.6 73.0 %copy-start.5 = (f32[2048]{0:T(1024)S(1)}, f32[2048]{0:T(1024)}, u32[]{:S(2)}) copy-start(f32[2048]{0:T(1024)} %param.28) | copy-start | bytes 24580
  194.0 102.9 %copy-start = (bf16[1,2048,768]{2,1,0:T(8,128)(2,1)S(1)}, bf16[1,2048,768]{2,1,0:T(8,128)(2,1)}, u32[]{:S(2)}) copy-start(bf16[1,2048,768]{2,1,0:T(8,128)(2,1)} %param.31) | copy-start | bytes 9437188
  322.1 8.4 %copy-start.7 = (f32[128,8]{0,1:T(8,128)S(1)}, f32[128,8]{0,1:T(8,128)}, u32[]{:S(2)}) copy-start(f32[128,8]{0,1:T(8,128)} %param.30) | copy-start | bytes 12292
  322.1 119.6 %all-to-all-start.1 = ((bf16[128,16,2048]{2,1,0:T(8,128)(2,1)}), bf16[128,16,2048]{2,1,0:T(8,128)(2,1)}, u32[]{:S(2)}, u32[]{:S(2)}) async-start(bf16[128,16,2048]{2,1,0:T(8,128)(2,1)} %bitcast.29), calls=%async_computation.1 | async-start | bytes 16777216 | tf_op jit(solution)/shard_map/all_to_all | solution.py:242
Sparse Core Ops, SparseCore 0:
  9.0 55.7 all-gather.2
  67.3 107.7 all-gather.4

commit v8 on v7

--- a/solution.py
+++ b/solution.py
@@ -1,3 +1,5 @@
+import functools
+
 import jax
 import jax.numpy as jnp
 from jax import lax
@@ -107,29 +109,34 @@
     )
 
 
-def projection_kernel(a_ref, w_ref, o_ref):
+def projection_kernel(a_ref, w_ref, o_ref, *, group_rows):
     @pl.when(pl.program_id(0) == 0)
     def _():
         o_ref[...] = jnp.zeros_like(o_ref)
 
-    part = jnp.dot(a_ref[...], w_ref[...], preferred_element_type=jnp.float32)
-    o_ref[...] += part.astype(jnp.bfloat16).astype(jnp.float32)
-
-
-def projection(attended, weight, group_rows):
+    total = o_ref[...]
+    for group in range(w_ref.shape[0] // group_rows):
+        rows = slice(group * group_rows, (group + 1) * group_rows)
+        part = jnp.dot(a_ref[:, rows], w_ref[rows, :], preferred_element_type=jnp.float32)
+        total = total + part.astype(jnp.bfloat16).astype(jnp.float32)
+    o_ref[...] = total
+
+
+def projection(attended, weight, group_rows, groups_per_step=4):
     tokens = attended.shape[0]
     width = weight.shape[1]
+    step_rows = group_rows * groups_per_step
     return pl.pallas_call(
-        projection_kernel,
-        grid=(weight.shape[0] // group_rows,),
+        functools.partial(projection_kernel, group_rows=group_rows),
+        grid=(weight.shape[0] // step_rows,),
         in_specs=[
-            pl.BlockSpec((tokens, group_rows), lambda j: (0, j)),
-            pl.BlockSpec((group_rows, width), lambda j: (j, 0)),
+            pl.BlockSpec((tokens, step_rows), lambda j: (0, j)),
+            pl.BlockSpec((step_rows, width), lambda j: (j, 0)),
         ],
         out_specs=pl.BlockSpec((tokens, width), lambda j: (0, 0)),
         out_shape=jax.ShapeDtypeStruct((tokens, width), jnp.float32),
+        compiler_params=pltpu.CompilerParams(vmem_limit_bytes=48 * 1024 * 1024),
     )(attended, weight)
-
 
 def expert_kernel(x_ref, wg_ref, wu_ref, wd_ref, o_ref):
     x = x_ref[...]
@@ -139,7 +146,7 @@
     o_ref[...] = jnp.dot(hidden, wd_ref[...], preferred_element_type=jnp.float32).astype(o_ref.dtype)
 
 
-def expert_ffn(stacked, gate_w, up_w, down_w, block_rows=256):
+def expert_ffn(stacked, gate_w, up_w, down_w, block_rows=512):
     rows, width = stacked.shape
     hidden = gate_w.shape[1]
     return pl.pallas_call(

time: 462 us -> 453 us (0.981)
  Pallas kernels: 80.9 us -> 73.7 us
    pallas_call x1, Pallas kernels: 14.9 us -> 7.8 us  [projection(): pl.pallas_call(functools.partial(projection_kernel, group_rows=group_rows...]
  transfers between devices with their start and end apart: 4 -> 4, of which waited for: 3 -> 3; matrix products, arithmetic and copies ran while one was open for 4% -> 3% of each run, Pallas kernels for 9% -> 9%
where the time goes in v8:
time: 453 us; the launch traced here: 447 us
  waiting for transfers between devices  220 us (49%)
  blocking collectives  103 us (23%)
  Pallas kernels  73.7 us (16%)
  other arithmetic  14.5 us (3%)
  between operations  14.2 us (3%)
  starting transfers between devices  9.25 us (2%)
  matrix products  8.99 us (2%)
    all_to_all x1, waiting for transfers between devices, on_device(): lax.all_to_all(expert_out.reshape(arrived.shape), TOKEN_AXES, split_axis=...  108 us
    all_to_all x1, blocking collectives, on_device(): lax.all_to_all(outgoing, TOKEN_AXES, split_axis=0, concat_axis=0, tiled=T...  103 us
    all_gather x1, waiting for transfers between devices, on_device(): lax.all_gather(out_weight, ('gyo', 'core'), axis=0, tiled=True)  57.5 us
    all_gather x1, waiting for transfers between devices, on_device(): lax.all_gather(kv_half(kv_cache, core), 'gx', axis=0, tiled=True)  54 us
    pallas_call x2, Pallas kernels, tree_attention(): pl.pallas_call(attention_kernel, grid=(local_heads,), in_specs=[pl.BlockS...  40.8 us
    pallas_call x1, Pallas kernels, expert_ffn(): pl.pallas_call(expert_kernel, grid=(rows // block_rows,), in_specs=[pl.Bl...  25.1 us
  transfers between devices with their start and end apart: 4, of which 3 were waited for; matrix products, arithmetic and copies ran while one was open for 3% of the time, Pallas kernels for 9%

profile of v8, /device:TPU:1, one launch (start us, length us, event | category | flops | bytes accessed | tf_op | source)
XLA Modules:
  0.0 447.1 jit_solution(8830096272165785366)
XLA Ops:
  6.6 1.4 fusion.18
  8.1 0.8 pad_maximum_fusion
  9.0 0.7 all-gather.5.cloned.1.call-update
  9.7 0.8 copy.38
  10.7 0.2 fusion.10
  10.9 54.0 %all-gather.3.cloned.1.call-done.kc_ref.vc_ref = bf16[4096,512]{1,0:T(8,128)(2,1)} async-done(((bf16[512,512]{1,0:T(8,128)(2,1)}), bf16[4096,512]{1,0:T(8,128)(2,1)}) %all-gather.3.cloned.1.call-update) | async-done | bytes 4194320 | tf_op jit(solution)/shard_map/all_gather | solution.py:200
  64.8 0.8 collective-permute-start
  66.0 0.4 fusion.7
  67.3 1.3 compare_reduce_fusion
  68.6 7.4 %fusion = pred[2048,128]{1,0:T(8,128)(4,1)S(1)} fusion(s32[128,8]{0,1:T(8,128)S(1)} %multiply_add_fusion), kind=kLoop, calls=%fused_computation.3 | loop fusion | flops 3932160 | bytes 266240 | tf_op jit(solution)/shard_map/reduce_or | solution.py:239
  76.2 0.2 broadcast_select_fusion.bf_ref
  76.5 20.5 %shard_map.163 = bf16[128,2048]{1,0:T(8,128)(2,1)S(1)} custom-call(bf16[128,2048]{1,0:T(8,128)(2,1)S(1)} %get-tuple-element.7.q_ref, bf16[4096,512]{1,0:T(8,128)(2,1)} %all-gather.3.cloned.1.call-done.kc_ref.vc_ref, bf16[4096,512]{1,0:T(8,128)(2,1)} %all-gather.3.cloned.1.call-done.kc_ref.vc_ref, bf16[128,512]{1,0:T(8,128)(2,1)S(1)} %pad_maximum_fusion.1.kn_ref.vn_ref, ...), custom_call_target="tpu_custom_call" | custom-call | tf_op jit(solution)/shard_map/pallas_call | solution.py:82
  97.0 20.4 %shard_map.164 = bf16[128,2048]{1,0:T(8,128)(2,1)S(1)} custom-call(bf16[128,2048]{1,0:T(8,128)(2,1)S(1)} %get-tuple-element.8.q_ref, bf16[4096,512]{1,0:T(8,128)(2,1)} %collective-permute-done.kc_ref.vc_ref, bf16[4096,512]{1,0:T(8,128)(2,1)} %collective-permute-done.kc_ref.vc_ref, bf16[128,512]{1,0:T(8,128)(2,1)S(1)} %pad_maximum_fusion.2.kn_ref.vn_ref, ...), custom_call_target="tpu_custom_call" | custom-call | tf_op jit(solution)/shard_map/pallas_call | solution.py:82
  117.3 0.3 maximum_select_fusion.a_ref
  117.6 57.5 %all-gather.5.cloned.1.call-done.w_ref = bf16[4096,2048]{1,0:T(8,128)(2,1)} async-done(((bf16[256,2048]{1,0:T(8,128)(2,1)}), bf16[4096,2048]{1,0:T(8,128)(2,1)}) %all-gather.5.cloned.1.call-update) | async-done | bytes 16777232 | tf_op jit(solution)/shard_map/all_gather | solution.py:219
  175.1 7.8 %shard_map.165 = f32[128,2048]{1,0:T(8,128)S(1)} custom-call(bf16[128,4096]{1,0:T(8,128)(2,1)S(1)} %maximum_select_fusion.a_ref, bf16[4096,2048]{1,0:T(8,128)(2,1)} %all-gather.5.cloned.1.call-done.w_ref), custom_call_target="tpu_custom_call" | custom-call | tf_op jit(solution)/shard_map/pallas_call | solution.py:129
  183.1 0.2 fusion.2
  183.3 2.4 convolution_convert_fusion
  185.7 102.9 %all_to_all.10 = bf16[128,16,2048]{2,1,0:T(8,128)(2,1)} all-to-all(bf16[128,16,2048]{2,1,0:T(8,128)(2,1)S(1)} %bitcast.28), channel_id=1, replica_groups=mesh['gx'=8,'gyo'=8,'core'=2] {'gx','gyo','core'}, dimensions={0} | all-to-all | bytes 16777216 | tf_op jit(solution)/shard_map/all_to_all | solution.py:246
  288.6 25.1 %shard_map.166 = bf16[2048,2048]{1,0:T(8,128)(2,1)} custom-call(bf16[2048,2048]{1,0:T(8,128)(2,1)} %bitcast.30, bf16[2048,768]{1,0:T(8,128)(2,1)S(1)} %bitcast.27, bf16[2048,768]{1,0:T(8,128)(2,1)} %bitcast.31, bf16[768,2048]{1,0:T(8,128)(2,1)} %bitcast.32), custom_call_target="tpu_custom_call" | custom-call | tf_op jit(solution)/shard_map/pallas_call | solution.py:152
  313.7 8.3 %all-to-all-start.1 = ((bf16[128,16,2048]{2,1,0:T(8,128)(2,1)}), bf16[128,16,2048]{2,1,0:T(8,128)(2,1)}, u32[]{:S(2)}, u32[]{:S(2)}) async-start(bf16[128,16,2048]{2,1,0:T(8,128)(2,1)} %bitcast.29), calls=%async_computation.1 | async-start | bytes 16777216 | tf_op jit(solution)/shard_map/all_to_all | solution.py:249
  322.2 2.7 select_reduce_fusion
  325.0 108.3 %all-to-all-done.1 = bf16[128,16,2048]{2,1,0:T(8,128)(2,1)} async-done(((bf16[128,16,2048]{2,1,0:T(8,128)(2,1)}), bf16[128,16,2048]{2,1,0:T(8,128)(2,1)}, u32[]{:S(2)}, u32[]{:S(2)}) %all-to-all-start.1) | async-done | bytes 8388640 | tf_op jit(solution)/shard_map/all_to_all | solution.py:249
  433.3 6.6 %fusion.1 = bf16[128,2048]{1,0:T(8,128)(2,1)} fusion(f32[128,2048]{1,0:T(8,128)S(1)} %select_reduce_fusion, bf16[2048,2048]{1,0:T(8,128)(2,1)} %bitcast.14, bf16[128,2048]{1,0:T(8,128)(2,1)S(1)} %add_convert_fusion), kind=kOutput, calls=%fused_computation.7 | convolution fusion | flops 3222011904 | bytes 10485760 | tf_op jit(solution)/shard_map/dot_general | solution.py:252
  (60 shorter events, 2.0 us)
Async XLA Ops:
  6.5 62.0 %copy-start.4 = (s32[128,8]{0,1:T(8,128)S(1)}, s32[128,8]{0,1:T(8,128)}, u32[]{:S(2)}) copy-start(s32[128,8]{0,1:T(8,128)} %param.29) | copy-start | bytes 12292
  6.5 59.9 %copy-start.8 = (s32[1,128]{1,0:T(1,128)S(1)}, s32[1,128]{1,0:T(1,128)}, u32[]{:S(2)}) copy-start(s32[1,128]{1,0:T(1,128)} %param.21) | copy-start | bytes 1540
  6.5 59.9 %copy-start.10 = (s32[1,8]{1,0:T(1,128)S(1)}, s32[1,8]{1,0:T(1,128)}, u32[]{:S(2)}) copy-start(s32[1,8]{1,0:T(1,128)} %param.22) | copy-start | bytes 100
  6.5 60.0 %copy-start.11 = (s32[16]{0:T(128)S(1)}, s32[16]{0:T(128)}, u32[]{:S(2)}) copy-start(s32[16]{0:T(128)} %param.24) | copy-start | bytes 196
  6.5 60.1 %copy-start.12 = (s32[8]{0:T(128)S(1)}, s32[8]{0:T(128)}, u32[]{:S(2)}) copy-start(s32[8]{0:T(128)} %param.23) | copy-start | bytes 100
  6.5 60.2 %copy-start.6 = (s32[28]{0:T(128)S(1)}, s32[28]{0:T(128)}, u32[]{:S(2)}) copy-start(s32[28]{0:T(128)} %param.25) | copy-start | bytes 340
  6.6 60.2 %copy-start.9 = (s32[28]{0:T(128)S(1)}, s32[28]{0:T(128)}, u32[]{:S(2)}) copy-start(s32[28]{0:T(128)} %param.26) | copy-start | bytes 340
  6.6 60.4 %copy-start.3 = (bf16[128,1024]{1,0:T(8,128)(2,1)S(1)}, bf16[128,1024]{1,0:T(8,128)(2,1)}, u32[]{:S(2)}) copy-start(bf16[128,1024]{1,0:T(8,128)(2,1)} %param.18) | copy-start | bytes 786436
  6.6 69.5 %copy-start.1 = (bf16[128,4096]{1,0:T(8,128)(2,1)S(1)}, bf16[128,4096]{1,0:T(8,128)(2,1)}, u32[]{:S(2)}) copy-start(bf16[128,4096]{1,0:T(8,128)(2,1)} %param.17) | copy-start | bytes 3145732
  6.6 58.3 %all-gather.3.cloned.1.call-start = ((), (), s32[]{:S(2)}) async-start(), calls=%async_computation.2 | async-start | bytes 4718592 | tf_op jit(solution)/shard_map/all_gather | solution.py:200
  8.9 166.2 %all-gather.5.cloned.1.call-start = ((), (), s32[]{:S(2)}) async-start(), calls=%async_computation.3 | async-start | bytes 17825792 | tf_op jit(solution)/shard_map/all_gather | solution.py:219
  64.8 32.1 %collective-permute-start = (bf16[4096,512]{1,0:T(8,128)(2,1)}, bf16[4096,512]{1,0:T(8,128)(2,1)}, u32[]{:S(2)}, u32[]{:S(2)}) collective-permute-start(bf16[4096,512]{1,0:T(8,128)(2,1)} %all-gather.3.cloned.1.call-done.kc_ref.vc_ref), channel_id=1, source_target_pairs={{0,1},{1,0},{2,3},{3,2},{4,5},{5,4},{6,7},{7,6},{8,9},{9,8},{10,11... | collective-permute-start | bytes 12582920 | tf_op jit(solution)/shard_map/ppermute | solution.py:201
  117.6 65.4 %copy-start.2 = (bf16[128,2048]{1,0:T(8,128)(2,1)S(1)}, bf16[128,2048]{1,0:T(8,128)(2,1)}, u32[]{:S(2)}) copy-start(bf16[128,2048]{1,0:T(8,128)(2,1)} %param.20) | copy-start | bytes 1572868
  117.6 65.7 %copy-start.5 = (f32[2048]{0:T(1024)S(1)}, f32[2048]{0:T(1024)}, u32[]{:S(2)}) copy-start(f32[2048]{0:T(1024)} %param.28) | copy-start | bytes 24580
  185.7 102.9 %copy-start = (bf16[1,2048,768]{2,1,0:T(8,128)(2,1)S(1)}, bf16[1,2048,768]{2,1,0:T(8,128)(2,1)}, u32[]{:S(2)}) copy-start(bf16[1,2048,768]{2,1,0:T(8,128)(2,1)} %param.31) | copy-start | bytes 9437188
  313.7 8.4 %copy-start.7 = (f32[128,8]{0,1:T(8,128)S(1)}, f32[128,8]{0,1:T(8,128)}, u32[]{:S(2)}) copy-start(f32[128,8]{0,1:T(8,128)} %param.30) | copy-start | bytes 12292
  313.7 119.6 %all-to-all-start.1 = ((bf16[128,16,2048]{2,1,0:T(8,128)(2,1)}), bf16[128,16,2048]{2,1,0:T(8,128)(2,1)}, u32[]{:S(2)}, u32[]{:S(2)}) async-start(bf16[128,16,2048]{2,1,0:T(8,128)(2,1)} %bitcast.29), calls=%async_computation.1 | async-start | bytes 16777216 | tf_op jit(solution)/shard_map/all_to_all | solution.py:249
Sparse Core Ops, SparseCore 0:
  9.0 55.7 all-gather.2
  67.3 107.7 all-gather.4

commit v9 on v8

--- a/solution.py
+++ b/solution.py
@@ -249,11 +249,11 @@
     returned = lax.all_to_all(
         expert_out.reshape(arrived.shape), TOKEN_AXES, split_axis=0, concat_axis=0, tiled=True
     )
-    routed_sum = jnp.dot(
-        weight_pick,
-        returned.reshape(-1, model_width).astype(jnp.float32),
-        precision=lax.Precision.HIGH,
-        preferred_element_type=jnp.float32,
+    returned_rows = returned.reshape(-1, model_width)
+    weight_high = weight_pick.astype(jnp.bfloat16)
+    weight_low = (weight_pick - weight_high.astype(jnp.float32)).astype(jnp.bfloat16)
+    routed_sum = jnp.dot(weight_high, returned_rows, preferred_element_type=jnp.float32) + jnp.dot(
+        weight_low, returned_rows, preferred_element_type=jnp.float32
     )
     return (mixed_float + routed_sum).astype(jnp.bfloat16)
 

time: 453 us -> 457 us (level)
    dot_general x1 -> x2, matrix products: 6.58 us -> 10.2 us  [the longest x1 5.53 us: on_device(): jnp.dot(weight_low, returned_rows, preferred_element_type=jnp.float32)]
where the time goes in v9:
time: 457 us; the launch traced here: 451 us
  waiting for transfers between devices  220 us (48%)
  blocking collectives  103 us (23%)
  Pallas kernels  73.7 us (16%)
  other arithmetic  14.5 us (3%)
  between operations  14.2 us (3%)
  matrix products  12.6 us (3%)
  starting transfers between devices  9.25 us (2%)
    all_to_all x1, waiting for transfers between devices, on_device(): lax.all_to_all(expert_out.reshape(arrived.shape), TOKEN_AXES, split_axis=...  108 us
    all_to_all x1, blocking collectives, on_device(): lax.all_to_all(outgoing, TOKEN_AXES, split_axis=0, concat_axis=0, tiled=T...  103 us
    all_gather x1, waiting for transfers between devices, on_device(): lax.all_gather(out_weight, ('gyo', 'core'), axis=0, tiled=True)  57.5 us
    all_gather x1, waiting for transfers between devices, on_device(): lax.all_gather(kv_half(kv_cache, core), 'gx', axis=0, tiled=True)  54 us
    pallas_call x2, Pallas kernels, tree_attention(): pl.pallas_call(attention_kernel, grid=(local_heads,), in_specs=[pl.BlockS...  40.8 us
    pallas_call x1, Pallas kernels, expert_ffn(): pl.pallas_call(expert_kernel, grid=(rows // block_rows,), in_specs=[pl.Bl...  25.1 us
  transfers between devices with their start and end apart: 4, of which 3 were waited for; matrix products, arithmetic and copies ran while one was open for 3% of the time, Pallas kernels for 9%

profile of v9, /device:TPU:1, one launch (start us, length us, event | category | flops | bytes accessed | tf_op | source)
XLA Modules:
  0.0 450.7 jit_solution(3710450605511036638)
XLA Ops:
  6.6 1.4 fusion.22
  8.1 0.8 pad_maximum_fusion
  9.0 0.7 all-gather.5.cloned.1.call-update
  9.7 0.8 copy.38
  10.7 0.2 fusion.11
  10.9 54.0 %all-gather.3.cloned.1.call-done.kc_ref.vc_ref = bf16[4096,512]{1,0:T(8,128)(2,1)} async-done(((bf16[512,512]{1,0:T(8,128)(2,1)}), bf16[4096,512]{1,0:T(8,128)(2,1)}) %all-gather.3.cloned.1.call-update) | async-done | bytes 4194320 | tf_op jit(solution)/shard_map/all_gather | solution.py:200
  64.8 0.8 collective-permute-start
  66.0 0.4 fusion.8
  67.3 1.3 compare_reduce_fusion
  68.6 7.4 %fusion = pred[2048,128]{1,0:T(8,128)(4,1)S(1)} fusion(s32[128,8]{0,1:T(8,128)S(1)} %multiply_add_fusion), kind=kLoop, calls=%fused_computation.3 | loop fusion | flops 3932160 | bytes 266240 | tf_op jit(solution)/shard_map/reduce_or | solution.py:239
  76.2 0.2 broadcast_select_fusion.bf_ref
  76.5 20.5 %shard_map.163 = bf16[128,2048]{1,0:T(8,128)(2,1)S(1)} custom-call(bf16[128,2048]{1,0:T(8,128)(2,1)S(1)} %get-tuple-element.7.q_ref, bf16[4096,512]{1,0:T(8,128)(2,1)} %all-gather.3.cloned.1.call-done.kc_ref.vc_ref, bf16[4096,512]{1,0:T(8,128)(2,1)} %all-gather.3.cloned.1.call-done.kc_ref.vc_ref, bf16[128,512]{1,0:T(8,128)(2,1)S(1)} %pad_maximum_fusion.1.kn_ref.vn_ref, ...), custom_call_target="tpu_custom_call" | custom-call | tf_op jit(solution)/shard_map/pallas_call | solution.py:82
  97.0 20.4 %shard_map.164 = bf16[128,2048]{1,0:T(8,128)(2,1)S(1)} custom-call(bf16[128,2048]{1,0:T(8,128)(2,1)S(1)} %get-tuple-element.8.q_ref, bf16[4096,512]{1,0:T(8,128)(2,1)} %collective-permute-done.kc_ref.vc_ref, bf16[4096,512]{1,0:T(8,128)(2,1)} %collective-permute-done.kc_ref.vc_ref, bf16[128,512]{1,0:T(8,128)(2,1)S(1)} %pad_maximum_fusion.2.kn_ref.vn_ref, ...), custom_call_target="tpu_custom_call" | custom-call | tf_op jit(solution)/shard_map/pallas_call | solution.py:82
  117.3 0.3 maximum_select_fusion.a_ref
  117.6 57.5 %all-gather.5.cloned.1.call-done.w_ref = bf16[4096,2048]{1,0:T(8,128)(2,1)} async-done(((bf16[256,2048]{1,0:T(8,128)(2,1)}), bf16[4096,2048]{1,0:T(8,128)(2,1)}) %all-gather.5.cloned.1.call-update) | async-done | bytes 16777232 | tf_op jit(solution)/shard_map/all_gather | solution.py:219
  175.1 7.8 %shard_map.165 = f32[128,2048]{1,0:T(8,128)S(1)} custom-call(bf16[128,4096]{1,0:T(8,128)(2,1)S(1)} %maximum_select_fusion.a_ref, bf16[4096,2048]{1,0:T(8,128)(2,1)} %all-gather.5.cloned.1.call-done.w_ref), custom_call_target="tpu_custom_call" | custom-call | tf_op jit(solution)/shard_map/pallas_call | solution.py:129
  183.3 2.4 convolution_convert_fusion
  185.7 102.9 %all_to_all.10 = bf16[128,16,2048]{2,1,0:T(8,128)(2,1)} all-to-all(bf16[128,16,2048]{2,1,0:T(8,128)(2,1)S(1)} %bitcast.28), channel_id=1, replica_groups=mesh['gx'=8,'gyo'=8,'core'=2] {'gx','gyo','core'}, dimensions={0} | all-to-all | bytes 16777216 | tf_op jit(solution)/shard_map/all_to_all | solution.py:246
  288.6 25.1 %shard_map.166 = bf16[2048,2048]{1,0:T(8,128)(2,1)} custom-call(bf16[2048,2048]{1,0:T(8,128)(2,1)} %bitcast.30, bf16[2048,768]{1,0:T(8,128)(2,1)S(1)} %bitcast.27, bf16[2048,768]{1,0:T(8,128)(2,1)} %bitcast.31, bf16[768,2048]{1,0:T(8,128)(2,1)} %bitcast.32), custom_call_target="tpu_custom_call" | custom-call | tf_op jit(solution)/shard_map/pallas_call | solution.py:152
  313.7 8.3 %all-to-all-start.1 = ((bf16[128,16,2048]{2,1,0:T(8,128)(2,1)}), bf16[128,16,2048]{2,1,0:T(8,128)(2,1)}, u32[]{:S(2)}, u32[]{:S(2)}) async-start(bf16[128,16,2048]{2,1,0:T(8,128)(2,1)} %bitcast.29), calls=%async_computation.1 | async-start | bytes 16777216 | tf_op jit(solution)/shard_map/all_to_all | solution.py:249
  322.2 2.7 select_reduce_fusion
  325.0 108.3 %all-to-all-done.1 = bf16[128,16,2048]{2,1,0:T(8,128)(2,1)} async-done(((bf16[128,16,2048]{2,1,0:T(8,128)(2,1)}), bf16[128,16,2048]{2,1,0:T(8,128)(2,1)}, u32[]{:S(2)}, u32[]{:S(2)}) %all-to-all-start.1) | async-done | bytes 8388640 | tf_op jit(solution)/shard_map/all_to_all | solution.py:249
  433.3 4.6 %fusion.15 = f32[128,2048]{1,0:T(8,128)S(1)} fusion(bf16[2048,2048]{1,0:T(8,128)(2,1)} %bitcast.14, f32[128,2048]{1,0:T(8,128)S(1)} %select_reduce_fusion), kind=kOutput, calls=%fused_computation.33 | convolution fusion | flops 1074003968 | bytes 10485760 | tf_op jit(solution)/shard_map/dot_general | solution.py:255
  437.9 5.5 %fusion.2 = bf16[128,2048]{1,0:T(8,128)(2,1)} fusion(f32[128,2048]{1,0:T(8,128)S(1)} %fusion.15, bf16[2048,2048]{1,0:T(8,128)(2,1)} %bitcast.14, bf16[128,2048]{1,0:T(8,128)(2,1)S(1)} %add_convert_fusion, f32[128,2048]{1,0:T(8,128)S(1)} %select_reduce_fusion), kind=kOutput, calls=%fused_computation.8 | convolution fusion | flops 1075838976 | bytes 11534336 | tf_op jit(solution)/shard_map/dot_general | solution.py:255
  (61 shorter events, 2.2 us)
Async XLA Ops:
  6.5 62.0 %copy-start.4 = (s32[128,8]{0,1:T(8,128)S(1)}, s32[128,8]{0,1:T(8,128)}, u32[]{:S(2)}) copy-start(s32[128,8]{0,1:T(8,128)} %param.29) | copy-start | bytes 12292
  6.5 59.9 %copy-start.8 = (s32[1,128]{1,0:T(1,128)S(1)}, s32[1,128]{1,0:T(1,128)}, u32[]{:S(2)}) copy-start(s32[1,128]{1,0:T(1,128)} %param.21) | copy-start | bytes 1540
  6.5 59.9 %copy-start.10 = (s32[1,8]{1,0:T(1,128)S(1)}, s32[1,8]{1,0:T(1,128)}, u32[]{:S(2)}) copy-start(s32[1,8]{1,0:T(1,128)} %param.22) | copy-start | bytes 100
  6.5 60.0 %copy-start.11 = (s32[16]{0:T(128)S(1)}, s32[16]{0:T(128)}, u32[]{:S(2)}) copy-start(s32[16]{0:T(128)} %param.24) | copy-start | bytes 196
  6.5 60.1 %copy-start.12 = (s32[8]{0:T(128)S(1)}, s32[8]{0:T(128)}, u32[]{:S(2)}) copy-start(s32[8]{0:T(128)} %param.23) | copy-start | bytes 100
  6.5 60.2 %copy-start.6 = (s32[28]{0:T(128)S(1)}, s32[28]{0:T(128)}, u32[]{:S(2)}) copy-start(s32[28]{0:T(128)} %param.25) | copy-start | bytes 340
  6.6 60.2 %copy-start.9 = (s32[28]{0:T(128)S(1)}, s32[28]{0:T(128)}, u32[]{:S(2)}) copy-start(s32[28]{0:T(128)} %param.26) | copy-start | bytes 340
  6.6 60.4 %copy-start.3 = (bf16[128,1024]{1,0:T(8,128)(2,1)S(1)}, bf16[128,1024]{1,0:T(8,128)(2,1)}, u32[]{:S(2)}) copy-start(bf16[128,1024]{1,0:T(8,128)(2,1)} %param.18) | copy-start | bytes 786436
  6.6 69.5 %copy-start.1 = (bf16[128,4096]{1,0:T(8,128)(2,1)S(1)}, bf16[128,4096]{1,0:T(8,128)(2,1)}, u32[]{:S(2)}) copy-start(bf16[128,4096]{1,0:T(8,128)(2,1)} %param.17) | copy-start | bytes 3145732
  6.6 58.3 %all-gather.3.cloned.1.call-start = ((), (), s32[]{:S(2)}) async-start(), calls=%async_computation.2 | async-start | bytes 4718592 | tf_op jit(solution)/shard_map/all_gather | solution.py:200
  8.9 166.2 %all-gather.5.cloned.1.call-start = ((), (), s32[]{:S(2)}) async-start(), calls=%async_computation.3 | async-start | bytes 17825792 | tf_op jit(solution)/shard_map/all_gather | solution.py:219
  64.8 32.1 %collective-permute-start = (bf16[4096,512]{1,0:T(8,128)(2,1)}, bf16[4096,512]{1,0:T(8,128)(2,1)}, u32[]{:S(2)}, u32[]{:S(2)}) collective-permute-start(bf16[4096,512]{1,0:T(8,128)(2,1)} %all-gather.3.cloned.1.call-done.kc_ref.vc_ref), channel_id=1, source_target_pairs={{0,1},{1,0},{2,3},{3,2},{4,5},{5,4},{6,7},{7,6},{8,9},{9,8},{10,11... | collective-permute-start | bytes 12582920 | tf_op jit(solution)/shard_map/ppermute | solution.py:201
  117.6 65.4 %copy-start.2 = (bf16[128,2048]{1,0:T(8,128)(2,1)S(1)}, bf16[128,2048]{1,0:T(8,128)(2,1)}, u32[]{:S(2)}) copy-start(bf16[128,2048]{1,0:T(8,128)(2,1)} %param.20) | copy-start | bytes 1572868
  117.6 65.7 %copy-start.5 = (f32[2048]{0:T(1024)S(1)}, f32[2048]{0:T(1024)}, u32[]{:S(2)}) copy-start(f32[2048]{0:T(1024)} %param.28) | copy-start | bytes 24580
  185.7 102.9 %copy-start = (bf16[1,2048,768]{2,1,0:T(8,128)(2,1)S(1)}, bf16[1,2048,768]{2,1,0:T(8,128)(2,1)}, u32[]{:S(2)}) copy-start(bf16[1,2048,768]{2,1,0:T(8,128)(2,1)} %param.31) | copy-start | bytes 9437188
  313.7 8.4 %copy-start.7 = (f32[128,8]{0,1:T(8,128)S(1)}, f32[128,8]{0,1:T(8,128)}, u32[]{:S(2)}) copy-start(f32[128,8]{0,1:T(8,128)} %param.30) | copy-start | bytes 12292
  313.7 119.6 %all-to-all-start.1 = ((bf16[128,16,2048]{2,1,0:T(8,128)(2,1)}), bf16[128,16,2048]{2,1,0:T(8,128)(2,1)}, u32[]{:S(2)}, u32[]{:S(2)}) async-start(bf16[128,16,2048]{2,1,0:T(8,128)(2,1)} %bitcast.29), calls=%async_computation.1 | async-start | bytes 16777216 | tf_op jit(solution)/shard_map/all_to_all | solution.py:249
Sparse Core Ops, SparseCore 0:
  9.0 55.7 all-gather.2
  67.3 107.7 all-gather.4

commit v10 on v8

--- a/solution.py
+++ b/solution.py
@@ -122,7 +122,7 @@
     o_ref[...] = total
 
 
-def projection(attended, weight, group_rows, groups_per_step=4):
+def projection(attended, weight, group_rows, groups_per_step=8):
     tokens = attended.shape[0]
     width = weight.shape[1]
     step_rows = group_rows * groups_per_step

time: 453 us -> 453 us (level)
  no operation moved by 1% of the time
where the time goes in v10:
time: 453 us; the launch traced here: 447 us
  waiting for transfers between devices  220 us (49%)
  blocking collectives  103 us (23%)
  Pallas kernels  73.4 us (16%)
  other arithmetic  14.5 us (3%)
  between operations  14.2 us (3%)
  starting transfers between devices  9.25 us (2%)
  matrix products  8.99 us (2%)
    all_to_all x1, waiting for transfers between devices, on_device(): lax.all_to_all(expert_out.reshape(arrived.shape), TOKEN_AXES, split_axis=...  108 us
    all_to_all x1, blocking collectives, on_device(): lax.all_to_all(outgoing, TOKEN_AXES, split_axis=0, concat_axis=0, tiled=T...  103 us
    all_gather x1, waiting for transfers between devices, on_device(): lax.all_gather(out_weight, ('gyo', 'core'), axis=0, tiled=True)  57.5 us
    all_gather x1, waiting for transfers between devices, on_device(): lax.all_gather(kv_half(kv_cache, core), 'gx', axis=0, tiled=True)  54 us
    pallas_call x2, Pallas kernels, tree_attention(): pl.pallas_call(attention_kernel, grid=(local_heads,), in_specs=[pl.BlockS...  40.8 us
    pallas_call x1, Pallas kernels, expert_ffn(): pl.pallas_call(expert_kernel, grid=(rows // block_rows,), in_specs=[pl.Bl...  25.1 us
  transfers between devices with their start and end apart: 4, of which 3 were waited for; matrix products, arithmetic and copies ran while one was open for 3% of the time, Pallas kernels for 9%

profile of v10, /device:TPU:1, one launch (start us, length us, event | category | flops | bytes accessed | tf_op | source)
XLA Modules:
  0.0 446.8 jit_solution(17974838760342401274)
XLA Ops:
  6.6 1.4 fusion.18
  8.1 0.8 pad_maximum_fusion
  9.0 0.7 all-gather.5.cloned.1.call-update
  9.7 0.8 copy.38
  10.7 0.2 fusion.10
  10.9 54.0 %all-gather.3.cloned.1.call-done.kc_ref.vc_ref = bf16[4096,512]{1,0:T(8,128)(2,1)} async-done(((bf16[512,512]{1,0:T(8,128)(2,1)}), bf16[4096,512]{1,0:T(8,128)(2,1)}) %all-gather.3.cloned.1.call-update) | async-done | bytes 4194320 | tf_op jit(solution)/shard_map/all_gather | solution.py:200
  64.8 0.8 collective-permute-start
  66.0 0.4 fusion.7
  67.3 1.3 compare_reduce_fusion
  68.6 7.4 %fusion = pred[2048,128]{1,0:T(8,128)(4,1)S(1)} fusion(s32[128,8]{0,1:T(8,128)S(1)} %multiply_add_fusion), kind=kLoop, calls=%fused_computation.3 | loop fusion | flops 3932160 | bytes 266240 | tf_op jit(solution)/shard_map/reduce_or | solution.py:239
  76.2 0.2 broadcast_select_fusion.bf_ref
  76.5 20.5 %shard_map.163 = bf16[128,2048]{1,0:T(8,128)(2,1)S(1)} custom-call(bf16[128,2048]{1,0:T(8,128)(2,1)S(1)} %get-tuple-element.7.q_ref, bf16[4096,512]{1,0:T(8,128)(2,1)} %all-gather.3.cloned.1.call-done.kc_ref.vc_ref, bf16[4096,512]{1,0:T(8,128)(2,1)} %all-gather.3.cloned.1.call-done.kc_ref.vc_ref, bf16[128,512]{1,0:T(8,128)(2,1)S(1)} %pad_maximum_fusion.1.kn_ref.vn_ref, ...), custom_call_target="tpu_custom_call" | custom-call | tf_op jit(solution)/shard_map/pallas_call | solution.py:82
  97.0 20.4 %shard_map.164 = bf16[128,2048]{1,0:T(8,128)(2,1)S(1)} custom-call(bf16[128,2048]{1,0:T(8,128)(2,1)S(1)} %get-tuple-element.8.q_ref, bf16[4096,512]{1,0:T(8,128)(2,1)} %collective-permute-done.kc_ref.vc_ref, bf16[4096,512]{1,0:T(8,128)(2,1)} %collective-permute-done.kc_ref.vc_ref, bf16[128,512]{1,0:T(8,128)(2,1)S(1)} %pad_maximum_fusion.2.kn_ref.vn_ref, ...), custom_call_target="tpu_custom_call" | custom-call | tf_op jit(solution)/shard_map/pallas_call | solution.py:82
  117.3 0.3 maximum_select_fusion.a_ref
  117.6 57.5 %all-gather.5.cloned.1.call-done.w_ref = bf16[4096,2048]{1,0:T(8,128)(2,1)} async-done(((bf16[256,2048]{1,0:T(8,128)(2,1)}), bf16[4096,2048]{1,0:T(8,128)(2,1)}) %all-gather.5.cloned.1.call-update) | async-done | bytes 16777232 | tf_op jit(solution)/shard_map/all_gather | solution.py:219
  175.1 7.5 %shard_map.165 = f32[128,2048]{1,0:T(8,128)S(1)} custom-call(bf16[128,4096]{1,0:T(8,128)(2,1)S(1)} %maximum_select_fusion.a_ref, bf16[4096,2048]{1,0:T(8,128)(2,1)} %all-gather.5.cloned.1.call-done.w_ref), custom_call_target="tpu_custom_call" | custom-call | tf_op jit(solution)/shard_map/pallas_call | solution.py:129
  182.7 0.2 fusion.2
  182.9 2.4 convolution_convert_fusion
  185.3 102.9 %all_to_all.10 = bf16[128,16,2048]{2,1,0:T(8,128)(2,1)} all-to-all(bf16[128,16,2048]{2,1,0:T(8,128)(2,1)S(1)} %bitcast.28), channel_id=1, replica_groups=mesh['gx'=8,'gyo'=8,'core'=2] {'gx','gyo','core'}, dimensions={0} | all-to-all | bytes 16777216 | tf_op jit(solution)/shard_map/all_to_all | solution.py:246
  288.3 25.1 %shard_map.166 = bf16[2048,2048]{1,0:T(8,128)(2,1)} custom-call(bf16[2048,2048]{1,0:T(8,128)(2,1)} %bitcast.30, bf16[2048,768]{1,0:T(8,128)(2,1)S(1)} %bitcast.27, bf16[2048,768]{1,0:T(8,128)(2,1)} %bitcast.31, bf16[768,2048]{1,0:T(8,128)(2,1)} %bitcast.32), custom_call_target="tpu_custom_call" | custom-call | tf_op jit(solution)/shard_map/pallas_call | solution.py:152
  313.4 8.3 %all-to-all-start.1 = ((bf16[128,16,2048]{2,1,0:T(8,128)(2,1)}), bf16[128,16,2048]{2,1,0:T(8,128)(2,1)}, u32[]{:S(2)}, u32[]{:S(2)}) async-start(bf16[128,16,2048]{2,1,0:T(8,128)(2,1)} %bitcast.29), calls=%async_computation.1 | async-start | bytes 16777216 | tf_op jit(solution)/shard_map/all_to_all | solution.py:249
  321.9 2.7 select_reduce_fusion
  324.7 108.3 %all-to-all-done.1 = bf16[128,16,2048]{2,1,0:T(8,128)(2,1)} async-done(((bf16[128,16,2048]{2,1,0:T(8,128)(2,1)}), bf16[128,16,2048]{2,1,0:T(8,128)(2,1)}, u32[]{:S(2)}, u32[]{:S(2)}) %all-to-all-start.1) | async-done | bytes 8388640 | tf_op jit(solution)/shard_map/all_to_all | solution.py:249
  432.9 6.6 %fusion.1 = bf16[128,2048]{1,0:T(8,128)(2,1)} fusion(f32[128,2048]{1,0:T(8,128)S(1)} %select_reduce_fusion, bf16[2048,2048]{1,0:T(8,128)(2,1)} %bitcast.14, bf16[128,2048]{1,0:T(8,128)(2,1)S(1)} %add_convert_fusion), kind=kOutput, calls=%fused_computation.7 | convolution fusion | flops 3222011904 | bytes 10485760 | tf_op jit(solution)/shard_map/dot_general | solution.py:252
  (60 shorter events, 2.0 us)
Async XLA Ops:
  6.5 62.0 %copy-start.4 = (s32[128,8]{0,1:T(8,128)S(1)}, s32[128,8]{0,1:T(8,128)}, u32[]{:S(2)}) copy-start(s32[128,8]{0,1:T(8,128)} %param.29) | copy-start | bytes 12292
  6.5 59.9 %copy-start.8 = (s32[1,128]{1,0:T(1,128)S(1)}, s32[1,128]{1,0:T(1,128)}, u32[]{:S(2)}) copy-start(s32[1,128]{1,0:T(1,128)} %param.21) | copy-start | bytes 1540
  6.5 59.9 %copy-start.10 = (s32[1,8]{1,0:T(1,128)S(1)}, s32[1,8]{1,0:T(1,128)}, u32[]{:S(2)}) copy-start(s32[1,8]{1,0:T(1,128)} %param.22) | copy-start | bytes 100
  6.5 60.0 %copy-start.11 = (s32[16]{0:T(128)S(1)}, s32[16]{0:T(128)}, u32[]{:S(2)}) copy-start(s32[16]{0:T(128)} %param.24) | copy-start | bytes 196
  6.5 60.1 %copy-start.12 = (s32[8]{0:T(128)S(1)}, s32[8]{0:T(128)}, u32[]{:S(2)}) copy-start(s32[8]{0:T(128)} %param.23) | copy-start | bytes 100
  6.5 60.2 %copy-start.6 = (s32[28]{0:T(128)S(1)}, s32[28]{0:T(128)}, u32[]{:S(2)}) copy-start(s32[28]{0:T(128)} %param.25) | copy-start | bytes 340
  6.6 60.2 %copy-start.9 = (s32[28]{0:T(128)S(1)}, s32[28]{0:T(128)}, u32[]{:S(2)}) copy-start(s32[28]{0:T(128)} %param.26) | copy-start | bytes 340
  6.6 60.4 %copy-start.3 = (bf16[128,1024]{1,0:T(8,128)(2,1)S(1)}, bf16[128,1024]{1,0:T(8,128)(2,1)}, u32[]{:S(2)}) copy-start(bf16[128,1024]{1,0:T(8,128)(2,1)} %param.18) | copy-start | bytes 786436
  6.6 69.5 %copy-start.1 = (bf16[128,4096]{1,0:T(8,128)(2,1)S(1)}, bf16[128,4096]{1,0:T(8,128)(2,1)}, u32[]{:S(2)}) copy-start(bf16[128,4096]{1,0:T(8,128)(2,1)} %param.17) | copy-start | bytes 3145732
  6.6 58.3 %all-gather.3.cloned.1.call-start = ((), (), s32[]{:S(2)}) async-start(), calls=%async_computation.2 | async-start | bytes 4718592 | tf_op jit(solution)/shard_map/all_gather | solution.py:200
  8.9 166.2 %all-gather.5.cloned.1.call-start = ((), (), s32[]{:S(2)}) async-start(), calls=%async_computation.3 | async-start | bytes 17825792 | tf_op jit(solution)/shard_map/all_gather | solution.py:219
  64.8 32.1 %collective-permute-start = (bf16[4096,512]{1,0:T(8,128)(2,1)}, bf16[4096,512]{1,0:T(8,128)(2,1)}, u32[]{:S(2)}, u32[]{:S(2)}) collective-permute-start(bf16[4096,512]{1,0:T(8,128)(2,1)} %all-gather.3.cloned.1.call-done.kc_ref.vc_ref), channel_id=1, source_target_pairs={{0,1},{1,0},{2,3},{3,2},{4,5},{5,4},{6,7},{7,6},{8,9},{9,8},{10,11... | collective-permute-start | bytes 12582920 | tf_op jit(solution)/shard_map/ppermute | solution.py:201
  117.6 65.0 %copy-start.2 = (bf16[128,2048]{1,0:T(8,128)(2,1)S(1)}, bf16[128,2048]{1,0:T(8,128)(2,1)}, u32[]{:S(2)}) copy-start(bf16[128,2048]{1,0:T(8,128)(2,1)} %param.20) | copy-start | bytes 1572868
  117.6 65.3 %copy-start.5 = (f32[2048]{0:T(1024)S(1)}, f32[2048]{0:T(1024)}, u32[]{:S(2)}) copy-start(f32[2048]{0:T(1024)} %param.28) | copy-start | bytes 24580
  185.3 102.9 %copy-start = (bf16[1,2048,768]{2,1,0:T(8,128)(2,1)S(1)}, bf16[1,2048,768]{2,1,0:T(8,128)(2,1)}, u32[]{:S(2)}) copy-start(bf16[1,2048,768]{2,1,0:T(8,128)(2,1)} %param.31) | copy-start | bytes 9437188
  313.4 8.4 %copy-start.7 = (f32[128,8]{0,1:T(8,128)S(1)}, f32[128,8]{0,1:T(8,128)}, u32[]{:S(2)}) copy-start(f32[128,8]{0,1:T(8,128)} %param.30) | copy-start | bytes 12292
  313.4 119.6 %all-to-all-start.1 = ((bf16[128,16,2048]{2,1,0:T(8,128)(2,1)}), bf16[128,16,2048]{2,1,0:T(8,128)(2,1)}, u32[]{:S(2)}, u32[]{:S(2)}) async-start(bf16[128,16,2048]{2,1,0:T(8,128)(2,1)} %bitcast.29), calls=%async_computation.1 | async-start | bytes 16777216 | tf_op jit(solution)/shard_map/all_to_all | solution.py:249
Sparse Core Ops, SparseCore 0:
  9.0 55.7 all-gather.2
  67.3 107.7 all-gather.4
